TPU v7x, 32 devices: a whole 2x2x4 slice. The times are simulated.
32 devices in a mesh: dp: 4 (over y, x), expert: 2 (over core), tensor: 4 (over z).
Axes of the slice: x: 2, y: 2, z: 4, core: 2. Of those that a mesh axis runs over, the one named last changes fastest.
Arguments:
- tokens: bfloat16 [4096, 2048], P(('dp', 'expert', 'tensor')), may hold values from -6 to 6
- norm_gain: float32 [2048], replicated, may hold values from 0.1 to 1.9
- expert_ids: int32 [4096, 8], P(('dp', 'expert', 'tensor')), may hold values from 0 to 31, all different within a row; in each aligned block of 128 rows (0 to 127, 128 to 255, ...) at most 64 rows name the same one
- gate_weights: float32 [4096, 8], P(('dp', 'expert', 'tensor')), may hold values from 0.03 to 0.4
- w_in: bfloat16 [32, 2048, 1536], P(('dp', 'expert', 'tensor')), may hold values from -1.875 to 1.875, as said below
- scale_in: float32 [32, 16, 12], P(('dp', 'expert', 'tensor')), may hold values from 0.03 to 0.12
- w_out: bfloat16 [32, 768, 2048], P(('dp', 'expert', 'tensor')), may hold values from -1.875 to 1.875, as said below
- scale_out: float32 [32, 6, 16], P(('dp', 'expert', 'tensor')), may hold values from 0.02 to 0.08
- w_sync: bfloat16 [2048, 2, 2048], P(None, None, 'tensor'), may hold values from -0.125 to 0.125
- head_weight: float32 [16], P('tensor'), may hold values from -3 to 3
- frame_rows: int32 [8, 2, 256], P(('dp', 'expert')), may hold values from 0 to 511, as said below
- lag_offsets: int32 [21], replicated, may hold values from -32 to 32, as said below
Outputs:
- mixed: bfloat16 [4096, 2048], P(('dp', 'expert', 'tensor'))
- sync_logits: float32 [8, 21], P(('dp', 'expert'))
Inputs may be any that keep to these rules, and one draw needn't show every extreme that they name: `expert_ids`: in each aligned block of 128 rows (the rows of one device) no expert is named by more than 64 of the block's choices; the choices of a row are different. `w_in`: every entry is an e4m3 value: a sign times (1 + m / 8) times 2 to the e, with whole m of 0 to 7 and e of -3 to 0. `w_out`: every entry is an e4m3 value: a sign times (1 + m / 8) times 2 to the e, with whole m of 0 to 7 and e of -3 to 0. `frame_rows`: for each clip the audio rows and the video rows together are each of 0 to 511 once. `lag_offsets`: 21 different lags in increasing order; the first is -32 and the last 32.
All inputs are finite; a program needn't handle non-finite values.
Results may differ from a plain program's by a relative error of at most 0.0035.
The roundings to bfloat16 on the way count: a program that leaves them out, or rounds other values in their place, can miss the bound.
Values may be sent and summed in bfloat16 or wider, within the bound.
No kernel may reach another device: no remote copies, remote signals or barrier semaphores. Data moves between devices by JAX's collectives and lax.ppermute only.
A program may use at most 128 MiB of HBM per device.

v0:
```python
import jax
import jax.numpy as jnp
from jax import lax
from jax.sharding import PartitionSpec as P


def dequant(weights, scales):
    block = weights.shape[0] // scales.shape[0]
    full = jnp.repeat(jnp.repeat(scales, block, axis=0), block, axis=1)
    return (weights.astype(jnp.float32) * full).astype(jnp.bfloat16)


def shards(
    tokens,
    norm_gain,
    expert_ids,
    gate_weights,
    w_in,
    scale_in,
    w_out,
    scale_out,
    w_sync,
    head_weight,
    frame_rows,
    lag_offsets,
):
    rows, width = tokens.shape
    top = expert_ids.shape[1]
    devices = lax.axis_size(("dp", "expert", "tensor"))
    experts_all = devices * w_in.shape[0]
    most = 2 * rows * top // experts_all
    x_float = tokens.astype(jnp.float32)
    normed = (
        x_float * lax.rsqrt(jnp.mean(x_float * x_float, axis=-1, keepdims=True) + 1e-06) * norm_gain
    ).astype(jnp.bfloat16)
    flat_ids = expert_ids.reshape(-1)
    pair_count = rows * top
    onehot = (flat_ids[:, None] == jnp.arange(experts_all, dtype=jnp.int32)[None, :]).astype(
        jnp.bfloat16
    )
    pair_index = jnp.arange(pair_count, dtype=jnp.int32)
    earlier = (pair_index[None, :] < pair_index[:, None]).astype(jnp.bfloat16)
    before = jnp.dot(earlier, onehot, preferred_element_type=jnp.float32)
    slots = jnp.sum(before * onehot.astype(jnp.float32), axis=1).astype(jnp.int32)
    target = flat_ids * most + slots
    target_grid = target.reshape(rows, top)
    slot_index = jnp.arange(experts_all * most, dtype=jnp.int32)
    selector = jnp.any(target_grid[None, :, :] == slot_index[:, None, None], axis=2).astype(
        jnp.bfloat16
    )
    outgoing = jnp.dot(selector, normed, preferred_element_type=jnp.float32).astype(jnp.bfloat16)
    outgoing = outgoing.reshape(experts_all, most, width)
    gate_up = dequant(w_in[0], scale_in[0])
    down_proj = dequant(w_out[0], scale_out[0])
    hidden_width = down_proj.shape[0]
    block = lax.all_to_all(
        outgoing, ("dp", "expert", "tensor"), split_axis=0, concat_axis=0, tiled=True
    )
    flat = block.reshape(-1, width)
    mixed_in = jnp.dot(flat, gate_up, preferred_element_type=jnp.float32)
    hidden = (jax.nn.silu(mixed_in[:, :hidden_width]) * mixed_in[:, hidden_width:]).astype(
        jnp.bfloat16
    )
    output = jnp.dot(hidden, down_proj, preferred_element_type=jnp.float32).astype(jnp.bfloat16)
    send_block = output.reshape(block.shape)
    back = lax.all_to_all(
        send_block, ("dp", "expert", "tensor"), split_axis=0, concat_axis=0, tiled=True
    )
    returned_rows = (
        jnp.take(back.reshape(-1, width), target, axis=0)
        .astype(jnp.float32)
        .reshape(rows, top, width)
    )
    combined = jnp.sum(returned_rows * gate_weights[:, :, None], axis=1)
    mixed = (x_float + combined).astype(jnp.bfloat16)
    local_sync = w_sync.reshape(width, -1)
    proj = jnp.dot(
        lax.all_gather(mixed, "tensor", axis=0, tiled=True),
        local_sync,
        preferred_element_type=jnp.float32,
    ).astype(jnp.bfloat16)
    half = proj.shape[1] // 2
    heads_here = head_weight.shape[0]
    head_size = half // heads_here
    frames = frame_rows.shape[2]
    clip_len = proj.shape[0]
    clip_index = jnp.arange(clip_len, dtype=jnp.int32)
    pick_audio = (frame_rows[0, 0][:, None] == clip_index[None, :]).astype(jnp.bfloat16)
    pick_video = (frame_rows[0, 1][:, None] == clip_index[None, :]).astype(jnp.bfloat16)
    audio = (
        jnp.dot(pick_audio, proj[:, :half], preferred_element_type=jnp.float32)
        .astype(jnp.bfloat16)
        .reshape(frames, heads_here, head_size)
    )
    video = (
        jnp.dot(pick_video, proj[:, half:], preferred_element_type=jnp.float32)
        .astype(jnp.bfloat16)
        .reshape(frames, heads_here, head_size)
    )
    grams = jnp.einsum("thd,shd->hts", audio, video, preferred_element_type=jnp.float32)
    times = jnp.arange(frames, dtype=jnp.int32)
    offsets = times[None, :] - times[:, None]
    diagonal = (
        (offsets[None, :, :] == lag_offsets[:, None, None])
        .astype(jnp.float32)
        .reshape(lag_offsets.shape[0], frames * frames)
    )
    sums = lax.dot_general(
        grams.reshape(heads_here, frames * frames),
        diagonal,
        (((1,), (1,)), ((), ())),
        precision=lax.Precision.HIGHEST,
        preferred_element_type=jnp.float32,
    )
    counts = (frames - jnp.abs(lag_offsets)).astype(jnp.float32)
    score = sums / jnp.sqrt(counts * head_size)[None, :]
    partial_logits = jnp.sum(head_weight[:, None] * score, axis=0)
    sync_logits = lax.psum(partial_logits, "tensor")
    return (mixed, sync_logits[None, :])


def solution(mesh):
    return jax.shard_map(
        shards,
        mesh=mesh,
        in_specs=(
            P(("dp", "expert", "tensor"), None),
            P(),
            P(("dp", "expert", "tensor"), None),
            P(("dp", "expert", "tensor"), None),
            P(("dp", "expert", "tensor"), None, None),
            P(("dp", "expert", "tensor"), None, None),
            P(("dp", "expert", "tensor"), None, None),
            P(("dp", "expert", "tensor"), None, None),
            P(None, None, "tensor"),
            P("tensor"),
            P(("dp", "expert"), None, None),
            P(),
        ),
        out_specs=(P(("dp", "expert", "tensor"), None), P(("dp", "expert"), None)),
        check_vma=False,
    )
```

profile of v0, /device:TPU:0, one launch (start us, length us, event | category | flops | bytes accessed | tf_op | source)
XLA Modules:
  0.0 537.3 jit_solution(8661923985950426051)
XLA Ops:
  7.2 0.8 copy.30
  8.0 0.5 fusion.16
  8.7 0.7 compare_and_fusion
  9.5 7.4 %fusion.1 = pred[2048,128]{1,0:T(8,128)(4,1)S(1)} fusion(s32[128,8]{0,1:T(8,128)S(1)} %get-tuple-element.3), kind=kLoop, calls=%fused_computation.5 | loop fusion | flops 3932160 | bytes 266240 | tf_op jit(solution)/shard_map/reduce_or | solution.py:48
  16.9 1.2 fusion.29
  18.1 6.7 %convolution_convert_fusion.1 = bf16[2048,2048]{1,0:T(8,128)(2,1)} fusion(pred[2048,128]{1,0:T(8,128)(4,1)S(1)} %fusion.1, bf16[128,2048]{1,0:T(8,128)(2,1)} %param.12, f32[2048]{0:T(1024)} %param.13, f32[128]{0:T(128)S(1)} %add_rsqrt_fusion), kind=kOutput, calls=%fused_computation.7 | convolution fusion | flops 1078984704 | bytes 9183744 | tf_op jit(solution)/shard_map/dot_general | solution.py:51
  24.8 7.6 %all-to-all-start = ((bf16[32,64,2048]{2,1,0:T(8,128)(2,1)}), bf16[32,64,2048]{2,1,0:T(8,128)(2,1)}, u32[]{:S(2)}, u32[]{:S(2)}) async-start(bf16[32,64,2048]{2,1,0:T(8,128)(2,1)} %bitcast.66), calls=%async_computation | async-start | bytes 16777216 | tf_op jit(solution)/shard_map/all_to_all | solution.py:56
  32.4 8.7 %copy.33 = bf16[1,2048,1536]{1,2,0:T(8,128)(2,1)} copy(bf16[1,2048,1536]{2,1,0:T(8,128)(2,1)} %param.16) | data formatting | bytes 12582912 | tf_op args[4]
  41.3 7.7 %fusion = bf16[2048,12,128]{0,2,1:T(8,128)(2,1)} fusion(bf16[2048,12,128]{0,2,1:T(8,128)(2,1)} %bitcast.67, f32[2048,12]{0,1:T(8,128)S(1)} %bitcast.74), kind=kLoop, calls=%fused_computation.2 | loop fusion | flops 9437184 | bytes 12681216 | tf_op jit(solution)/shard_map/convert_element_type | solution.py:10
  49.0 164.7 %all-to-all-done = bf16[32,64,2048]{2,1,0:T(8,128)(2,1)} async-done(((bf16[32,64,2048]{2,1,0:T(8,128)(2,1)}), bf16[32,64,2048]{2,1,0:T(8,128)(2,1)}, u32[]{:S(2)}, u32[]{:S(2)}) %all-to-all-start) | async-done | bytes 8388640 | tf_op jit(solution)/shard_map/all_to_all | solution.py:56
  213.7 19.3 %fusion.52 = f32[2048,1536]{1,0:T(8,128)} fusion(bf16[2048,2048]{1,0:T(8,128)(2,1)} %bitcast.1, bf16[2048,1536]{0,1:T(8,128)(2,1)} %bitcast.69), kind=kOutput, calls=%fused_computation.70 | convolution fusion | flops 12884901888 | bytes 27262976 | tf_op jit(solution)/shard_map/dot_general | solution.py:60
  233.0 1.8 broadcast_in_dim.24
  234.9 15.8 %convolution_convert_fusion = bf16[2048,2048]{1,0:T(8,128)(2,1)} fusion(f32[2048,1536]{1,0:T(8,128)} %fusion.52, f32[96,8,16,128]{3,2,1,0:T(8,128)S(1)} %bitcast.70, bf16[1,768,2048]{2,1,0:T(8,128)(2,1)S(1)} %copy-done.6), kind=kOutput, calls=%fused_computation.6 | convolution fusion | flops 6460801024 | bytes 30408704 | tf_op jit(solution)/shard_map/dot_general | solution.py:64
  250.7 8.5 %all-to-all-start.1 = ((bf16[32,64,2048]{2,1,0:T(8,128)(2,1)}), bf16[32,64,2048]{2,1,0:T(8,128)(2,1)}, u32[]{:S(2)}, u32[]{:S(2)}) async-start(bf16[32,64,2048]{2,1,0:T(8,128)(2,1)} %bitcast.68), calls=%async_computation.1 | async-start | bytes 16777216 | tf_op jit(solution)/shard_map/all_to_all | solution.py:66
  259.9 180.7 %all-to-all-done.1 = bf16[32,64,2048]{2,1,0:T(8,128)(2,1)} async-done(((bf16[32,64,2048]{2,1,0:T(8,128)(2,1)}), bf16[32,64,2048]{2,1,0:T(8,128)(2,1)}, u32[]{:S(2)}, u32[]{:S(2)}) %all-to-all-start.1) | async-done | bytes 8388640 | tf_op jit(solution)/shard_map/all_to_all | solution.py:66
  440.7 13.4 %gather_fusion = bf16[1024,2048]{1,0:T(8,128)(2,1)} fusion(bf16[2048,2048]{1,0:T(8,128)(2,1)} %bitcast.7, s32[1024]{0:T(1024)S(1)} %broadcast_clamp_fusion), kind=kCustom, calls=%fused_computation | custom fusion | bytes 8392704 | tf_op jit(solution)/shard_map/jit(_take)/gather | solution.py:70
  454.0 5.6 %multiply_reduce_fusion = f32[128,2048]{1,0:T(8,128)S(1)} fusion(bf16[1024,2048]{1,0:T(8,128)(2,1)} %gather_fusion, f32[128,8]{1,0:T(8,128)S(1)} %copy.35, pred[128,8]{1,0:T(8,128)(4,1)S(1)} %copy.32), kind=kLoop, calls=%fused_computation.3 | loop fusion | flops 8126464 | bytes 5248000 | tf_op jit(solution)/shard_map/reduce_sum | solution.py:74
  459.7 0.9 fusion.32
  460.6 5.3 copy.45
  466.0 44.5 %all-gather.2.cloned.1.call-done = bf16[512,2048]{1,0:T(8,128)(2,1)} async-done(((bf16[128,2048]{1,0:T(8,128)(2,1)}), bf16[512,2048]{1,0:T(8,128)(2,1)}) %all-gather.2.cloned.1.call-update) | async-done | bytes 2097168 | tf_op jit(solution)/shard_map/all_gather | solution.py:78
  510.5 5.2 convolution_convert_fusion.2
  515.7 0.4 fusion.13
  516.7 3.7 fusion.26
  520.4 10.0 %psum.7 = f32[1,21]{1,0:T(1,128)} all-reduce(f32[1,21]{1,0:T(1,128)S(1)} %bitcast.82), channel_id=1, replica_groups=mesh['dp'=4,'expert'=2,'tensor'=4] {'tensor'}, use_global_device_ids=true, to_apply=%region_5.6 | all-reduce | flops 21 | bytes 168 | tf_op jit(solution)/shard_map/psum | solution.py:118
  (43 shorter events, 1.9 us)
Async XLA Ops:
  24.8 188.9 %all-to-all-start = ((bf16[32,64,2048]{2,1,0:T(8,128)(2,1)}), bf16[32,64,2048]{2,1,0:T(8,128)(2,1)}, u32[]{:S(2)}, u32[]{:S(2)}) async-start(bf16[32,64,2048]{2,1,0:T(8,128)(2,1)} %bitcast.66), calls=%async_computation | async-start | bytes 16777216 | tf_op jit(solution)/shard_map/all_to_all | solution.py:56
  32.4 8.7 %copy-start.2 = (f32[1,16,12]{1,0,2:T(1,128)S(1)}, f32[1,16,12]{1,0,2:T(1,128)}, u32[]{:S(2)}) copy-start(f32[1,16,12]{1,0,2:T(1,128)} %param.17) | copy-start | bytes 2308
  32.4 8.9 %copy-start.4 = (f32[1,6,16]{2,0,1:T(1,128)S(1)}, f32[1,6,16]{2,0,1:T(1,128)}, u32[]{:S(2)}) copy-start(f32[1,6,16]{2,0,1:T(1,128)} %param.19) | copy-start | bytes 1156
  233.0 1.9 copy-start.6
  250.7 8.8 %copy-start.1 = (s32[128,8]{0,1:T(8,128)S(1)}, s32[128,8]{0,1:T(8,128)}, u32[]{:S(2)}) copy-start(s32[128,8]{0,1:T(8,128)} %param.14) | copy-start | bytes 12292
  250.7 9.1 %copy-start.3 = (f32[128,8]{0,1:T(8,128)S(1)}, f32[128,8]{0,1:T(8,128)}, u32[]{:S(2)}) copy-start(f32[128,8]{0,1:T(8,128)} %param.15) | copy-start | bytes 12292
  250.7 190.0 %all-to-all-start.1 = ((bf16[32,64,2048]{2,1,0:T(8,128)(2,1)}), bf16[32,64,2048]{2,1,0:T(8,128)(2,1)}, u32[]{:S(2)}, u32[]{:S(2)}) async-start(bf16[32,64,2048]{2,1,0:T(8,128)(2,1)} %bitcast.68), calls=%async_computation.1 | async-start | bytes 16777216 | tf_op jit(solution)/shard_map/all_to_all | solution.py:66
  259.2 251.3 %all-gather.2.cloned.1.call-start = ((), (), s32[]{:S(2)}) async-start(), calls=%async_computation.2 | async-start | bytes 2621440 | tf_op jit(solution)/shard_map/all_gather | solution.py:78
  440.7 19.0 %copy-start = (bf16[128,2048]{1,0:T(8,128)(2,1)S(1)}, bf16[128,2048]{1,0:T(8,128)(2,1)}, u32[]{:S(2)}) copy-start(bf16[128,2048]{1,0:T(8,128)(2,1)} %param.12) | copy-start | bytes 1572868
  459.6 6.3 %copy-start.7 = (s32[21]{0:T(128)S(1)}, s32[21]{0:T(128)}, u32[]{:S(2)}) copy-start(s32[21]{0:T(128)} %param.23) | copy-start | bytes 256
  459.7 6.3 %copy-start.5 = (s32[1,2,256]{2,1,0:T(2,128)S(1)}, s32[1,2,256]{2,1,0:T(2,128)}, u32[]{:S(2)}) copy-start(s32[1,2,256]{2,1,0:T(2,128)} %param.22) | copy-start | bytes 6148
  510.5 6.2 %copy-start.8 = (f32[4]{0:T(128)S(1)}, f32[4]{0:T(128)}, u32[]{:S(2)}) copy-start(f32[4]{0:T(128)} %param.21) | copy-start | bytes 52
Sparse Core Ops, SparseCore 0:
  460.7 49.7 all-gather.1
where the time goes:
time: 538 us; the launch traced here: 537 us
  waiting for transfers between devices  390 us (72%)
  matrix products  52.2 us (10%)
  local copies, waits for them, and re-layouts  30.9 us (6%)
  other arithmetic  23.6 us (4%)
  starting transfers between devices  16.4 us (3%)
  between operations  14.3 us (3%)
  blocking collectives  10 us (2%)
    all_to_all x1, waiting for transfers between devices, shards(): lax.all_to_all(send_block, ('dp', 'expert', 'tensor'), split_axis=0, conc...  181 us
    all_to_all x1, waiting for transfers between devices, shards(): lax.all_to_all(outgoing, ('dp', 'expert', 'tensor'), split_axis=0, concat...  165 us
    all_gather x1, waiting for transfers between devices, shards(): lax.all_gather(mixed, 'tensor', axis=0, tiled=True)  44.5 us
    dot_general x1, matrix products, shards(): mixed_in = jnp.dot(flat, gate_up, preferred_element_type=jnp.float32)  19.3 us
    dot_general x1, matrix products, shards(): jnp.dot(hidden, down_proj, preferred_element_type=jnp.float32)  15.8 us
    unnamed x27, local copies, waits for them, and re-layouts  15.2 us
    gather x1, local copies, waits for them, and re-layouts, shards(): jnp.take(back.reshape(-1, width), target, axis=0).astype(jnp.float32)  13.4 us
  transfers between devices with their start and end apart: 3, of which 3 were waited for; matrix products, arithmetic and copies ran while one was open for 4% of the time, Pallas kernels for 0%

commit v1 on v0

--- a/solution.py
+++ b/solution.py
@@ -26,13 +26,17 @@
 ):
     rows, width = tokens.shape
     top = expert_ids.shape[1]
-    devices = lax.axis_size(("dp", "expert", "tensor"))
-    experts_all = devices * w_in.shape[0]
+    lines = lax.axis_size("tensor")
+    plane = lax.axis_size(("dp", "expert"))
+    experts_all = plane * lines * w_in.shape[0]
     most = 2 * rows * top // experts_all
+    cap = lines * most
+    here = lax.axis_index("tensor")
     x_float = tokens.astype(jnp.float32)
     normed = (
         x_float * lax.rsqrt(jnp.mean(x_float * x_float, axis=-1, keepdims=True) + 1e-06) * norm_gain
     ).astype(jnp.bfloat16)
+
     flat_ids = expert_ids.reshape(-1)
     pair_count = rows * top
     onehot = (flat_ids[:, None] == jnp.arange(experts_all, dtype=jnp.int32)[None, :]).astype(
@@ -41,21 +45,42 @@
     pair_index = jnp.arange(pair_count, dtype=jnp.int32)
     earlier = (pair_index[None, :] < pair_index[:, None]).astype(jnp.bfloat16)
     before = jnp.dot(earlier, onehot, preferred_element_type=jnp.float32)
-    slots = jnp.sum(before * onehot.astype(jnp.float32), axis=1).astype(jnp.int32)
-    target = flat_ids * most + slots
-    target_grid = target.reshape(rows, top)
-    slot_index = jnp.arange(experts_all * most, dtype=jnp.int32)
-    selector = jnp.any(target_grid[None, :, :] == slot_index[:, None, None], axis=2).astype(
-        jnp.bfloat16
+    slots = jnp.sum(before * onehot.astype(jnp.float32), axis=1).reshape(rows, top)
+    routing = jnp.concatenate(
+        [expert_ids.astype(jnp.float32), slots, gate_weights.astype(jnp.float32)], axis=1
     )
-    outgoing = jnp.dot(selector, normed, preferred_element_type=jnp.float32).astype(jnp.bfloat16)
-    outgoing = outgoing.reshape(experts_all, most, width)
+
+    line_normed = lax.all_gather(normed, "tensor", axis=0, tiled=True)
+    line_routing = lax.all_gather(routing, "tensor", axis=0, tiled=False)
+    ids_l = line_routing[:, :, :top].astype(jnp.int32)
+    slot_l = line_routing[:, :, top : 2 * top].astype(jnp.int32)
+    gate_l = line_routing[:, :, 2 * top :]
+    mine = (ids_l % lines) == here
+    target = jnp.where(mine, (ids_l // lines) * most + slot_l, -1)
+    slot_ids = jnp.arange(plane * most, dtype=jnp.int32)
+    match = target[:, None, :, :] == slot_ids[None, :, None, None]
+    select = jnp.any(match, axis=3)
+    weight = jnp.sum(jnp.where(match, gate_l[:, None, :, :], 0.0), axis=3)
+    same = (
+        jnp.arange(lines, dtype=jnp.int32)[:, None] == jnp.arange(lines, dtype=jnp.int32)[None, :]
+    )
+    select = select.reshape(lines, plane, most, rows)
+    select_full = (
+        select.transpose(1, 0, 2, 3)[:, :, :, None, :] & same[None, :, None, :, None]
+    ).reshape(plane * cap, lines * rows)
+    weight = weight.reshape(lines, plane, most, rows).transpose(1, 0, 2, 3)
+    weight_full = jnp.where(
+        same[None, :, None, :, None], weight[:, :, :, None, :], 0.0
+    ).reshape(plane * cap, lines * rows)
+    outgoing = jnp.dot(
+        select_full.astype(jnp.bfloat16), line_normed, preferred_element_type=jnp.float32
+    ).astype(jnp.bfloat16)
+    outgoing = outgoing.reshape(plane, cap, width)
+
     gate_up = dequant(w_in[0], scale_in[0])
     down_proj = dequant(w_out[0], scale_out[0])
     hidden_width = down_proj.shape[0]
-    block = lax.all_to_all(
-        outgoing, ("dp", "expert", "tensor"), split_axis=0, concat_axis=0, tiled=True
-    )
+    block = lax.all_to_all(outgoing, ("dp", "expert"), split_axis=0, concat_axis=0, tiled=True)
     flat = block.reshape(-1, width)
     mixed_in = jnp.dot(flat, gate_up, preferred_element_type=jnp.float32)
     hidden = (jax.nn.silu(mixed_in[:, :hidden_width]) * mixed_in[:, hidden_width:]).astype(
@@ -63,16 +88,19 @@
     )
     output = jnp.dot(hidden, down_proj, preferred_element_type=jnp.float32).astype(jnp.bfloat16)
     send_block = output.reshape(block.shape)
-    back = lax.all_to_all(
-        send_block, ("dp", "expert", "tensor"), split_axis=0, concat_axis=0, tiled=True
-    )
-    returned_rows = (
-        jnp.take(back.reshape(-1, width), target, axis=0)
-        .astype(jnp.float32)
-        .reshape(rows, top, width)
-    )
-    combined = jnp.sum(returned_rows * gate_weights[:, :, None], axis=1)
+    back = lax.all_to_all(send_block, ("dp", "expert"), split_axis=0, concat_axis=0, tiled=True)
+    back = back.reshape(-1, width)
+
+    weight_top = lax.reduce_precision(weight_full, exponent_bits=8, mantissa_bits=7)
+    weight_hi = weight_top.astype(jnp.bfloat16)
+    weight_lo = (weight_full - weight_top).astype(jnp.bfloat16)
+    contract = (((0,), (0,)), ((), ()))
+    partial = lax.dot_general(
+        weight_hi, back, contract, preferred_element_type=jnp.float32
+    ) + lax.dot_general(weight_lo, back, contract, preferred_element_type=jnp.float32)
+    combined = lax.psum_scatter(partial, "tensor", scatter_dimension=0, tiled=True)
     mixed = (x_float + combined).astype(jnp.bfloat16)
+
     local_sync = w_sync.reshape(width, -1)
     proj = jnp.dot(
         lax.all_gather(mixed, "tensor", axis=0, tiled=True),

time: 538 us -> 470 us (0.87)
  waiting for transfers between devices: 390 us -> 305 us
  matrix products: 52.2 us -> 70.8 us
  blocking collectives: 10 us -> 25.1 us
  local copies, waits for them, and re-layouts: 30.9 us -> 17.1 us
  starting transfers between devices: 16.4 us -> 10.7 us
    all_to_all x2, waiting for transfers between devices: 345 us -> 164 us  [the longest x1 86.9 us: shards(): lax.all_to_all(send_block, ('dp', 'expert'), split_axis=0, concat_axis=0,...]
    reduce_scatter x0 -> x1, waiting for transfers between devices: none -> 73.6 us  [shards(): lax.psum_scatter(partial, 'tensor', scatter_dimension=0, tiled=True)]
    all_gather x0 -> x1, waiting for transfers between devices: none -> 25.7 us  [shards(): line_normed = lax.all_gather(normed, 'tensor', axis=0, tiled=True)]
    dot_general x1 -> x3, matrix products: 6.68 us -> 25.3 us  [the longest x1 9.51 us: shards(): lax.dot_general(weight_lo, back, contract, preferred_element_type=jnp.flo...]
    all_gather x0 -> x1, blocking collectives: none -> 15.1 us  [shards(): line_routing = lax.all_gather(routing, 'tensor', axis=0, tiled=False)]
    gather x1 -> x0, local copies, waits for them, and re-layouts: 13.4 us -> none  [shards(): jnp.take(back.reshape(-1, width), target, axis=0).astype(jnp.float32)]
    convert_element_type x1 -> x3, other arithmetic: 0.01 us -> 6.44 us  [the longest x1 3.72 us: shards(): weight_lo = (weight_full - weight_top).astype(jnp.bfloat16)]
    all_to_all x2, starting transfers between devices: 16.1 us -> 10.1 us  [the longest x1 5.18 us: shards(): lax.all_to_all(outgoing, ('dp', 'expert'), split_axis=0, concat_axis=0, t...]
  transfers between devices with their start and end apart: 3 -> 5, of which waited for: 3 -> 5; matrix products, arithmetic and copies ran while one was open for 4% -> 8% of each run, Pallas kernels for 0% -> 0%
where the time goes in v1:
time: 470 us; the launch traced here: 469 us
  waiting for transfers between devices  305 us (65%)
  matrix products  70.8 us (15%)
  other arithmetic  26.9 us (6%)
  blocking collectives  25.1 us (5%)
  local copies, waits for them, and re-layouts  17.1 us (4%)
  between operations  14 us (3%)
  starting transfers between devices  10.7 us (2%)
    all_to_all x1, waiting for transfers between devices, shards(): lax.all_to_all(send_block, ('dp', 'expert'), split_axis=0, concat_axis=0,...  86.9 us
    all_to_all x1, waiting for transfers between devices, shards(): lax.all_to_all(outgoing, ('dp', 'expert'), split_axis=0, concat_axis=0, t...  77.3 us
    reduce_scatter x1, waiting for transfers between devices, shards(): lax.psum_scatter(partial, 'tensor', scatter_dimension=0, tiled=True)  73.6 us
    all_gather x1, waiting for transfers between devices, shards(): lax.all_gather(mixed, 'tensor', axis=0, tiled=True)  41.2 us
    all_gather x1, waiting for transfers between devices, shards(): line_normed = lax.all_gather(normed, 'tensor', axis=0, tiled=True)  25.7 us
    dot_general x1, matrix products, shards(): mixed_in = jnp.dot(flat, gate_up, preferred_element_type=jnp.float32)  19.3 us
    dot_general x1, matrix products, shards(): jnp.dot(hidden, down_proj, preferred_element_type=jnp.float32)  15.7 us
    all_gather x1, blocking collectives, shards(): line_routing = lax.all_gather(routing, 'tensor', axis=0, tiled=False)  15.1 us
  transfers between devices with their start and end apart: 5, of which 5 were waited for; matrix products, arithmetic and copies ran while one was open for 8% of the time, Pallas kernels for 0%

profile of v1, /device:TPU:0, one launch (start us, length us, event | category | flops | bytes accessed | tf_op | source)
XLA Modules:
  0.0 469.4 jit_solution(4436198014707928312)
XLA Ops:
  8.4 2.0 fusion.39
  13.5 15.1 %all-gather = f32[512,24]{0,1:T(8,128)S(1)} all-gather(f32[128,24]{0,1:T(8,128)S(1)} %pad_maximum_fusion), channel_id=2, replica_groups=mesh['dp'=4,'expert'=2,'tensor'=4] {'tensor'}, dimensions={0}, use_global_device_ids=true | all-gather | bytes 61440 | tf_op jit(solution)/shard_map/all_gather | solution.py:54
  28.7 3.9 fusion.1
  34.1 25.7 %all-gather.4.cloned.1.call-done = bf16[512,2048]{1,0:T(8,128)(2,1)} async-done(((bf16[128,2048]{1,0:T(8,128)(2,1)}), bf16[512,2048]{1,0:T(8,128)(2,1)}) %all-gather.4.cloned.1.call-update) | async-done | bytes 2097168 | tf_op jit(solution)/shard_map/all_gather | solution.py:53
  59.8 8.2 %convolution_convert_fusion.1 = bf16[2048,2048]{1,0:T(8,128)(2,1)} fusion(bf16[512,2048]{1,0:T(8,128)(2,1)} %all-gather.4.cloned.1.call-done, pred[256,8,4,128]{3,2,1,0:T(4,128)(4,1)S(1)} %bitcast.97), kind=kOutput, calls=%fused_computation.6 | convolution fusion | flops 4299161600 | bytes 11534336 | tf_op jit(solution)/shard_map/dot_general | solution.py:75
  68.0 5.2 %all-to-all-start = ((bf16[8,256,2048]{2,1,0:T(8,128)(2,1)}), bf16[8,256,2048]{2,1,0:T(8,128)(2,1)}, u32[]{:S(2)}, u32[]{:S(2)}) async-start(bf16[8,256,2048]{2,1,0:T(8,128)(2,1)} %bitcast.88), calls=%async_computation | async-start | bytes 16777216 | tf_op jit(solution)/shard_map/all_to_all | solution.py:83
  73.3 8.7 %copy.39 = bf16[1,2048,1536]{1,2,0:T(8,128)(2,1)} copy(bf16[1,2048,1536]{2,1,0:T(8,128)(2,1)} %param.16) | data formatting | bytes 12582912 | tf_op args[4]
  82.1 7.7 %fusion = bf16[2048,12,128]{0,2,1:T(8,128)(2,1)} fusion(bf16[2048,12,128]{0,2,1:T(8,128)(2,1)} %bitcast.85, f32[2048,12]{0,1:T(8,128)S(1)} %bitcast.98), kind=kLoop, calls=%fused_computation.1 | loop fusion | flops 9437184 | bytes 12681216 | tf_op jit(solution)/shard_map/convert_element_type | solution.py:10
  89.8 77.3 %all-to-all-done = bf16[8,256,2048]{2,1,0:T(8,128)(2,1)} async-done(((bf16[8,256,2048]{2,1,0:T(8,128)(2,1)}), bf16[8,256,2048]{2,1,0:T(8,128)(2,1)}, u32[]{:S(2)}, u32[]{:S(2)}) %all-to-all-start) | async-done | bytes 8388640 | tf_op jit(solution)/shard_map/all_to_all | solution.py:83
  167.1 19.3 %fusion.61 = f32[2048,1536]{1,0:T(8,128)} fusion(bf16[2048,2048]{1,0:T(8,128)(2,1)} %bitcast.5, bf16[2048,1536]{0,1:T(8,128)(2,1)} %bitcast.89), kind=kOutput, calls=%fused_computation.88 | convolution fusion | flops 12884901888 | bytes 27262976 | tf_op jit(solution)/shard_map/dot_general | solution.py:85
  188.3 15.7 %convolution_convert_fusion = bf16[2048,2048]{1,0:T(8,128)(2,1)} fusion(f32[2048,1536]{1,0:T(8,128)} %fusion.61, f32[96,8,16,128]{3,2,1,0:T(8,128)S(1)} %bitcast.90, bf16[1,768,2048]{2,1,0:T(8,128)(2,1)S(1)} %copy-done.4), kind=kOutput, calls=%fused_computation.5 | convolution fusion | flops 6460801024 | bytes 30408704 | tf_op jit(solution)/shard_map/dot_general | solution.py:89
  204.0 4.9 %all-to-all-start.1 = ((bf16[8,256,2048]{2,1,0:T(8,128)(2,1)}), bf16[8,256,2048]{2,1,0:T(8,128)(2,1)}, u32[]{:S(2)}, u32[]{:S(2)}) async-start(bf16[8,256,2048]{2,1,0:T(8,128)(2,1)} %bitcast.87), calls=%async_computation.1 | async-start | bytes 16777216 | tf_op jit(solution)/shard_map/all_to_all | solution.py:91
  209.3 3.1 select_reduce_fusion
  212.4 3.7 fusion.6
  216.1 86.9 %all-to-all-done.1 = bf16[8,256,2048]{2,1,0:T(8,128)(2,1)} async-done(((bf16[8,256,2048]{2,1,0:T(8,128)(2,1)}), bf16[8,256,2048]{2,1,0:T(8,128)(2,1)}, u32[]{:S(2)}, u32[]{:S(2)}) %all-to-all-start.1) | async-done | bytes 8388640 | tf_op jit(solution)/shard_map/all_to_all | solution.py:91
  303.0 7.6 %fusion.18 = f32[512,2048]{1,0:T(8,128)S(1)} fusion(bf16[2048,2048]{1,0:T(8,128)(2,1)} %bitcast.11, bf16[256,8,4,128]{3,2,1,0:T(4,128)(2,1)} %bitcast.94), kind=kOutput, calls=%fused_computation.27 | convolution fusion | flops 4294967296 | bytes 14680064 | tf_op jit(solution)/shard_map/dot_general | solution.py:98
  310.7 9.5 %convolution_add_fusion = f32[512,2048]{1,0:T(8,128)} fusion(f32[512,2048]{1,0:T(8,128)S(1)} %fusion.18, bf16[2048,2048]{1,0:T(8,128)(2,1)} %bitcast.11, bf16[256,8,4,128]{3,2,1,0:T(4,128)(2,1)S(1)} %bitcast.86), kind=kOutput, calls=%fused_computation.24 | convolution fusion | flops 4296015872 | bytes 18874368 | tf_op jit(solution)/shard_map/dot_general | solution.py:100
  320.5 73.6 %reduce-scatter.2.cloned.1.call-done = f32[128,2048]{1,0:T(8,128)} async-done(((f32[512,2048]{1,0:T(8,128)}), f32[128,2048]{1,0:T(8,128)}) %reduce-scatter.2.cloned.1.call-update) | async-done | bytes 1048592 | tf_op jit(solution)/shard_map/reduce_scatter | solution.py:101
  394.2 2.1 fusion.40
  396.3 5.3 %copy.52 = bf16[256,8,2,512]{3,1,2,0:T(8,128)(2,1)} copy(bf16[256,8,2,512]{3,2,1,0:T(2,128)(2,1)} %bitcast.91) | data formatting | bytes 8388608
  401.7 41.2 %all-gather.6.cloned.1.call-done = bf16[512,2048]{1,0:T(8,128)(2,1)} async-done(((bf16[128,2048]{1,0:T(8,128)(2,1)}), bf16[512,2048]{1,0:T(8,128)(2,1)}) %all-gather.6.cloned.1.call-update) | async-done | bytes 2097168 | tf_op jit(solution)/shard_map/all_gather | solution.py:106
  442.9 5.2 %convolution_convert_fusion.2 = bf16[512,1024]{1,0:T(8,128)(2,1)S(1)} fusion(bf16[512,2048]{1,0:T(8,128)(2,1)} %all-gather.6.cloned.1.call-done, bf16[2048,1024]{1,0:T(8,128)(2,1)} %bitcast.92), kind=kOutput, calls=%fused_computation.34 | convolution fusion | flops 2148007936 | bytes 7340032 | tf_op jit(solution)/shard_map/dot_general | solution.py:105
  449.1 3.7 fusion.34
  452.8 10.0 %psum.7 = f32[1,21]{1,0:T(1,128)} all-reduce(f32[1,21]{1,0:T(1,128)S(1)} %bitcast.104), channel_id=1, replica_groups=mesh['dp'=4,'expert'=2,'tensor'=4] {'tensor'}, use_global_device_ids=true, to_apply=%region_6.7 | all-reduce | flops 21 | bytes 168 | tf_op jit(solution)/shard_map/psum | solution.py:146
  (49 shorter events, 9.5 us)
Async XLA Ops:
  7.2 52.6 %all-gather.4.cloned.1.call-start = ((), (), s32[]{:S(2)}) async-start(), calls=%async_computation.3 | async-start | bytes 2621440 | tf_op jit(solution)/shard_map/all_gather | solution.py:53
  68.0 99.1 %all-to-all-start = ((bf16[8,256,2048]{2,1,0:T(8,128)(2,1)}), bf16[8,256,2048]{2,1,0:T(8,128)(2,1)}, u32[]{:S(2)}, u32[]{:S(2)}) async-start(bf16[8,256,2048]{2,1,0:T(8,128)(2,1)} %bitcast.88), calls=%async_computation | async-start | bytes 16777216 | tf_op jit(solution)/shard_map/all_to_all | solution.py:83
  73.2 8.7 %copy-start.1 = (f32[1,16,12]{1,0,2:T(1,128)S(1)}, f32[1,16,12]{1,0,2:T(1,128)}, u32[]{:S(2)}) copy-start(f32[1,16,12]{1,0,2:T(1,128)} %param.17) | copy-start | bytes 2308
  73.2 8.8 %copy-start.2 = (f32[1,6,16]{2,0,1:T(1,128)S(1)}, f32[1,6,16]{2,0,1:T(1,128)}, u32[]{:S(2)}) copy-start(f32[1,6,16]{2,0,1:T(1,128)} %param.19) | copy-start | bytes 1156
  186.4 1.9 copy-start.4
  204.0 99.0 %all-to-all-start.1 = ((bf16[8,256,2048]{2,1,0:T(8,128)(2,1)}), bf16[8,256,2048]{2,1,0:T(8,128)(2,1)}, u32[]{:S(2)}, u32[]{:S(2)}) async-start(bf16[8,256,2048]{2,1,0:T(8,128)(2,1)} %bitcast.87), calls=%async_computation.1 | async-start | bytes 16777216 | tf_op jit(solution)/shard_map/all_to_all | solution.py:91
  209.0 185.2 %reduce-scatter.2.cloned.1.call-start = ((), (), s32[]{:S(2)}) async-start(), calls=%async_computation.4 | async-start | bytes 5242880 | tf_op jit(solution)/shard_map/reduce_scatter | solution.py:101
  310.7 83.5 %copy-start = (bf16[128,2048]{1,0:T(8,128)(2,1)S(1)}, bf16[128,2048]{1,0:T(8,128)(2,1)}, u32[]{:S(2)}) copy-start(bf16[128,2048]{1,0:T(8,128)(2,1)} %param.12) | copy-start | bytes 1572868
  320.2 81.4 %copy-start.5 = (s32[21]{0:T(128)S(1)}, s32[21]{0:T(128)}, u32[]{:S(2)}) copy-start(s32[21]{0:T(128)} %param.23) | copy-start | bytes 256
  320.2 81.5 %copy-start.3 = (s32[1,2,256]{2,1,0:T(2,128)S(1)}, s32[1,2,256]{2,1,0:T(2,128)}, u32[]{:S(2)}) copy-start(s32[1,2,256]{2,1,0:T(2,128)} %param.22) | copy-start | bytes 6148
  320.2 122.7 %all-gather.6.cloned.1.call-start = ((), (), s32[]{:S(2)}) async-start(), calls=%async_computation.5 | async-start | bytes 2621440 | tf_op jit(solution)/shard_map/all_gather | solution.py:106
  442.9 6.2 %copy-start.6 = (f32[4]{0:T(128)S(1)}, f32[4]{0:T(128)}, u32[]{:S(2)}) copy-start(f32[4]{0:T(128)} %param.21) | copy-start | bytes 52
Sparse Core Ops, SparseCore 0:
  10.6 49.1 all-gather.3
  320.3 73.7 reduce-scatter.1
  396.4 46.4 all-gather.5

commit v2 on v1

--- a/solution.py
+++ b/solution.py
@@ -46,66 +46,110 @@
     earlier = (pair_index[None, :] < pair_index[:, None]).astype(jnp.bfloat16)
     before = jnp.dot(earlier, onehot, preferred_element_type=jnp.float32)
     slots = jnp.sum(before * onehot.astype(jnp.float32), axis=1).reshape(rows, top)
+    gate = gate_weights.astype(jnp.float32)
+    gate_top = lax.reduce_precision(gate, exponent_bits=8, mantissa_bits=7)
     routing = jnp.concatenate(
-        [expert_ids.astype(jnp.float32), slots, gate_weights.astype(jnp.float32)], axis=1
-    )
-
-    line_normed = lax.all_gather(normed, "tensor", axis=0, tiled=True)
-    line_routing = lax.all_gather(routing, "tensor", axis=0, tiled=False)
+        [
+            expert_ids.astype(jnp.bfloat16),
+            slots.astype(jnp.bfloat16),
+            gate_top.astype(jnp.bfloat16),
+            (gate - gate_top).astype(jnp.bfloat16),
+        ],
+        axis=1,
+    )
+    extra = rows * 4 * top // width
+    padded = rows + 16
+    packed = jnp.concatenate(
+        [
+            normed,
+            routing.reshape(extra, width),
+            jnp.zeros((padded - rows - extra, width), jnp.bfloat16),
+        ],
+        axis=0,
+    )
+    line = lax.all_gather(packed, "tensor", axis=0, tiled=False)
+    line_routing = line[:, rows : rows + extra, :].reshape(lines, rows, 4 * top)
     ids_l = line_routing[:, :, :top].astype(jnp.int32)
     slot_l = line_routing[:, :, top : 2 * top].astype(jnp.int32)
-    gate_l = line_routing[:, :, 2 * top :]
+    gate_hi = line_routing[:, :, 2 * top : 3 * top].astype(jnp.float32)
+    gate_lo = line_routing[:, :, 3 * top :].astype(jnp.float32)
     mine = (ids_l % lines) == here
     target = jnp.where(mine, (ids_l // lines) * most + slot_l, -1)
     slot_ids = jnp.arange(plane * most, dtype=jnp.int32)
     match = target[:, None, :, :] == slot_ids[None, :, None, None]
     select = jnp.any(match, axis=3)
-    weight = jnp.sum(jnp.where(match, gate_l[:, None, :, :], 0.0), axis=3)
+    weight_hi = jnp.sum(jnp.where(match, gate_hi[:, None, :, :], 0.0), axis=3)
+    weight_lo = jnp.sum(jnp.where(match, gate_lo[:, None, :, :], 0.0), axis=3)
     same = (
         jnp.arange(lines, dtype=jnp.int32)[:, None] == jnp.arange(lines, dtype=jnp.int32)[None, :]
     )
-    select = select.reshape(lines, plane, most, rows)
+    select = select.reshape(lines, plane, most, rows).transpose(1, 0, 2, 3)
+    select = jnp.pad(select, ((0, 0), (0, 0), (0, 0), (0, padded - rows)))
     select_full = (
-        select.transpose(1, 0, 2, 3)[:, :, :, None, :] & same[None, :, None, :, None]
-    ).reshape(plane * cap, lines * rows)
-    weight = weight.reshape(lines, plane, most, rows).transpose(1, 0, 2, 3)
-    weight_full = jnp.where(
-        same[None, :, None, :, None], weight[:, :, :, None, :], 0.0
-    ).reshape(plane * cap, lines * rows)
-    outgoing = jnp.dot(
-        select_full.astype(jnp.bfloat16), line_normed, preferred_element_type=jnp.float32
-    ).astype(jnp.bfloat16)
-    outgoing = outgoing.reshape(plane, cap, width)
-
+        (select[:, :, :, None, :] & same[None, :, None, :, None])
+        .reshape(plane * cap, lines * padded)
+        .astype(jnp.bfloat16)
+    )
+
+    def spread(weight):
+        weight = weight.reshape(lines, plane, most, rows).transpose(1, 0, 2, 3)
+        return (
+            jnp.where(same[None, :, None, :, None], weight[:, :, :, None, :], 0.0)
+            .reshape(plane * cap, lines * rows)
+            .astype(jnp.bfloat16)
+        )
+
+    weight_hi = spread(weight_hi)
+    weight_lo = spread(weight_lo)
+    line_flat = line.reshape(lines * padded, width)
+    half = width // 2
     gate_up = dequant(w_in[0], scale_in[0])
     down_proj = dequant(w_out[0], scale_out[0])
     hidden_width = down_proj.shape[0]
-    block = lax.all_to_all(outgoing, ("dp", "expert"), split_axis=0, concat_axis=0, tiled=True)
-    flat = block.reshape(-1, width)
-    mixed_in = jnp.dot(flat, gate_up, preferred_element_type=jnp.float32)
+    group = ("dp", "expert")
+
+    def send(part):
+        moved = lax.all_to_all(
+            part.reshape(plane, cap, part.shape[1]), group, split_axis=0, concat_axis=0, tiled=True
+        )
+        return moved.reshape(plane * cap, part.shape[1])
+
+    blocks = [
+        send(
+            jnp.dot(
+                select_full, line_flat[:, h * half : (h + 1) * half], preferred_element_type=jnp.float32
+            ).astype(jnp.bfloat16)
+        )
+        for h in range(2)
+    ]
+    mixed_in = jnp.dot(blocks[0], gate_up[:half], preferred_element_type=jnp.float32) + jnp.dot(
+        blocks[1], gate_up[half:], preferred_element_type=jnp.float32
+    )
     hidden = (jax.nn.silu(mixed_in[:, :hidden_width]) * mixed_in[:, hidden_width:]).astype(
         jnp.bfloat16
     )
-    output = jnp.dot(hidden, down_proj, preferred_element_type=jnp.float32).astype(jnp.bfloat16)
-    send_block = output.reshape(block.shape)
-    back = lax.all_to_all(send_block, ("dp", "expert"), split_axis=0, concat_axis=0, tiled=True)
-    back = back.reshape(-1, width)
-
-    weight_top = lax.reduce_precision(weight_full, exponent_bits=8, mantissa_bits=7)
-    weight_hi = weight_top.astype(jnp.bfloat16)
-    weight_lo = (weight_full - weight_top).astype(jnp.bfloat16)
     contract = (((0,), (0,)), ((), ()))
-    partial = lax.dot_general(
-        weight_hi, back, contract, preferred_element_type=jnp.float32
-    ) + lax.dot_general(weight_lo, back, contract, preferred_element_type=jnp.float32)
-    combined = lax.psum_scatter(partial, "tensor", scatter_dimension=0, tiled=True)
-    mixed = (x_float + combined).astype(jnp.bfloat16)
+    mixed_parts = []
+    for h in range(2):
+        output = jnp.dot(
+            hidden, down_proj[:, h * half : (h + 1) * half], preferred_element_type=jnp.float32
+        ).astype(jnp.bfloat16)
+        back = send(output)
+        partial = lax.dot_general(
+            weight_hi, back, contract, preferred_element_type=jnp.float32
+        ) + lax.dot_general(weight_lo, back, contract, preferred_element_type=jnp.float32)
+        combined = lax.psum_scatter(partial, "tensor", scatter_dimension=0, tiled=True)
+        mixed_parts.append((x_float[:, h * half : (h + 1) * half] + combined).astype(jnp.bfloat16))
+    mixed = jnp.concatenate(mixed_parts, axis=1)
 
     local_sync = w_sync.reshape(width, -1)
-    proj = jnp.dot(
-        lax.all_gather(mixed, "tensor", axis=0, tiled=True),
-        local_sync,
-        preferred_element_type=jnp.float32,
+    proj = sum(
+        jnp.dot(
+            lax.all_gather(mixed_parts[h], "tensor", axis=0, tiled=True),
+            local_sync[h * half : (h + 1) * half],
+            preferred_element_type=jnp.float32,
+        )
+        for h in range(2)
     ).astype(jnp.bfloat16)
     half = proj.shape[1] // 2
     heads_here = head_weight.shape[0]

time: 470 us -> 465 us (0.989); the launches traced: 469 us -> 456 us
  waiting for transfers between devices: 305 us -> 267 us
  blocking collectives: 25.1 us -> 10.8 us
  matrix products: 70.8 us -> 81.2 us
  local copies, waits for them, and re-layouts: 17.1 us -> 26.9 us
  other arithmetic: 26.9 us -> 35.7 us
  starting transfers between devices: 10.7 us -> 19.5 us
    all_to_all x2 -> x4, waiting for transfers between devices: 164 us -> 130 us  [send(): lax.all_to_all(part.reshape(plane, cap, part.shape[1]), group, split_axis...]
    reduce_scatter x1 -> x2, waiting for transfers between devices: 73.6 us -> 40.9 us  [shards(): lax.psum_scatter(partial, 'tensor', scatter_dimension=0, tiled=True)]
    all_gather x2 -> x3, waiting for transfers between devices: 66.9 us -> 96 us  [the longest x1 53.3 us: shards(): line = lax.all_gather(packed, 'tensor', axis=0, tiled=False)]
    all_gather x1 -> x0, blocking collectives: 15.1 us -> none  [shards(): line_routing = lax.all_gather(routing, 'tensor', axis=0, tiled=False)]
    all_to_all x2 -> x4, starting transfers between devices: 10.1 us -> 18.8 us  [send(): lax.all_to_all(part.reshape(plane, cap, part.shape[1]), group, split_axis...]
    slice x2 -> x3, local copies, waits for them, and re-layouts: 0.01 us -> 5.75 us  [the longest x1 4.68 us: shards(): local_sync[h * half:(h + 1) * half]]
    dot_general x4 -> x8, matrix products: 48.4 us -> 53.8 us  [the longest x2 12.5 us: shards(): jnp.dot(select_full, line_flat[:, h * half:(h + 1) * half], preferred_ele...]
    dot_general x1 -> x2, matrix products: 7.6 us -> 11.8 us  [shards(): lax.dot_general(weight_hi, back, contract, preferred_element_type=jnp.flo...]
  transfers between devices with their start and end apart: 5 -> 9, of which waited for: 5 -> 8; matrix products, arithmetic and copies ran while one was open for 8% -> 19% of each run, Pallas kernels for 0% -> 0%
where the time goes in v2:
time: 465 us; the launch traced here: 456 us
  waiting for transfers between devices  267 us (57%)
  matrix products  81.2 us (17%)
  other arithmetic  35.7 us (8%)
  local copies, waits for them, and re-layouts  26.9 us (6%)
  starting transfers between devices  19.5 us (4%)
  between operations  14.7 us (3%)
  blocking collectives  10.8 us (2%)
    all_to_all x4, waiting for transfers between devices, send(): lax.all_to_all(part.reshape(plane, cap, part.shape[1]), group, split_axis...  130 us
    all_gather x1, waiting for transfers between devices, shards(): line = lax.all_gather(packed, 'tensor', axis=0, tiled=False)  53.3 us
    all_gather x2, waiting for transfers between devices, shards(): lax.all_gather(mixed_parts[h], 'tensor', axis=0, tiled=True)  42.7 us
    reduce_scatter x2, waiting for transfers between devices, shards(): lax.psum_scatter(partial, 'tensor', scatter_dimension=0, tiled=True)  40.9 us
    all_to_all x4, starting transfers between devices, send(): lax.all_to_all(part.reshape(plane, cap, part.shape[1]), group, split_axis...  18.8 us
    unnamed x44, local copies, waits for them, and re-layouts  15.2 us
    dot_general x2, matrix products, shards(): jnp.dot(select_full, line_flat[:, h * half:(h + 1) * half], preferred_ele...  12.5 us
    dot_general x2, matrix products, shards(): lax.dot_general(weight_hi, back, contract, preferred_element_type=jnp.flo...  11.8 us
  transfers between devices with their start and end apart: 9, of which 8 were waited for; matrix products, arithmetic and copies ran while one was open for 19% of the time, Pallas kernels for 0%

profile of v2, /device:TPU:0, one launch (start us, length us, event | category | flops | bytes accessed | tf_op | source)
XLA Modules:
  0.0 456.2 jit_solution(1475538238732239450)
XLA Ops:
  14.1 53.3 %all-gather.9.cloned.1.call-done = bf16[576,2048]{1,0:T(8,128)(2,1)} async-done(((bf16[144,2048]{1,0:T(8,128)(2,1)}), bf16[576,2048]{1,0:T(8,128)(2,1)}) %all-gather.9.cloned.1.call-update) | async-done | bytes 2359312 | tf_op jit(solution)/shard_map/all_gather | solution.py:70
  79.1 6.2 %convolution_convert_fusion.1 = bf16[2048,1024]{1,0:T(8,128)(2,1)} fusion(pred[2048,576]{1,0:T(32,128)(4,1)S(1)} %and.33, bf16[576,2048]{1,0:T(8,128)(2,1)} %all-gather.9.cloned.1.call-done), kind=kOutput, calls=%fused_computation.19 | convolution fusion | flops 2418016256 | bytes 6553600 | tf_op jit(solution)/shard_map/dot_general | solution.py:119
  89.9 6.3 %convolution_convert_fusion = bf16[2048,1024]{1,0:T(8,128)(2,1)} fusion(pred[2048,576]{1,0:T(32,128)(4,1)S(1)} %and.33, bf16[576,2048]{1,0:T(8,128)(2,1)} %all-gather.9.cloned.1.call-done), kind=kOutput, calls=%fused_computation.18 | convolution fusion | flops 2418016256 | bytes 6553600 | tf_op jit(solution)/shard_map/dot_general | solution.py:119
  96.1 42.8 %all-to-all-done = bf16[8,256,1024]{2,1,0:T(8,128)(2,1)} async-done(((bf16[8,256,1024]{2,1,0:T(8,128)(2,1)}), bf16[8,256,1024]{2,1,0:T(8,128)(2,1)}, u32[]{:S(2)}, u32[]{:S(2)}) %all-to-all-start) | async-done | bytes 4194336 | tf_op jit(solution)/shard_map/all_to_all | solution.py:112
  139.0 5.0 %all-to-all-start.1 = ((bf16[8,256,1024]{2,1,0:T(8,128)(2,1)}), bf16[8,256,1024]{2,1,0:T(8,128)(2,1)}, u32[]{:S(2)}, u32[]{:S(2)}) async-start(bf16[8,256,1024]{2,1,0:T(8,128)(2,1)} %bitcast.105), calls=%async_computation.1 | async-start | bytes 8388608 | tf_op jit(solution)/shard_map/all_to_all | solution.py:112
  144.0 8.7 %copy.66 = bf16[1,2048,1536]{1,2,0:T(8,128)(2,1)} copy(bf16[1,2048,1536]{2,1,0:T(8,128)(2,1)} %param.16) | data formatting | bytes 12582912 | tf_op args[4]
  165.9 11.6 %fusion.8 = f32[2048,1536]{1,0:T(8,128)} fusion(bf16[2048,1024]{1,0:T(8,128)(2,1)} %bitcast.6, bf16[2048,1536]{0,1:T(8,128)(2,1)S(1)} %fusion), kind=kOutput, calls=%fused_computation.23 | convolution fusion | flops 6442450944 | bytes 19922944 | tf_op jit(solution)/shard_map/dot_general | solution.py:125
  177.5 15.7 %all-to-all-done.1 = bf16[8,256,1024]{2,1,0:T(8,128)(2,1)} async-done(((bf16[8,256,1024]{2,1,0:T(8,128)(2,1)}), bf16[8,256,1024]{2,1,0:T(8,128)(2,1)}, u32[]{:S(2)}, u32[]{:S(2)}) %all-to-all-start.1) | async-done | bytes 4194336 | tf_op jit(solution)/shard_map/all_to_all | solution.py:112
  193.1 11.7 %convolution_add_fusion = f32[2048,1536]{1,0:T(8,128)S(1)} fusion(f32[2048,1536]{1,0:T(8,128)} %fusion.8, bf16[2048,1024]{1,0:T(8,128)(2,1)} %bitcast.10, bf16[2048,1536]{0,1:T(8,128)(2,1)} %copy-done), kind=kOutput, calls=%fused_computation.2 | convolution fusion | flops 6445596672 | bytes 32505856 | tf_op jit(solution)/shard_map/dot_general | solution.py:125
  207.0 5.3 %convolution_convert_fusion.3 = bf16[2048,1024]{1,0:T(8,128)(2,1)} fusion(bf16[2048,768]{1,0:T(8,128)(2,1)S(1)} %fusion.3, bf16[768,2048]{1,0:T(8,128)(2,1)S(1)} %copy-done.3), kind=kOutput, calls=%fused_computation.21 | convolution fusion | flops 3223322624 | bytes 8912896 | tf_op jit(solution)/shard_map/dot_general | solution.py:134
  212.3 4.7 %all-to-all-start.2 = ((bf16[8,256,1024]{2,1,0:T(8,128)(2,1)}), bf16[8,256,1024]{2,1,0:T(8,128)(2,1)}, u32[]{:S(2)}, u32[]{:S(2)}) async-start(bf16[8,256,1024]{2,1,0:T(8,128)(2,1)} %bitcast.104), calls=%async_computation.2 | async-start | bytes 8388608 | tf_op jit(solution)/shard_map/all_to_all | solution.py:112
  217.4 6.0 %select_reduce_fusion.1 = (bf16[4,512,128]{2,1,0:T(8,128)(2,1)S(1)}, bf16[4,512,128]{2,1,0:T(8,128)(2,1)S(1)}) fusion(f32[4,128,8]{1,2,0:T(8,128)S(1)} %convert_element_type.140, s32[4,128,8]{1,2,0:T(8,128)S(1)} %copy.62, f32[4,128,8]{1,2,0:T(8,128)S(1)} %convert_element_type.153), kind=kLoop, calls=%fused_computation.4 | loop fusion | flops 9961472 | bytes 1097728 | tf_op jit(solution)/shard_map/reduce_sum | solution.py:81
  227.2 5.0 %convolution_convert_fusion.2 = bf16[2048,1024]{1,0:T(8,128)(2,1)} fusion(bf16[2048,768]{1,0:T(8,128)(2,1)S(1)} %copy-done.6, bf16[768,2048]{1,0:T(8,128)(2,1)S(1)} %copy-done.4), kind=kOutput, calls=%fused_computation.20 | convolution fusion | flops 3223322624 | bytes 8912896 | tf_op jit(solution)/shard_map/dot_general | solution.py:134
  232.2 34.0 %all-to-all-done.2 = bf16[8,256,1024]{2,1,0:T(8,128)(2,1)} async-done(((bf16[8,256,1024]{2,1,0:T(8,128)(2,1)}), bf16[8,256,1024]{2,1,0:T(8,128)(2,1)}, u32[]{:S(2)}, u32[]{:S(2)}) %all-to-all-start.2) | async-done | bytes 4194336 | tf_op jit(solution)/shard_map/all_to_all | solution.py:112
  270.9 5.2 %fusion.14 = f32[512,1024]{1,0:T(8,128)S(1)} fusion(bf16[2048,1024]{1,0:T(8,128)(2,1)} %bitcast.14, bf16[256,8,4,128]{3,2,1,0:T(4,128)(2,1)} %bitcast.110), kind=kOutput, calls=%fused_computation.29 | convolution fusion | flops 2147483648 | bytes 8388608 | tf_op jit(solution)/shard_map/dot_general | solution.py:140
  276.1 5.8 %fusion.26 = f32[512,1024]{1,0:T(8,128)} fusion(f32[512,1024]{1,0:T(8,128)S(1)} %fusion.14, bf16[2048,1024]{1,0:T(8,128)(2,1)} %bitcast.14, bf16[256,8,4,128]{3,2,1,0:T(4,128)(2,1)S(1)} %bitcast.108), kind=kOutput, calls=%fused_computation.42 | convolution fusion | flops 2148007936 | bytes 10485760 | tf_op jit(solution)/shard_map/dot_general | solution.py:138
  282.0 37.8 %all-to-all-done.3 = bf16[8,256,1024]{2,1,0:T(8,128)(2,1)} async-done(((bf16[8,256,1024]{2,1,0:T(8,128)(2,1)}), bf16[8,256,1024]{2,1,0:T(8,128)(2,1)}, u32[]{:S(2)}, u32[]{:S(2)}) %all-to-all-start.3) | async-done | bytes 4194336 | tf_op jit(solution)/shard_map/all_to_all | solution.py:112
  319.8 5.2 %fusion.12 = f32[512,1024]{1,0:T(8,128)S(1)} fusion(bf16[2048,1024]{1,0:T(8,128)(2,1)} %bitcast.18, bf16[256,8,4,128]{3,2,1,0:T(4,128)(2,1)} %bitcast.111), kind=kOutput, calls=%fused_computation.27 | convolution fusion | flops 2147483648 | bytes 8388608 | tf_op jit(solution)/shard_map/dot_general | solution.py:140
  325.0 5.9 %fusion.29 = f32[512,1024]{1,0:T(8,128)} fusion(f32[512,1024]{1,0:T(8,128)S(1)} %fusion.12, bf16[2048,1024]{1,0:T(8,128)(2,1)} %bitcast.18, bf16[256,8,4,128]{3,2,1,0:T(4,128)(2,1)S(1)} %bitcast.109), kind=kOutput, calls=%fused_computation.43 | convolution fusion | flops 2148007936 | bytes 10485760 | tf_op jit(solution)/shard_map/dot_general | solution.py:138
  331.2 40.9 %reduce-scatter.5.cloned.1.call-done = f32[128,1024]{1,0:T(8,128)} async-done(((f32[512,1024]{1,0:T(8,128)}), f32[128,1024]{1,0:T(8,128)}) %reduce-scatter.5.cloned.1.call-update) | async-done | bytes 524304 | tf_op jit(solution)/shard_map/reduce_scatter | solution.py:141
  374.8 4.7 %fusion.74 = (bf16[1024,2,512]{2,1,0:T(2,128)(2,1)S(1)}, bf16[1024,2,512]{2,1,0:T(2,128)(2,1)S(1)}) fusion(bf16[2048,2,512]{2,1,0:T(2,128)(2,1)} %param.20), kind=kLoop, calls=%fused_computation.107 | loop fusion | bytes 8388608 | tf_op jit(solution)/shard_map/slice | solution.py:149
  383.3 18.3 %all-gather.5.cloned.1.call-done = bf16[512,1024]{1,0:T(8,128)(2,1)} async-done(((bf16[128,1024]{1,0:T(8,128)(2,1)}), bf16[512,1024]{1,0:T(8,128)(2,1)}) %all-gather.5.cloned.1.call-update) | async-done | bytes 1048592 | tf_op jit(solution)/shard_map/all_gather | solution.py:148
  406.1 24.4 %all-gather.7.cloned.1.call-done = bf16[512,1024]{1,0:T(8,128)(2,1)} async-done(((bf16[128,1024]{1,0:T(8,128)(2,1)}), bf16[512,1024]{1,0:T(8,128)(2,1)}) %all-gather.7.cloned.1.call-update) | async-done | bytes 1048592 | tf_op jit(solution)/shard_map/all_gather | solution.py:148
  438.5 10.8 %psum.7 = f32[1,21]{1,0:T(1,128)} all-reduce(f32[1,21]{1,0:T(1,128)S(1)} %bitcast.125), channel_id=1, replica_groups=mesh['dp'=4,'expert'=2,'tensor'=4] {'tensor'}, use_global_device_ids=true, to_apply=%region_8.9 | all-reduce | flops 21 | bytes 168 | tf_op jit(solution)/shard_map/psum | solution.py:190
  (101 shorter events, 66.3 us)
Async XLA Ops:
  7.2 60.2 %all-gather.9.cloned.1.call-start = ((), (), s32[]{:S(2)}) async-start(), calls=%async_computation.10 | async-start | bytes 2949120 | tf_op jit(solution)/shard_map/all_gather | solution.py:70
  14.1 59.1 %copy-start.12 = (pred[4,4]{1,0:T(4,128)(4,1)}, pred[4,4]{1,0:T(4,128)(4,1)S(1)}, u32[]{:S(2)}) copy-start(pred[4,4]{1,0:T(4,128)(4,1)S(1)} %iota_compare_fusion.13) | copy-start | bytes 52
  85.3 53.7 %all-to-all-start = ((bf16[8,256,1024]{2,1,0:T(8,128)(2,1)}), bf16[8,256,1024]{2,1,0:T(8,128)(2,1)}, u32[]{:S(2)}, u32[]{:S(2)}) async-start(bf16[8,256,1024]{2,1,0:T(8,128)(2,1)} %bitcast.107), calls=%async_computation | async-start | bytes 8388608 | tf_op jit(solution)/shard_map/all_to_all | solution.py:112
  139.0 54.2 %all-to-all-start.1 = ((bf16[8,256,1024]{2,1,0:T(8,128)(2,1)}), bf16[8,256,1024]{2,1,0:T(8,128)(2,1)}, u32[]{:S(2)}, u32[]{:S(2)}) async-start(bf16[8,256,1024]{2,1,0:T(8,128)(2,1)} %bitcast.105), calls=%async_computation.1 | async-start | bytes 8388608 | tf_op jit(solution)/shard_map/all_to_all | solution.py:112
  144.0 8.8 %copy-start.9 = (f32[1,16,12]{1,0,2:T(1,128)S(1)}, f32[1,16,12]{1,0,2:T(1,128)}, u32[]{:S(2)}) copy-start(f32[1,16,12]{1,0,2:T(1,128)} %param.17) | copy-start | bytes 2308
  144.0 8.9 %copy-start.10 = (f32[1,6,16]{2,0,1:T(1,128)S(1)}, f32[1,6,16]{2,0,1:T(1,128)}, u32[]{:S(2)}) copy-start(f32[1,6,16]{2,0,1:T(1,128)} %param.19) | copy-start | bytes 1156
  157.5 8.4 %copy-start = (bf16[2048,1536]{0,1:T(8,128)(2,1)}, bf16[2048,1536]{0,1:T(8,128)(2,1)S(1)}, u32[]{:S(2)}) copy-start(bf16[2048,1536]{0,1:T(8,128)(2,1)S(1)} %fusion) | copy-start | bytes 18874372
  157.6 4.1 copy-start.2
  204.9 2.1 copy-start.3
  207.0 5.3 %copy-start.5 = (bf16[2048,768]{1,0:T(8,128)(2,1)}, bf16[2048,768]{1,0:T(8,128)(2,1)S(1)}, u32[]{:S(2)}) copy-start(bf16[2048,768]{1,0:T(8,128)(2,1)S(1)} %fusion.3) | copy-start | bytes 9437188
  212.3 11.1 %copy-start.13 = (pred[4,4]{1,0:T(4,128)(4,1)S(1)}, pred[4,4]{1,0:T(4,128)(4,1)}, u32[]{:S(2)}) copy-start(pred[4,4]{1,0:T(4,128)(4,1)} %copy-done.12) | copy-start | bytes 52
  212.3 53.8 %all-to-all-start.2 = ((bf16[8,256,1024]{2,1,0:T(8,128)(2,1)}), bf16[8,256,1024]{2,1,0:T(8,128)(2,1)}, u32[]{:S(2)}, u32[]{:S(2)}) async-start(bf16[8,256,1024]{2,1,0:T(8,128)(2,1)} %bitcast.104), calls=%async_computation.2 | async-start | bytes 8388608 | tf_op jit(solution)/shard_map/all_to_all | solution.py:112
  217.3 9.8 %copy-start.4 = (bf16[768,2048]{1,0:T(8,128)(2,1)S(1)}, bf16[768,2048]{1,0:T(8,128)(2,1)}, u32[]{:S(2)}) copy-start(bf16[768,2048]{1,0:T(8,128)(2,1)} %fusion.2) | copy-start | bytes 9437188
  217.4 9.8 %copy-start.6 = (bf16[2048,768]{1,0:T(8,128)(2,1)S(1)}, bf16[2048,768]{1,0:T(8,128)(2,1)}, u32[]{:S(2)}) copy-start(bf16[2048,768]{1,0:T(8,128)(2,1)} %copy-done.5) | copy-start | bytes 9437188
  266.1 53.7 %all-to-all-start.3 = ((bf16[8,256,1024]{2,1,0:T(8,128)(2,1)}), bf16[8,256,1024]{2,1,0:T(8,128)(2,1)}, u32[]{:S(2)}, u32[]{:S(2)}) async-start(bf16[8,256,1024]{2,1,0:T(8,128)(2,1)} %bitcast.106), calls=%async_computation.4 | async-start | bytes 8388608 | tf_op jit(solution)/shard_map/all_to_all | solution.py:112
  270.7 60.5 %reduce-scatter.3.cloned.1.call-start = ((), (), s32[]{:S(2)}) async-start(), calls=%async_computation.6 | async-start | bytes 2621440 | tf_op jit(solution)/shard_map/reduce_scatter | solution.py:141
  282.0 90.0 %reduce-scatter.5.cloned.1.call-start = ((), (), s32[]{:S(2)}) async-start(), calls=%async_computation.7 | async-start | bytes 2621440 | tf_op jit(solution)/shard_map/reduce_scatter | solution.py:141
  325.0 6.0 %copy-start.1 = (bf16[128,2048]{1,0:T(8,128)(2,1)S(1)}, bf16[128,2048]{1,0:T(8,128)(2,1)}, u32[]{:S(2)}) copy-start(bf16[128,2048]{1,0:T(8,128)(2,1)} %param.12) | copy-start | bytes 1572868
  331.0 70.7 %all-gather.5.cloned.1.call-start = ((), (), s32[]{:S(2)}) async-start(), calls=%async_computation.8 | async-start | bytes 1310720 | tf_op jit(solution)/shard_map/all_gather | solution.py:148
  374.2 56.3 %all-gather.7.cloned.1.call-start = ((), (), s32[]{:S(2)}) async-start(), calls=%async_computation.9 | async-start | bytes 1310720 | tf_op jit(solution)/shard_map/all_gather | solution.py:148
  381.4 0.7 copy-start.11
  381.4 1.0 copy-start.7
  381.4 1.1 copy-start.8
  433.7 1.0 copy-start.15
  (1 other events, 0.7 us)
Sparse Core Ops, SparseCore 0:
  14.2 53.1 all-gather.8
  282.1 43.0 reduce-scatter.2
  331.1 40.8 reduce-scatter.4
  374.3 27.2 all-gather.4
  403.0 27.4 all-gather.6

commit v3 on v2

--- a/solution.py
+++ b/solution.py
@@ -57,18 +57,20 @@
         ],
         axis=1,
     )
-    extra = rows * 4 * top // width
+    half = width // 2
+    extra = rows * 4 * top // half
     padded = rows + 16
     packed = jnp.concatenate(
         [
-            normed,
-            routing.reshape(extra, width),
-            jnp.zeros((padded - rows - extra, width), jnp.bfloat16),
+            normed[:, :half],
+            routing.reshape(extra, half),
+            jnp.zeros((padded - rows - extra, half), jnp.bfloat16),
         ],
         axis=0,
     )
-    line = lax.all_gather(packed, "tensor", axis=0, tiled=False)
-    line_routing = line[:, rows : rows + extra, :].reshape(lines, rows, 4 * top)
+    line_a = lax.all_gather(packed, "tensor", axis=0, tiled=False)
+    line_b = lax.all_gather(normed[:, half:], "tensor", axis=0, tiled=False)
+    line_routing = line_a[:, rows : rows + extra, :].reshape(lines, rows, 4 * top)
     ids_l = line_routing[:, :, :top].astype(jnp.int32)
     slot_l = line_routing[:, :, top : 2 * top].astype(jnp.int32)
     gate_hi = line_routing[:, :, 2 * top : 3 * top].astype(jnp.float32)
@@ -84,12 +86,14 @@
         jnp.arange(lines, dtype=jnp.int32)[:, None] == jnp.arange(lines, dtype=jnp.int32)[None, :]
     )
     select = select.reshape(lines, plane, most, rows).transpose(1, 0, 2, 3)
-    select = jnp.pad(select, ((0, 0), (0, 0), (0, 0), (0, padded - rows)))
     select_full = (
         (select[:, :, :, None, :] & same[None, :, None, :, None])
-        .reshape(plane * cap, lines * padded)
+        .reshape(plane * cap, lines * rows)
         .astype(jnp.bfloat16)
     )
+    select_pad = jnp.pad(
+        select_full.reshape(plane * cap, lines, rows), ((0, 0), (0, 0), (0, padded - rows))
+    ).reshape(plane * cap, lines * padded)
 
     def spread(weight):
         weight = weight.reshape(lines, plane, most, rows).transpose(1, 0, 2, 3)
@@ -101,8 +105,8 @@
 
     weight_hi = spread(weight_hi)
     weight_lo = spread(weight_lo)
-    line_flat = line.reshape(lines * padded, width)
-    half = width // 2
+    line_parts = [line_a.reshape(lines * padded, half), line_b.reshape(lines * rows, half)]
+    select_parts = [select_pad, select_full]
     gate_up = dequant(w_in[0], scale_in[0])
     down_proj = dequant(w_out[0], scale_out[0])
     hidden_width = down_proj.shape[0]
@@ -117,7 +121,7 @@
     blocks = [
         send(
             jnp.dot(
-                select_full, line_flat[:, h * half : (h + 1) * half], preferred_element_type=jnp.float32
+                select_parts[h], line_parts[h], preferred_element_type=jnp.float32
             ).astype(jnp.bfloat16)
         )
         for h in range(2)

time: 465 us -> 447 us (0.961)
  waiting for transfers between devices: 267 us -> 245 us
  other arithmetic: 35.7 us -> 44.9 us
    all_to_all x4, waiting for transfers between devices: 130 us -> 100 us  [send(): lax.all_to_all(part.reshape(plane, cap, part.shape[1]), group, split_axis...]
    convert_element_type x1, other arithmetic: 2.08 us -> 11.4 us  [shards(): (jax.nn.silu(mixed_in[:, :hidden_width]) * mixed_in[:, hidden_width:]).as...]
    all_gather x1 -> x2, waiting for transfers between devices: 53.3 us -> 60.7 us  [the longest x1 33.1 us: shards(): line_a = lax.all_gather(packed, 'tensor', axis=0, tiled=False)]
    unnamed x44 -> x41, local copies, waits for them, and re-layouts: 15.2 us -> 15.2 us
  transfers between devices with their start and end apart: 9 -> 10, of which waited for: 8 -> 9; matrix products, arithmetic and copies ran while one was open for 19% -> 20% of each run, Pallas kernels for 0% -> 0%
where the time goes in v3:
time: 447 us; the launch traced here: 440 us
  waiting for transfers between devices  245 us (55%)
  matrix products  79.4 us (18%)
  other arithmetic  44.9 us (10%)
  local copies, waits for them, and re-layouts  25 us (6%)
  starting transfers between devices  19.2 us (4%)
  between operations  15 us (3%)
  blocking collectives  10.8 us (2%)
    all_to_all x4, waiting for transfers between devices, send(): lax.all_to_all(part.reshape(plane, cap, part.shape[1]), group, split_axis...  100 us
    all_gather x2, waiting for transfers between devices, shards(): lax.all_gather(mixed_parts[h], 'tensor', axis=0, tiled=True)  42.7 us
    reduce_scatter x2, waiting for transfers between devices, shards(): lax.psum_scatter(partial, 'tensor', scatter_dimension=0, tiled=True)  41.2 us
    all_gather x1, waiting for transfers between devices, shards(): line_a = lax.all_gather(packed, 'tensor', axis=0, tiled=False)  33.1 us
    all_gather x1, waiting for transfers between devices, shards(): line_b = lax.all_gather(normed[:, half:], 'tensor', axis=0, tiled=False)  27.6 us
    all_to_all x4, starting transfers between devices, send(): lax.all_to_all(part.reshape(plane, cap, part.shape[1]), group, split_axis...  18.2 us
    unnamed x41, local copies, waits for them, and re-layouts  15.2 us
    dot_general x2, matrix products, shards(): lax.dot_general(weight_hi, back, contract, preferred_element_type=jnp.flo...  11.8 us
  transfers between devices with their start and end apart: 10, of which 9 were waited for; matrix products, arithmetic and copies ran while one was open for 20% of the time, Pallas kernels for 0%

profile of v3, /device:TPU:0, one launch (start us, length us, event | category | flops | bytes accessed | tf_op | source)
XLA Modules:
  0.0 439.6 jit_solution(11637669467178076485)
XLA Ops:
  14.8 33.1 %all-gather.11.cloned.1.call-done = bf16[576,1024]{1,0:T(8,128)(2,1)} async-done(((bf16[144,1024]{1,0:T(8,128)(2,1)}), bf16[576,1024]{1,0:T(8,128)(2,1)}) %all-gather.11.cloned.1.call-update) | async-done | bytes 1179664 | tf_op jit(solution)/shard_map/all_gather | solution.py:71
  54.5 5.0 %bitcast_convert_fusion = bf16[2048,1024]{1,0:T(8,128)(2,1)} fusion(bf16[4,144,1024]{2,1,0:T(8,128)(2,1)S(1)} %bitcast.140, pred[2048,4,128]{0,2,1:T(8,128)(4,1)S(1)} %broadcast_and_fusion.1), kind=kOutput, calls=%fused_computation.3 | convolution fusion | flops 2418016256 | bytes 6422528 | tf_op jit(solution)/shard_map/dot_general | solution.py:123
  66.4 27.6 %all-gather.13.cloned.1.call-done = bf16[512,1024]{1,0:T(8,128)(2,1)} async-done(((bf16[128,1024]{1,0:T(8,128)(2,1)}), bf16[512,1024]{1,0:T(8,128)(2,1)}) %all-gather.13.cloned.1.call-update) | async-done | bytes 1048592 | tf_op jit(solution)/shard_map/all_gather | solution.py:72
  94.0 5.6 %fusion.14 = bf16[2048,1024]{1,0:T(8,128)(2,1)} fusion(bf16[512,1024]{1,0:T(8,128)(2,1)} %all-gather.13.cloned.1.call-done, pred[256,8,4,128]{3,2,1,0:T(4,128)(4,1)S(1)} %bitcast.131), kind=kOutput, calls=%fused_computation.23 | convolution fusion | flops 2149580800 | bytes 6291456 | tf_op jit(solution)/shard_map/dot_general | solution.py:123
  99.6 13.6 %all-to-all-done = bf16[8,256,1024]{2,1,0:T(8,128)(2,1)} async-done(((bf16[8,256,1024]{2,1,0:T(8,128)(2,1)}), bf16[8,256,1024]{2,1,0:T(8,128)(2,1)}, u32[]{:S(2)}, u32[]{:S(2)}) %all-to-all-start) | async-done | bytes 4194336 | tf_op jit(solution)/shard_map/all_to_all | solution.py:116
  117.8 8.8 %copy.68 = bf16[1,2048,1536]{1,2,0:T(8,128)(2,1)} copy(bf16[1,2048,1536]{2,1,0:T(8,128)(2,1)} %param.16) | data formatting | bytes 12582912 | tf_op args[4]
  139.2 11.6 %fusion.18 = f32[2048,1536]{1,0:T(8,128)} fusion(bf16[2048,1024]{1,0:T(8,128)(2,1)} %bitcast.8, bf16[2048,1536]{0,1:T(8,128)(2,1)S(1)} %fusion), kind=kOutput, calls=%fused_computation.27 | convolution fusion | flops 6442450944 | bytes 19922944 | tf_op jit(solution)/shard_map/dot_general | solution.py:129
  150.8 16.1 %all-to-all-done.1 = bf16[8,256,1024]{2,1,0:T(8,128)(2,1)} async-done(((bf16[8,256,1024]{2,1,0:T(8,128)(2,1)}), bf16[8,256,1024]{2,1,0:T(8,128)(2,1)}, u32[]{:S(2)}, u32[]{:S(2)}) %all-to-all-start.1) | async-done | bytes 4194336 | tf_op jit(solution)/shard_map/all_to_all | solution.py:116
  166.9 11.7 %convolution_add_fusion = f32[2048,1536]{1,0:T(8,128)S(1)} fusion(f32[2048,1536]{1,0:T(8,128)} %fusion.18, bf16[2048,1024]{1,0:T(8,128)(2,1)} %bitcast.13, bf16[2048,1536]{0,1:T(8,128)(2,1)} %copy-done), kind=kOutput, calls=%fused_computation.2 | convolution fusion | flops 6445596672 | bytes 32505856 | tf_op jit(solution)/shard_map/dot_general | solution.py:129
  178.6 11.4 %fusion.3 = bf16[2048,768]{1,0:T(8,128)(2,1)S(1)} fusion(f32[2048,1536]{1,0:T(8,128)S(1)} %convolution_add_fusion), kind=kLoop, calls=%fused_computation.11 | loop fusion | flops 9437184 | bytes 15728640 | tf_op jit(solution)/shard_map/convert_element_type | solution.py:132
  190.1 5.2 %convolution_convert_fusion.1 = bf16[2048,1024]{1,0:T(8,128)(2,1)} fusion(bf16[2048,768]{1,0:T(8,128)(2,1)S(1)} %fusion.3, bf16[768,2048]{1,0:T(8,128)(2,1)S(1)} %fusion.2), kind=kOutput, calls=%fused_computation.25 | convolution fusion | flops 3223322624 | bytes 8912896 | tf_op jit(solution)/shard_map/dot_general | solution.py:138
  200.2 6.0 %select_reduce_fusion.1 = (bf16[4,512,128]{2,1,0:T(8,128)(2,1)S(1)}, bf16[4,512,128]{2,1,0:T(8,128)(2,1)S(1)}) fusion(f32[4,128,8]{1,2,0:T(8,128)S(1)} %convert_element_type.141, s32[4,128,8]{1,2,0:T(8,128)S(1)} %copy.63, f32[4,128,8]{1,2,0:T(8,128)S(1)} %convert_element_type.154), kind=kLoop, calls=%fused_computation.5 | loop fusion | flops 9961472 | bytes 1097728 | tf_op jit(solution)/shard_map/reduce_sum | solution.py:83
  206.2 5.1 %select_convert_fusion.1 = (bf16[8,4,64,4,128]{4,3,2,1,0:T(4,128)(2,1)}, bf16[8,4,64,4,128]{4,3,2,1,0:T(4,128)(2,1)}) fusion(pred[4,4]{1,0:T(4,128)(4,1)} %copy-done.11, bf16[8,4,64,128]{3,2,0,1:T(8,128)(2,1)S(1)} %bitcast.129, bf16[8,4,64,128]{3,2,0,1:T(8,128)(2,1)S(1)} %bitcast.128), kind=kLoop, calls=%fused_computation.17 | loop fusion | flops 2097152 | bytes 5242896 | tf_op jit(solution)/shard_map/convert_element_type | solution.py:103
  211.2 5.0 %convolution_convert_fusion = bf16[2048,1024]{1,0:T(8,128)(2,1)} fusion(bf16[2048,768]{1,0:T(8,128)(2,1)S(1)} %copy-done.4, bf16[768,2048]{1,0:T(8,128)(2,1)S(1)} %fusion.2), kind=kOutput, calls=%fused_computation.24 | convolution fusion | flops 3223322624 | bytes 8912896 | tf_op jit(solution)/shard_map/dot_general | solution.py:138
  216.2 32.7 %all-to-all-done.2 = bf16[8,256,1024]{2,1,0:T(8,128)(2,1)} async-done(((bf16[8,256,1024]{2,1,0:T(8,128)(2,1)}), bf16[8,256,1024]{2,1,0:T(8,128)(2,1)}, u32[]{:S(2)}, u32[]{:S(2)}) %all-to-all-start.2) | async-done | bytes 4194336 | tf_op jit(solution)/shard_map/all_to_all | solution.py:116
  253.8 5.3 %fusion.24 = f32[512,1024]{1,0:T(8,128)S(1)} fusion(bf16[2048,1024]{1,0:T(8,128)(2,1)} %bitcast.17, bf16[256,8,4,128]{3,2,1,0:T(4,128)(2,1)} %bitcast.124), kind=kOutput, calls=%fused_computation.33 | convolution fusion | flops 2147483648 | bytes 8388608 | tf_op jit(solution)/shard_map/dot_general | solution.py:144
  259.1 5.9 %fusion.36 = f32[512,1024]{1,0:T(8,128)} fusion(f32[512,1024]{1,0:T(8,128)S(1)} %fusion.24, bf16[2048,1024]{1,0:T(8,128)(2,1)} %bitcast.17, bf16[256,8,4,128]{3,2,1,0:T(4,128)(2,1)S(1)} %bitcast.122), kind=kOutput, calls=%fused_computation.48 | convolution fusion | flops 2148007936 | bytes 10485760 | tf_op jit(solution)/shard_map/dot_general | solution.py:142
  265.0 37.6 %all-to-all-done.3 = bf16[8,256,1024]{2,1,0:T(8,128)(2,1)} async-done(((bf16[8,256,1024]{2,1,0:T(8,128)(2,1)}), bf16[8,256,1024]{2,1,0:T(8,128)(2,1)}, u32[]{:S(2)}, u32[]{:S(2)}) %all-to-all-start.3) | async-done | bytes 4194336 | tf_op jit(solution)/shard_map/all_to_all | solution.py:116
  302.6 5.2 %fusion.22 = f32[512,1024]{1,0:T(8,128)S(1)} fusion(bf16[2048,1024]{1,0:T(8,128)(2,1)} %bitcast.21, bf16[256,8,4,128]{3,2,1,0:T(4,128)(2,1)} %bitcast.125), kind=kOutput, calls=%fused_computation.31 | convolution fusion | flops 2147483648 | bytes 8388608 | tf_op jit(solution)/shard_map/dot_general | solution.py:144
  307.8 6.0 %fusion.39 = f32[512,1024]{1,0:T(8,128)} fusion(f32[512,1024]{1,0:T(8,128)S(1)} %fusion.22, bf16[2048,1024]{1,0:T(8,128)(2,1)} %bitcast.21, bf16[256,8,4,128]{3,2,1,0:T(4,128)(2,1)S(1)} %bitcast.123), kind=kOutput, calls=%fused_computation.49 | convolution fusion | flops 2148007936 | bytes 10485760 | tf_op jit(solution)/shard_map/dot_general | solution.py:142
  314.0 41.1 %reduce-scatter.5.cloned.1.call-done = f32[128,1024]{1,0:T(8,128)} async-done(((f32[512,1024]{1,0:T(8,128)}), f32[128,1024]{1,0:T(8,128)}) %reduce-scatter.5.cloned.1.call-update) | async-done | bytes 524304 | tf_op jit(solution)/shard_map/reduce_scatter | solution.py:145
  366.4 18.3 %all-gather.7.cloned.1.call-done = bf16[512,1024]{1,0:T(8,128)(2,1)} async-done(((bf16[128,1024]{1,0:T(8,128)(2,1)}), bf16[512,1024]{1,0:T(8,128)(2,1)}) %all-gather.7.cloned.1.call-update) | async-done | bytes 1048592 | tf_op jit(solution)/shard_map/all_gather | solution.py:152
  389.2 24.4 %all-gather.9.cloned.1.call-done = bf16[512,1024]{1,0:T(8,128)(2,1)} async-done(((bf16[128,1024]{1,0:T(8,128)(2,1)}), bf16[512,1024]{1,0:T(8,128)(2,1)}) %all-gather.9.cloned.1.call-update) | async-done | bytes 1048592 | tf_op jit(solution)/shard_map/all_gather | solution.py:152
  421.6 10.8 %psum.7 = f32[1,21]{1,0:T(1,128)} all-reduce(f32[1,21]{1,0:T(1,128)S(1)} %bitcast.141), channel_id=1, replica_groups=mesh['dp'=4,'expert'=2,'tensor'=4] {'tensor'}, use_global_device_ids=true, to_apply=%region_8.9 | all-reduce | flops 21 | bytes 168 | tf_op jit(solution)/shard_map/psum | solution.py:194
  (106 shorter events, 71.6 us)
Async XLA Ops:
  7.2 40.8 %all-gather.11.cloned.1.call-start = ((), (), s32[]{:S(2)}) async-start(), calls=%async_computation.10 | async-start | bytes 1474560 | tf_op jit(solution)/shard_map/all_gather | solution.py:71
  47.9 6.6 %copy-start.12 = (bf16[576,1024]{1,0:T(8,128)(2,1)S(1)}, bf16[576,1024]{1,0:T(8,128)(2,1)}, u32[]{:S(2)}) copy-start(bf16[576,1024]{1,0:T(8,128)(2,1)} %all-gather.11.cloned.1.call-done) | copy-start | bytes 3538948
  59.5 53.7 %all-to-all-start = ((bf16[8,256,1024]{2,1,0:T(8,128)(2,1)}), bf16[8,256,1024]{2,1,0:T(8,128)(2,1)}, u32[]{:S(2)}, u32[]{:S(2)}) async-start(bf16[8,256,1024]{2,1,0:T(8,128)(2,1)} %bitcast.118), calls=%async_computation | async-start | bytes 8388608 | tf_op jit(solution)/shard_map/all_to_all | solution.py:116
  64.1 29.9 %all-gather.13.cloned.1.call-start = ((), (), s32[]{:S(2)}) async-start(), calls=%async_computation.11 | async-start | bytes 1310720 | tf_op jit(solution)/shard_map/all_gather | solution.py:72
  65.0 34.7 %copy-start.11 = (pred[4,4]{1,0:T(4,128)(4,1)}, pred[4,4]{1,0:T(4,128)(4,1)S(1)}, u32[]{:S(2)}) copy-start(pred[4,4]{1,0:T(4,128)(4,1)S(1)} %copy.59) | copy-start | bytes 52
  113.2 53.7 %all-to-all-start.1 = ((bf16[8,256,1024]{2,1,0:T(8,128)(2,1)}), bf16[8,256,1024]{2,1,0:T(8,128)(2,1)}, u32[]{:S(2)}, u32[]{:S(2)}) async-start(bf16[8,256,1024]{2,1,0:T(8,128)(2,1)} %bitcast.117), calls=%async_computation.1 | async-start | bytes 8388608 | tf_op jit(solution)/shard_map/all_to_all | solution.py:116
  117.8 8.8 %copy-start.8 = (f32[1,16,12]{1,0,2:T(1,128)S(1)}, f32[1,16,12]{1,0,2:T(1,128)}, u32[]{:S(2)}) copy-start(f32[1,16,12]{1,0,2:T(1,128)} %param.17) | copy-start | bytes 2308
  117.8 8.9 %copy-start.9 = (f32[1,6,16]{2,0,1:T(1,128)S(1)}, f32[1,6,16]{2,0,1:T(1,128)}, u32[]{:S(2)}) copy-start(f32[1,6,16]{2,0,1:T(1,128)} %param.19) | copy-start | bytes 1156
  131.3 7.9 %copy-start = (bf16[2048,1536]{0,1:T(8,128)(2,1)}, bf16[2048,1536]{0,1:T(8,128)(2,1)S(1)}, u32[]{:S(2)}) copy-start(bf16[2048,1536]{0,1:T(8,128)(2,1)S(1)} %fusion) | copy-start | bytes 18874372
  131.4 4.1 copy-start.2
  190.1 5.2 %copy-start.3 = (bf16[2048,768]{1,0:T(8,128)(2,1)}, bf16[2048,768]{1,0:T(8,128)(2,1)S(1)}, u32[]{:S(2)}) copy-start(bf16[2048,768]{1,0:T(8,128)(2,1)S(1)} %fusion.3) | copy-start | bytes 9437188
  195.2 53.7 %all-to-all-start.2 = ((bf16[8,256,1024]{2,1,0:T(8,128)(2,1)}), bf16[8,256,1024]{2,1,0:T(8,128)(2,1)}, u32[]{:S(2)}, u32[]{:S(2)}) async-start(bf16[8,256,1024]{2,1,0:T(8,128)(2,1)} %bitcast.116), calls=%async_computation.2 | async-start | bytes 8388608 | tf_op jit(solution)/shard_map/all_to_all | solution.py:116
  200.2 11.1 %copy-start.4 = (bf16[2048,768]{1,0:T(8,128)(2,1)S(1)}, bf16[2048,768]{1,0:T(8,128)(2,1)}, u32[]{:S(2)}) copy-start(bf16[2048,768]{1,0:T(8,128)(2,1)} %copy-done.3) | copy-start | bytes 9437188
  248.9 53.7 %all-to-all-start.3 = ((bf16[8,256,1024]{2,1,0:T(8,128)(2,1)}), bf16[8,256,1024]{2,1,0:T(8,128)(2,1)}, u32[]{:S(2)}, u32[]{:S(2)}) async-start(bf16[8,256,1024]{2,1,0:T(8,128)(2,1)} %bitcast.119), calls=%async_computation.4 | async-start | bytes 8388608 | tf_op jit(solution)/shard_map/all_to_all | solution.py:116
  253.5 60.5 %reduce-scatter.3.cloned.1.call-start = ((), (), s32[]{:S(2)}) async-start(), calls=%async_computation.6 | async-start | bytes 2621440 | tf_op jit(solution)/shard_map/reduce_scatter | solution.py:145
  253.8 5.3 %copy-start.7 = (bf16[8,4,64,4,128]{4,3,2,1,0:T(4,128)(2,1)S(1)}, bf16[8,4,64,4,128]{4,3,2,1,0:T(4,128)(2,1)}, u32[]{:S(2)}) copy-start(bf16[8,4,64,4,128]{4,3,2,1,0:T(4,128)(2,1)} %get-tuple-element.16) | copy-start | bytes 6291460
  265.0 90.2 %reduce-scatter.5.cloned.1.call-start = ((), (), s32[]{:S(2)}) async-start(), calls=%async_computation.7 | async-start | bytes 2621440 | tf_op jit(solution)/shard_map/reduce_scatter | solution.py:145
  307.8 6.1 %copy-start.1 = (bf16[128,2048]{1,0:T(8,128)(2,1)S(1)}, bf16[128,2048]{1,0:T(8,128)(2,1)}, u32[]{:S(2)}) copy-start(bf16[128,2048]{1,0:T(8,128)(2,1)} %param.12) | copy-start | bytes 1572868
  313.8 70.9 %all-gather.7.cloned.1.call-start = ((), (), s32[]{:S(2)}) async-start(), calls=%async_computation.8 | async-start | bytes 1310720 | tf_op jit(solution)/shard_map/all_gather | solution.py:152
  357.3 56.3 %all-gather.9.cloned.1.call-start = ((), (), s32[]{:S(2)}) async-start(), calls=%async_computation.9 | async-start | bytes 1310720 | tf_op jit(solution)/shard_map/all_gather | solution.py:152
  364.5 0.7 copy-start.10
  364.5 1.0 copy-start.5
  364.5 1.1 copy-start.6
  416.8 1.0 copy-start.14
  (1 other events, 0.7 us)
Sparse Core Ops, SparseCore 0:
  14.8 33.1 all-gather.10
  66.5 27.4 all-gather.12
  265.1 43.3 reduce-scatter.2
  313.9 41.1 reduce-scatter.4
  357.4 27.2 all-gather.6
  386.2 27.4 all-gather.8

commit v4 on v3

--- a/solution.py
+++ b/solution.py
@@ -82,31 +82,12 @@
     select = jnp.any(match, axis=3)
     weight_hi = jnp.sum(jnp.where(match, gate_hi[:, None, :, :], 0.0), axis=3)
     weight_lo = jnp.sum(jnp.where(match, gate_lo[:, None, :, :], 0.0), axis=3)
-    same = (
-        jnp.arange(lines, dtype=jnp.int32)[:, None] == jnp.arange(lines, dtype=jnp.int32)[None, :]
-    )
-    select = select.reshape(lines, plane, most, rows).transpose(1, 0, 2, 3)
-    select_full = (
-        (select[:, :, :, None, :] & same[None, :, None, :, None])
-        .reshape(plane * cap, lines * rows)
-        .astype(jnp.bfloat16)
-    )
-    select_pad = jnp.pad(
-        select_full.reshape(plane * cap, lines, rows), ((0, 0), (0, 0), (0, padded - rows))
-    ).reshape(plane * cap, lines * padded)
-
-    def spread(weight):
-        weight = weight.reshape(lines, plane, most, rows).transpose(1, 0, 2, 3)
-        return (
-            jnp.where(same[None, :, None, :, None], weight[:, :, :, None, :], 0.0)
-            .reshape(plane * cap, lines * rows)
-            .astype(jnp.bfloat16)
-        )
-
-    weight_hi = spread(weight_hi)
-    weight_lo = spread(weight_lo)
-    line_parts = [line_a.reshape(lines * padded, half), line_b.reshape(lines * rows, half)]
-    select_parts = [select_pad, select_full]
+    select = select.astype(jnp.bfloat16).reshape(lines, plane, most, rows)
+    select_pad = jnp.pad(select, ((0, 0), (0, 0), (0, 0), (0, padded - rows)))
+    weight_hi = weight_hi.astype(jnp.bfloat16).reshape(lines, plane, most, rows)
+    weight_lo = weight_lo.astype(jnp.bfloat16).reshape(lines, plane, most, rows)
+    line_parts = [line_a, line_b]
+    select_parts = [select_pad, select]
     gate_up = dequant(w_in[0], scale_in[0])
     down_proj = dequant(w_out[0], scale_out[0])
     hidden_width = down_proj.shape[0]
@@ -120,9 +101,11 @@
 
     blocks = [
         send(
-            jnp.dot(
-                select_parts[h], line_parts[h], preferred_element_type=jnp.float32
-            ).astype(jnp.bfloat16)
+            jnp.einsum(
+                "bpsr,brd->pbsd", select_parts[h], line_parts[h], preferred_element_type=jnp.float32
+            )
+            .astype(jnp.bfloat16)
+            .reshape(plane * cap, half)
         )
         for h in range(2)
     ]
@@ -132,28 +115,27 @@
     hidden = (jax.nn.silu(mixed_in[:, :hidden_width]) * mixed_in[:, hidden_width:]).astype(
         jnp.bfloat16
     )
-    contract = (((0,), (0,)), ((), ()))
     mixed_parts = []
     for h in range(2):
         output = jnp.dot(
             hidden, down_proj[:, h * half : (h + 1) * half], preferred_element_type=jnp.float32
         ).astype(jnp.bfloat16)
         back = send(output)
-        partial = lax.dot_general(
-            weight_hi, back, contract, preferred_element_type=jnp.float32
-        ) + lax.dot_general(weight_lo, back, contract, preferred_element_type=jnp.float32)
-        combined = lax.psum_scatter(partial, "tensor", scatter_dimension=0, tiled=True)
-        mixed_parts.append((x_float[:, h * half : (h + 1) * half] + combined).astype(jnp.bfloat16))
-    mixed = jnp.concatenate(mixed_parts, axis=1)
+        back = back.reshape(plane, lines, most, half)
+        partial = jnp.einsum(
+            "bpsr,pbsd->brd", weight_hi, back, preferred_element_type=jnp.float32
+        ) + jnp.einsum("bpsr,pbsd->brd", weight_lo, back, preferred_element_type=jnp.float32)
+        combined = lax.psum_scatter(
+            partial.reshape(lines * rows, half), "tensor", scatter_dimension=0, tiled=True
+        )
+        mixed_parts.append(x_float[:, h * half : (h + 1) * half] + combined)
+    mixed = jnp.concatenate(mixed_parts, axis=1).astype(jnp.bfloat16)
 
     local_sync = w_sync.reshape(width, -1)
-    proj = sum(
-        jnp.dot(
-            lax.all_gather(mixed_parts[h], "tensor", axis=0, tiled=True),
-            local_sync[h * half : (h + 1) * half],
-            preferred_element_type=jnp.float32,
-        )
-        for h in range(2)
+    proj = jnp.dot(
+        lax.all_gather(mixed, "tensor", axis=0, tiled=True),
+        local_sync,
+        preferred_element_type=jnp.float32,
     ).astype(jnp.bfloat16)
     half = proj.shape[1] // 2
     heads_here = head_weight.shape[0]

time: 447 us -> 424 us (0.949)
  other arithmetic: 44.9 us -> 27.8 us
  matrix products: 79.4 us -> 67.4 us
  waiting for transfers between devices: 245 us -> 250 us
    dot_general x8 -> x7, matrix products: 40.6 us -> 24.9 us  [the longest x2 8.8 us: shards(): jnp.einsum('bpsr,pbsd->brd', weight_hi, back, preferred_element_type=jnp....]
    convert_element_type x1, other arithmetic: 11.4 us -> 2.29 us  [shards(): (jax.nn.silu(mixed_in[:, :hidden_width]) * mixed_in[:, hidden_width:]).as...]
    convert_element_type x2 -> x0, other arithmetic: 7.19 us -> none  [the longest x1 5.05 us: spread(): return jnp.where(same[None, :, None, :, None], weight[:, :, :, None, :],...]
    all_to_all x4, waiting for transfers between devices: 100 us -> 106 us  [send(): lax.all_to_all(part.reshape(plane, cap, part.shape[1]), group, split_axis...]
    convert_element_type x0 -> x2, local copies, waits for them, and re-layouts: none -> 4.86 us  [shards(): blocks = [send(jnp.einsum('bpsr,brd->pbsd', select_parts[h], line_parts[h...]
    slice x1 -> x0, local copies, waits for them, and re-layouts: 4.68 us -> none  [shards(): local_sync[h * half:(h + 1) * half]]
    all_gather x2 -> x1, waiting for transfers between devices: 42.7 us -> 40 us  [shards(): lax.all_gather(mixed, 'tensor', axis=0, tiled=True)]
    unnamed x41 -> x30, local copies, waits for them, and re-layouts: 15.2 us -> 17.6 us
  transfers between devices with their start and end apart: 10 -> 9, of which waited for: 9 -> 8; matrix products, arithmetic and copies ran while one was open for 20% -> 17% of each run, Pallas kernels for 0% -> 0%
where the time goes in v4:
time: 424 us; the launch traced here: 416 us
  waiting for transfers between devices  250 us (59%)
  matrix products  67.4 us (16%)
  other arithmetic  27.8 us (7%)
  local copies, waits for them, and re-layouts  26.8 us (6%)
  starting transfers between devices  18.9 us (4%)
  between operations  14.6 us (3%)
  blocking collectives  10 us (2%)
    all_to_all x4, waiting for transfers between devices, send(): lax.all_to_all(part.reshape(plane, cap, part.shape[1]), group, split_axis...  106 us
    reduce_scatter x2, waiting for transfers between devices, shards(): lax.psum_scatter(partial.reshape(lines * rows, half), 'tensor', scatter_d...  41.2 us
    all_gather x1, waiting for transfers between devices, shards(): lax.all_gather(mixed, 'tensor', axis=0, tiled=True)  40 us
    all_gather x1, waiting for transfers between devices, shards(): line_a = lax.all_gather(packed, 'tensor', axis=0, tiled=False)  33.3 us
    all_gather x1, waiting for transfers between devices, shards(): line_b = lax.all_gather(normed[:, half:], 'tensor', axis=0, tiled=False)  29.2 us
    all_to_all x4, starting transfers between devices, send(): lax.all_to_all(part.reshape(plane, cap, part.shape[1]), group, split_axis...  18.4 us
    unnamed x30, local copies, waits for them, and re-layouts  17.6 us
    dot_general x2, matrix products, shards(): jnp.dot(hidden, down_proj[:, h * half:(h + 1) * half], preferred_element_...  12.8 us
  transfers between devices with their start and end apart: 9, of which 8 were waited for; matrix products, arithmetic and copies ran while one was open for 17% of the time, Pallas kernels for 0%

profile of v4, /device:TPU:0, one launch (start us, length us, event | category | flops | bytes accessed | tf_op | source)
XLA Modules:
  0.0 415.7 jit_solution(7019889560752308272)
XLA Ops:
  14.6 33.3 %all-gather.8.cloned.1.call-done = bf16[576,1024]{1,0:T(8,128)(2,1)} async-done(((bf16[144,1024]{1,0:T(8,128)(2,1)}), bf16[576,1024]{1,0:T(8,128)(2,1)}) %all-gather.8.cloned.1.call-update) | async-done | bytes 1179664 | tf_op jit(solution)/shard_map/all_gather | solution.py:71
  58.2 4.6 %all-to-all-start = ((bf16[8,256,1024]{2,1,0:T(8,128)(2,1)}), bf16[8,256,1024]{2,1,0:T(8,128)(2,1)}, u32[]{:S(2)}, u32[]{:S(2)}) async-start(bf16[8,256,1024]{2,1,0:T(8,128)(2,1)} %bitcast.103), calls=%async_computation | async-start | bytes 8388608 | tf_op jit(solution)/shard_map/all_to_all | solution.py:97
  63.5 29.2 %all-gather.10.cloned.1.call-done = bf16[512,1024]{1,0:T(8,128)(2,1)} async-done(((bf16[128,1024]{1,0:T(8,128)(2,1)}), bf16[512,1024]{1,0:T(8,128)(2,1)}) %all-gather.10.cloned.1.call-update) | async-done | bytes 1048592 | tf_op jit(solution)/shard_map/all_gather | solution.py:72
  97.7 14.3 %all-to-all-done = bf16[8,256,1024]{2,1,0:T(8,128)(2,1)} async-done(((bf16[8,256,1024]{2,1,0:T(8,128)(2,1)}), bf16[8,256,1024]{2,1,0:T(8,128)(2,1)}, u32[]{:S(2)}, u32[]{:S(2)}) %all-to-all-start) | async-done | bytes 4194336 | tf_op jit(solution)/shard_map/all_to_all | solution.py:97
  111.9 4.7 %all-to-all-start.1 = ((bf16[8,256,1024]{2,1,0:T(8,128)(2,1)}), bf16[8,256,1024]{2,1,0:T(8,128)(2,1)}, u32[]{:S(2)}, u32[]{:S(2)}) async-start(bf16[8,256,1024]{2,1,0:T(8,128)(2,1)} %bitcast.102), calls=%async_computation.1 | async-start | bytes 8388608 | tf_op jit(solution)/shard_map/all_to_all | solution.py:97
  116.7 8.8 %copy.63 = bf16[1,2048,1536]{1,2,0:T(8,128)(2,1)} copy(bf16[1,2048,1536]{2,1,0:T(8,128)(2,1)} %param.16) | data formatting | bytes 12582912 | tf_op args[4]
  125.6 4.6 %fusion = bf16[2048,1536]{0,1:T(8,128)(2,1)S(1)} fusion(bf16[1,2048,1536]{1,2,0:T(8,128)(2,1)} %copy.63, f32[2048,12]{0,1:T(8,128)S(1)} %bitcast.120), kind=kLoop, calls=%fused_computation.1 | loop fusion | flops 9437184 | bytes 12681216 | tf_op jit(solution)/shard_map/convert_element_type | solution.py:10
  138.1 12.7 %fusion.16 = f32[2048,1536]{1,0:T(8,128)} fusion(bf16[2048,1024]{1,0:T(8,128)(2,1)} %bitcast.7, bf16[2048,1536]{0,1:T(8,128)(2,1)S(1)} %fusion), kind=kOutput, calls=%fused_computation.28 | convolution fusion | flops 6442450944 | bytes 19922944 | tf_op jit(solution)/shard_map/dot_general | solution.py:112
  150.7 15.1 %all-to-all-done.1 = bf16[8,256,1024]{2,1,0:T(8,128)(2,1)} async-done(((bf16[8,256,1024]{2,1,0:T(8,128)(2,1)}), bf16[8,256,1024]{2,1,0:T(8,128)(2,1)}, u32[]{:S(2)}, u32[]{:S(2)}) %all-to-all-start.1) | async-done | bytes 4194336 | tf_op jit(solution)/shard_map/all_to_all | solution.py:97
  165.8 11.7 %convolution_add_fusion = f32[2048,1536]{1,0:T(8,128)S(1)} fusion(f32[2048,1536]{1,0:T(8,128)} %fusion.16, bf16[2048,1024]{1,0:T(8,128)(2,1)} %bitcast.15, bf16[2048,1536]{0,1:T(8,128)(2,1)} %copy-done), kind=kOutput, calls=%fused_computation.2 | convolution fusion | flops 6445596672 | bytes 32505856 | tf_op jit(solution)/shard_map/dot_general | solution.py:112
  179.9 5.1 %convolution_convert_fusion = bf16[2048,1024]{1,0:T(8,128)(2,1)} fusion(bf16[2048,768]{1,0:T(8,128)(2,1)S(1)} %fusion.3, bf16[768,2048]{1,0:T(8,128)(2,1)S(1)} %fusion.2), kind=kOutput, calls=%fused_computation.17 | convolution fusion | flops 3223322624 | bytes 8912896 | tf_op jit(solution)/shard_map/dot_general | solution.py:120
  185.0 4.6 %all-to-all-start.3 = ((bf16[8,256,1024]{2,1,0:T(8,128)(2,1)}), bf16[8,256,1024]{2,1,0:T(8,128)(2,1)}, u32[]{:S(2)}, u32[]{:S(2)}) async-start(bf16[8,256,1024]{2,1,0:T(8,128)(2,1)} %bitcast.112), calls=%async_computation.4 | async-start | bytes 8388608 | tf_op jit(solution)/shard_map/all_to_all | solution.py:97
  189.9 6.0 %select_reduce_fusion.1 = (bf16[4,512,128]{2,1,0:T(8,128)(2,1)S(1)}, bf16[4,512,128]{2,1,0:T(8,128)(2,1)S(1)}) fusion(f32[4,128,8]{1,2,0:T(8,128)S(1)} %convert_element_type.124, s32[4,128,8]{1,2,0:T(8,128)S(1)} %copy.60, f32[4,128,8]{1,2,0:T(8,128)S(1)} %convert_element_type.139), kind=kLoop, calls=%fused_computation.4 | loop fusion | flops 9961472 | bytes 1097728 | tf_op jit(solution)/shard_map/reduce_sum | solution.py:83
  195.9 7.7 %convolution_convert_fusion.1 = bf16[2048,1024]{1,0:T(8,128)(2,1)} fusion(bf16[2048,768]{1,0:T(8,128)(2,1)} %copy-done.4, bf16[768,2048]{1,0:T(8,128)(2,1)} %copy-done.3), kind=kOutput, calls=%fused_computation.18 | convolution fusion | flops 3223322624 | bytes 8912896 | tf_op jit(solution)/shard_map/dot_general | solution.py:120
  203.6 35.0 %all-to-all-done.3 = bf16[8,256,1024]{2,1,0:T(8,128)(2,1)} async-done(((bf16[8,256,1024]{2,1,0:T(8,128)(2,1)}), bf16[8,256,1024]{2,1,0:T(8,128)(2,1)}, u32[]{:S(2)}, u32[]{:S(2)}) %all-to-all-start.3) | async-done | bytes 4194336 | tf_op jit(solution)/shard_map/all_to_all | solution.py:97
  238.6 4.6 %all-to-all-start.2 = ((bf16[8,256,1024]{2,1,0:T(8,128)(2,1)}), bf16[8,256,1024]{2,1,0:T(8,128)(2,1)}, u32[]{:S(2)}, u32[]{:S(2)}) async-start(bf16[8,256,1024]{2,1,0:T(8,128)(2,1)} %bitcast.111), calls=%async_computation.2 | async-start | bytes 8388608 | tf_op jit(solution)/shard_map/all_to_all | solution.py:97
  246.2 4.4 %bitcast_add_fusion = f32[4,128,1024]{2,1,0:T(8,128)} fusion(f32[4,128,1024,1]{2,1,3,0:T(8,128)S(1)} %fusion.7, bf16[4,8,64,128]{3,2,1,0:T(8,128)(2,1)S(1)} %bitcast.106, bf16[8,4,64,1024]{3,2,1,0:T(8,128)(2,1)} %bitcast.27), kind=kOutput, calls=%fused_computation.32 | convolution fusion | flops 537395200 | bytes 8912896 | tf_op jit(solution)/shard_map/bpsr,pbsd->brd/dot_general | solution.py:125
  250.9 41.4 %all-to-all-done.2 = bf16[8,256,1024]{2,1,0:T(8,128)(2,1)} async-done(((bf16[8,256,1024]{2,1,0:T(8,128)(2,1)}), bf16[8,256,1024]{2,1,0:T(8,128)(2,1)}, u32[]{:S(2)}, u32[]{:S(2)}) %all-to-all-start.2) | async-done | bytes 4194336 | tf_op jit(solution)/shard_map/all_to_all | solution.py:97
  295.3 4.4 %bitcast_add_fusion.1 = f32[4,128,1024]{2,1,0:T(8,128)} fusion(f32[4,128,1024,1]{2,1,3,0:T(8,128)S(1)} %fusion.11, bf16[4,8,64,128]{3,2,1,0:T(8,128)(2,1)S(1)} %bitcast.107, bf16[8,4,64,1024]{3,2,1,0:T(8,128)(2,1)} %bitcast.19), kind=kOutput, calls=%fused_computation.33 | convolution fusion | flops 537395200 | bytes 8912896 | tf_op jit(solution)/shard_map/bpsr,pbsd->brd/dot_general | solution.py:125
  300.0 41.2 %reduce-scatter.3.cloned.1.call-done = f32[128,1024]{1,0:T(8,128)} async-done(((f32[512,1024]{1,0:T(8,128)}), f32[128,1024]{1,0:T(8,128)}) %reduce-scatter.3.cloned.1.call-update) | async-done | bytes 524304 | tf_op jit(solution)/shard_map/reduce_scatter | solution.py:128
  343.4 5.3 %copy.87 = bf16[256,8,2,512]{3,1,2,0:T(8,128)(2,1)} copy(bf16[256,8,2,512]{3,2,1,0:T(2,128)(2,1)} %bitcast.110) | data formatting | bytes 8388608
  348.9 40.0 %all-gather.6.cloned.1.call-done = bf16[512,2048]{1,0:T(8,128)(2,1)} async-done(((bf16[128,2048]{1,0:T(8,128)(2,1)}), bf16[512,2048]{1,0:T(8,128)(2,1)}) %all-gather.6.cloned.1.call-update) | async-done | bytes 2097168 | tf_op jit(solution)/shard_map/all_gather | solution.py:136
  388.8 5.2 %convolution_convert_fusion.2 = bf16[512,1024]{1,0:T(8,128)(2,1)S(1)} fusion(bf16[512,2048]{1,0:T(8,128)(2,1)} %all-gather.6.cloned.1.call-done, bf16[2048,1024]{1,0:T(8,128)(2,1)} %bitcast.113), kind=kOutput, calls=%fused_computation.37 | convolution fusion | flops 2148007936 | bytes 7340032 | tf_op jit(solution)/shard_map/dot_general | solution.py:135
  398.8 10.0 %psum.7 = f32[1,21]{1,0:T(1,128)} all-reduce(f32[1,21]{1,0:T(1,128)S(1)} %bitcast.126), channel_id=1, replica_groups=mesh['dp'=4,'expert'=2,'tensor'=4] {'tensor'}, use_global_device_ids=true, to_apply=%region_8.9 | all-reduce | flops 21 | bytes 168 | tf_op jit(solution)/shard_map/psum | solution.py:176
  (83 shorter events, 47.4 us)
Async XLA Ops:
  7.2 40.8 %all-gather.8.cloned.1.call-start = ((), (), s32[]{:S(2)}) async-start(), calls=%async_computation.9 | async-start | bytes 1474560 | tf_op jit(solution)/shard_map/all_gather | solution.py:71
  58.2 53.7 %all-to-all-start = ((bf16[8,256,1024]{2,1,0:T(8,128)(2,1)}), bf16[8,256,1024]{2,1,0:T(8,128)(2,1)}, u32[]{:S(2)}, u32[]{:S(2)}) async-start(bf16[8,256,1024]{2,1,0:T(8,128)(2,1)} %bitcast.103), calls=%async_computation | async-start | bytes 8388608 | tf_op jit(solution)/shard_map/all_to_all | solution.py:97
  62.8 29.9 %all-gather.10.cloned.1.call-start = ((), (), s32[]{:S(2)}) async-start(), calls=%async_computation.10 | async-start | bytes 1310720 | tf_op jit(solution)/shard_map/all_gather | solution.py:72
  111.9 53.9 %all-to-all-start.1 = ((bf16[8,256,1024]{2,1,0:T(8,128)(2,1)}), bf16[8,256,1024]{2,1,0:T(8,128)(2,1)}, u32[]{:S(2)}, u32[]{:S(2)}) async-start(bf16[8,256,1024]{2,1,0:T(8,128)(2,1)} %bitcast.102), calls=%async_computation.1 | async-start | bytes 8388608 | tf_op jit(solution)/shard_map/all_to_all | solution.py:97
  116.7 8.8 %copy-start.5 = (f32[1,16,12]{1,0,2:T(1,128)S(1)}, f32[1,16,12]{1,0,2:T(1,128)}, u32[]{:S(2)}) copy-start(f32[1,16,12]{1,0,2:T(1,128)} %param.17) | copy-start | bytes 2308
  116.7 8.9 %copy-start.6 = (f32[1,6,16]{2,0,1:T(1,128)S(1)}, f32[1,6,16]{2,0,1:T(1,128)}, u32[]{:S(2)}) copy-start(f32[1,6,16]{2,0,1:T(1,128)} %param.19) | copy-start | bytes 1156
  130.2 7.9 %copy-start = (bf16[2048,1536]{0,1:T(8,128)(2,1)}, bf16[2048,1536]{0,1:T(8,128)(2,1)S(1)}, u32[]{:S(2)}) copy-start(bf16[2048,1536]{0,1:T(8,128)(2,1)S(1)} %fusion) | copy-start | bytes 18874372
  130.2 4.2 %copy-start.2 = (bf16[1,768,2048]{2,1,0:T(8,128)(2,1)S(1)}, bf16[1,768,2048]{2,1,0:T(8,128)(2,1)}, u32[]{:S(2)}) copy-start(bf16[1,768,2048]{2,1,0:T(8,128)(2,1)} %param.18) | copy-start | bytes 9437188
  138.0 41.8 %copy-start.3 = (bf16[768,2048]{1,0:T(8,128)(2,1)}, bf16[768,2048]{1,0:T(8,128)(2,1)S(1)}, u32[]{:S(2)}) copy-start(bf16[768,2048]{1,0:T(8,128)(2,1)S(1)} %fusion.2) | copy-start | bytes 9437188
  179.8 5.1 %copy-start.4 = (bf16[2048,768]{1,0:T(8,128)(2,1)}, bf16[2048,768]{1,0:T(8,128)(2,1)S(1)}, u32[]{:S(2)}) copy-start(bf16[2048,768]{1,0:T(8,128)(2,1)S(1)} %fusion.3) | copy-start | bytes 9437188
  185.0 53.7 %all-to-all-start.3 = ((bf16[8,256,1024]{2,1,0:T(8,128)(2,1)}), bf16[8,256,1024]{2,1,0:T(8,128)(2,1)}, u32[]{:S(2)}, u32[]{:S(2)}) async-start(bf16[8,256,1024]{2,1,0:T(8,128)(2,1)} %bitcast.112), calls=%async_computation.4 | async-start | bytes 8388608 | tf_op jit(solution)/shard_map/all_to_all | solution.py:97
  238.6 53.7 %all-to-all-start.2 = ((bf16[8,256,1024]{2,1,0:T(8,128)(2,1)}), bf16[8,256,1024]{2,1,0:T(8,128)(2,1)}, u32[]{:S(2)}, u32[]{:S(2)}) async-start(bf16[8,256,1024]{2,1,0:T(8,128)(2,1)} %bitcast.111), calls=%async_computation.2 | async-start | bytes 8388608 | tf_op jit(solution)/shard_map/all_to_all | solution.py:97
  243.2 56.8 %reduce-scatter.5.cloned.1.call-start = ((), (), s32[]{:S(2)}) async-start(), calls=%async_computation.7 | async-start | bytes 2621440 | tf_op jit(solution)/shard_map/reduce_scatter | solution.py:128
  250.6 90.6 %reduce-scatter.3.cloned.1.call-start = ((), (), s32[]{:S(2)}) async-start(), calls=%async_computation.6 | async-start | bytes 2621440 | tf_op jit(solution)/shard_map/reduce_scatter | solution.py:128
  295.3 4.5 %copy-start.1 = (bf16[128,2048]{1,0:T(8,128)(2,1)S(1)}, bf16[128,2048]{1,0:T(8,128)(2,1)}, u32[]{:S(2)}) copy-start(bf16[128,2048]{1,0:T(8,128)(2,1)} %param.12) | copy-start | bytes 1572868
  299.8 89.0 %all-gather.6.cloned.1.call-start = ((), (), s32[]{:S(2)}) async-start(), calls=%async_computation.8 | async-start | bytes 2621440 | tf_op jit(solution)/shard_map/all_gather | solution.py:136
  343.4 5.4 %copy-start.8 = (s32[21]{0:T(128)S(1)}, s32[21]{0:T(128)}, u32[]{:S(2)}) copy-start(s32[21]{0:T(128)} %param.23) | copy-start | bytes 256
  343.4 5.4 %copy-start.7 = (s32[1,2,256]{2,1,0:T(2,128)S(1)}, s32[1,2,256]{2,1,0:T(2,128)}, u32[]{:S(2)}) copy-start(s32[1,2,256]{2,1,0:T(2,128)} %param.22) | copy-start | bytes 6148
  388.8 6.2 %copy-start.9 = (f32[4]{0:T(128)S(1)}, f32[4]{0:T(128)}, u32[]{:S(2)}) copy-start(f32[4]{0:T(128)} %param.21) | copy-start | bytes 52
Sparse Core Ops, SparseCore 0:
  14.7 33.1 all-gather.7
  65.2 27.4 all-gather.9
  250.8 43.3 reduce-scatter.4
  299.9 41.2 reduce-scatter.2
  343.5 45.2 all-gather.5

commit v5 on v4

--- a/solution.py
+++ b/solution.py
@@ -69,7 +69,13 @@
         axis=0,
     )
     line_a = lax.all_gather(packed, "tensor", axis=0, tiled=False)
-    line_b = lax.all_gather(normed[:, half:], "tensor", axis=0, tiled=False)
+    line_b = lax.all_to_all(
+        jnp.broadcast_to(normed[None, :, half:], (lines, rows, half)),
+        "tensor",
+        split_axis=0,
+        concat_axis=0,
+        tiled=True,
+    )
     line_routing = line_a[:, rows : rows + extra, :].reshape(lines, rows, 4 * top)
     ids_l = line_routing[:, :, :top].astype(jnp.int32)
     slot_l = line_routing[:, :, top : 2 * top].astype(jnp.int32)
@@ -125,9 +131,14 @@
         partial = jnp.einsum(
             "bpsr,pbsd->brd", weight_hi, back, preferred_element_type=jnp.float32
         ) + jnp.einsum("bpsr,pbsd->brd", weight_lo, back, preferred_element_type=jnp.float32)
-        combined = lax.psum_scatter(
-            partial.reshape(lines * rows, half), "tensor", scatter_dimension=0, tiled=True
-        )
+        if h == 0:
+            combined = lax.psum_scatter(
+                partial.reshape(lines * rows, half), "tensor", scatter_dimension=0, tiled=True
+            )
+        else:
+            combined = jnp.sum(
+                lax.all_to_all(partial, "tensor", split_axis=0, concat_axis=0, tiled=True), axis=0
+            )
         mixed_parts.append(x_float[:, h * half : (h + 1) * half] + combined)
     mixed = jnp.concatenate(mixed_parts, axis=1).astype(jnp.bfloat16)
 

time: 424 us -> 456 us (1.075); the launches traced: 416 us -> 453 us
  waiting for transfers between devices: 250 us -> 267 us
  starting transfers between devices: 18.9 us -> 28.9 us
  matrix products: 67.4 us -> 75.3 us
    all_to_all x0 -> x2, waiting for transfers between devices: none -> 44.1 us  [the longest x1 44.1 us: shards(): lax.all_to_all(partial, 'tensor', split_axis=0, concat_axis=0, tiled=True)]
    reduce_scatter x2 -> x1, waiting for transfers between devices: 41.2 us -> 0.02 us  [shards(): lax.psum_scatter(partial.reshape(lines * rows, half), 'tensor', scatter_d...]
    all_to_all x4, waiting for transfers between devices: 106 us -> 138 us  [send(): lax.all_to_all(part.reshape(plane, cap, part.shape[1]), group, split_axis...]
    all_gather x1 -> x0, waiting for transfers between devices: 29.2 us -> none  [shards(): line_b = lax.all_gather(normed[:, half:], 'tensor', axis=0, tiled=False)]
    all_gather x1, waiting for transfers between devices: 33.3 us -> 44.2 us  [shards(): line_a = lax.all_gather(packed, 'tensor', axis=0, tiled=False)]
    dot_general x2, matrix products: 12.8 us -> 23.1 us  [shards(): jnp.dot(hidden, down_proj[:, h * half:(h + 1) * half], preferred_element_...]
    all_to_all x0 -> x2, starting transfers between devices: none -> 10.1 us  [the longest x1 6.31 us: shards(): lax.all_to_all(jnp.broadcast_to(normed[None, :, half:], (lines, rows, hal...]
  transfers between devices with their start and end apart: 9 -> 9, of which waited for: 8 -> 7; matrix products, arithmetic and copies ran while one was open for 17% -> 18% of each run, Pallas kernels for 0% -> 0%
where the time goes in v5:
time: 456 us; the launch traced here: 453 us
  waiting for transfers between devices  267 us (59%)
  matrix products  75.3 us (17%)
  other arithmetic  29.5 us (6%)
  starting transfers between devices  28.9 us (6%)
  local copies, waits for them, and re-layouts  27.2 us (6%)
  between operations  14.4 us (3%)
  blocking collectives  10 us (2%)
    all_to_all x4, waiting for transfers between devices, send(): lax.all_to_all(part.reshape(plane, cap, part.shape[1]), group, split_axis...  138 us
    all_gather x1, waiting for transfers between devices, shards(): line_a = lax.all_gather(packed, 'tensor', axis=0, tiled=False)  44.2 us
    all_to_all x1, waiting for transfers between devices, shards(): lax.all_to_all(partial, 'tensor', split_axis=0, concat_axis=0, tiled=True)  44.1 us
    all_gather x1, waiting for transfers between devices, shards(): lax.all_gather(mixed, 'tensor', axis=0, tiled=True)  41.1 us
    dot_general x2, matrix products, shards(): jnp.dot(hidden, down_proj[:, h * half:(h + 1) * half], preferred_element_...  23.1 us
    all_to_all x4, starting transfers between devices, send(): lax.all_to_all(part.reshape(plane, cap, part.shape[1]), group, split_axis...  18.5 us
    unnamed x30, local copies, waits for them, and re-layouts  17.6 us
    dot_general x1, matrix products, shards(): jnp.dot(blocks[1], gate_up[half:], preferred_element_type=jnp.float32)  11.7 us
  transfers between devices with their start and end apart: 9, of which 7 were waited for; matrix products, arithmetic and copies ran while one was open for 18% of the time, Pallas kernels for 0%

profile of v5, /device:TPU:0, one launch (start us, length us, event | category | flops | bytes accessed | tf_op | source)
XLA Modules:
  0.0 452.5 jit_solution(5645678991984897313)
XLA Ops:
  15.0 6.3 %all-to-all-start.1 = ((bf16[4,128,1024]{2,1,0:T(8,128)(2,1)}), bf16[4,128,1024]{2,1,0:T(8,128)(2,1)S(1)}, u32[]{:S(2)}, u32[]{:S(2)}) async-start(bf16[4,128,1024]{2,1,0:T(8,128)(2,1)} %broadcast_in_dim.66), calls=%async_computation.1 | async-start | bytes 2097152 | tf_op jit(solution)/shard_map/all_to_all | solution.py:72
  21.3 44.2 %all-gather.6.cloned.1.call-done = bf16[576,1024]{1,0:T(8,128)(2,1)} async-done(((bf16[144,1024]{1,0:T(8,128)(2,1)}), bf16[576,1024]{1,0:T(8,128)(2,1)}) %all-gather.6.cloned.1.call-update) | async-done | bytes 1179664 | tf_op jit(solution)/shard_map/all_gather | solution.py:71
  75.8 4.6 %all-to-all-start = ((bf16[8,256,1024]{2,1,0:T(8,128)(2,1)}), bf16[8,256,1024]{2,1,0:T(8,128)(2,1)}, u32[]{:S(2)}, u32[]{:S(2)}) async-start(bf16[8,256,1024]{2,1,0:T(8,128)(2,1)} %bitcast.101), calls=%async_computation | async-start | bytes 8388608 | tf_op jit(solution)/shard_map/all_to_all | solution.py:103
  84.1 45.4 %all-to-all-done = bf16[8,256,1024]{2,1,0:T(8,128)(2,1)} async-done(((bf16[8,256,1024]{2,1,0:T(8,128)(2,1)}), bf16[8,256,1024]{2,1,0:T(8,128)(2,1)}, u32[]{:S(2)}, u32[]{:S(2)}) %all-to-all-start) | async-done | bytes 4194336 | tf_op jit(solution)/shard_map/all_to_all | solution.py:103
  129.5 4.8 %all-to-all-start.2 = ((bf16[8,256,1024]{2,1,0:T(8,128)(2,1)}), bf16[8,256,1024]{2,1,0:T(8,128)(2,1)}, u32[]{:S(2)}, u32[]{:S(2)}) async-start(bf16[8,256,1024]{2,1,0:T(8,128)(2,1)} %bitcast.100), calls=%async_computation.2 | async-start | bytes 8388608 | tf_op jit(solution)/shard_map/all_to_all | solution.py:103
  134.4 8.8 %copy.63 = bf16[1,2048,1536]{1,2,0:T(8,128)(2,1)} copy(bf16[1,2048,1536]{2,1,0:T(8,128)(2,1)} %param.16) | data formatting | bytes 12582912 | tf_op args[4]
  143.3 4.6 %fusion = bf16[2048,1536]{0,1:T(8,128)(2,1)S(1)} fusion(bf16[1,2048,1536]{1,2,0:T(8,128)(2,1)} %copy.63, f32[2048,12]{0,1:T(8,128)S(1)} %bitcast.116), kind=kLoop, calls=%fused_computation.1 | loop fusion | flops 9437184 | bytes 12681216 | tf_op jit(solution)/shard_map/convert_element_type | solution.py:10
  156.3 11.6 %fusion.16 = f32[2048,1536]{1,0:T(8,128)} fusion(bf16[2048,1024]{1,0:T(8,128)(2,1)} %bitcast.7, bf16[2048,1536]{0,1:T(8,128)(2,1)S(1)} %fusion), kind=kOutput, calls=%fused_computation.28 | convolution fusion | flops 6442450944 | bytes 19922944 | tf_op jit(solution)/shard_map/dot_general | solution.py:118
  167.8 15.6 %all-to-all-done.2 = bf16[8,256,1024]{2,1,0:T(8,128)(2,1)} async-done(((bf16[8,256,1024]{2,1,0:T(8,128)(2,1)}), bf16[8,256,1024]{2,1,0:T(8,128)(2,1)}, u32[]{:S(2)}, u32[]{:S(2)}) %all-to-all-start.2) | async-done | bytes 4194336 | tf_op jit(solution)/shard_map/all_to_all | solution.py:103
  183.5 11.7 %convolution_add_fusion = f32[2048,1536]{1,0:T(8,128)S(1)} fusion(f32[2048,1536]{1,0:T(8,128)} %fusion.16, bf16[2048,1024]{1,0:T(8,128)(2,1)} %bitcast.14, bf16[2048,1536]{0,1:T(8,128)(2,1)} %copy-done), kind=kOutput, calls=%fused_computation.2 | convolution fusion | flops 6445596672 | bytes 32505856 | tf_op jit(solution)/shard_map/dot_general | solution.py:118
  197.3 15.4 %convolution_convert_fusion.1 = bf16[2048,1024]{1,0:T(8,128)(2,1)} fusion(bf16[2048,768]{1,0:T(8,128)(2,1)S(1)} %fusion.3, bf16[768,2048]{1,0:T(8,128)(2,1)S(1)} %copy-done.3), kind=kOutput, calls=%fused_computation.18 | convolution fusion | flops 3223322624 | bytes 8912896 | tf_op jit(solution)/shard_map/dot_general | solution.py:126
  212.7 4.6 %all-to-all-start.3 = ((bf16[8,256,1024]{2,1,0:T(8,128)(2,1)}), bf16[8,256,1024]{2,1,0:T(8,128)(2,1)}, u32[]{:S(2)}, u32[]{:S(2)}) async-start(bf16[8,256,1024]{2,1,0:T(8,128)(2,1)} %bitcast.110), calls=%async_computation.3 | async-start | bytes 8388608 | tf_op jit(solution)/shard_map/all_to_all | solution.py:103
  217.3 7.7 %convolution_convert_fusion = bf16[2048,1024]{1,0:T(8,128)(2,1)} fusion(bf16[2048,768]{1,0:T(8,128)(2,1)} %copy-done.4, bf16[768,2048]{1,0:T(8,128)(2,1)} %fusion.2), kind=kOutput, calls=%fused_computation.17 | convolution fusion | flops 3223322624 | bytes 8912896 | tf_op jit(solution)/shard_map/dot_general | solution.py:126
  225.0 41.4 %all-to-all-done.3 = bf16[8,256,1024]{2,1,0:T(8,128)(2,1)} async-done(((bf16[8,256,1024]{2,1,0:T(8,128)(2,1)}), bf16[8,256,1024]{2,1,0:T(8,128)(2,1)}, u32[]{:S(2)}, u32[]{:S(2)}) %all-to-all-start.3) | async-done | bytes 4194336 | tf_op jit(solution)/shard_map/all_to_all | solution.py:103
  266.4 4.6 %all-to-all-start.4 = ((bf16[8,256,1024]{2,1,0:T(8,128)(2,1)}), bf16[8,256,1024]{2,1,0:T(8,128)(2,1)}, u32[]{:S(2)}, u32[]{:S(2)}) async-start(bf16[8,256,1024]{2,1,0:T(8,128)(2,1)} %bitcast.108), calls=%async_computation.5 | async-start | bytes 8388608 | tf_op jit(solution)/shard_map/all_to_all | solution.py:103
  271.4 6.0 %select_reduce_fusion.1 = (bf16[4,512,128]{2,1,0:T(8,128)(2,1)S(1)}, bf16[4,512,128]{2,1,0:T(8,128)(2,1)S(1)}) fusion(f32[4,128,8]{1,2,0:T(8,128)S(1)} %convert_element_type.124, s32[4,128,8]{1,2,0:T(8,128)S(1)} %copy.60, f32[4,128,8]{1,2,0:T(8,128)S(1)} %convert_element_type.139), kind=kLoop, calls=%fused_computation.4 | loop fusion | flops 9961472 | bytes 1097728 | tf_op jit(solution)/shard_map/reduce_sum | solution.py:89
  280.4 4.4 bitcast_add_fusion.1
  284.8 35.4 %all-to-all-done.4 = bf16[8,256,1024]{2,1,0:T(8,128)(2,1)} async-done(((bf16[8,256,1024]{2,1,0:T(8,128)(2,1)}), bf16[8,256,1024]{2,1,0:T(8,128)(2,1)}, u32[]{:S(2)}, u32[]{:S(2)}) %all-to-all-start.4) | async-done | bytes 4194336 | tf_op jit(solution)/shard_map/all_to_all | solution.py:103
  323.1 4.4 bitcast_add_fusion
  332.6 44.1 %all-to-all-done.5 = f32[4,128,1024]{2,1,0:T(8,128)S(1)} async-done(((f32[4,128,1024]{2,1,0:T(8,128)}), f32[4,128,1024]{2,1,0:T(8,128)S(1)}, u32[]{:S(2)}, u32[]{:S(2)}) %all-to-all-start.5) | async-done | bytes 2097184 | tf_op jit(solution)/shard_map/all_to_all | solution.py:140
  379.3 5.3 %copy.87 = bf16[256,8,2,512]{3,1,2,0:T(8,128)(2,1)} copy(bf16[256,8,2,512]{3,2,1,0:T(2,128)(2,1)} %bitcast.107) | data formatting | bytes 8388608
  384.7 41.1 %all-gather.4.cloned.1.call-done = bf16[512,2048]{1,0:T(8,128)(2,1)} async-done(((bf16[128,2048]{1,0:T(8,128)(2,1)}), bf16[512,2048]{1,0:T(8,128)(2,1)}) %all-gather.4.cloned.1.call-update) | async-done | bytes 2097168 | tf_op jit(solution)/shard_map/all_gather | solution.py:147
  425.8 5.2 %convolution_convert_fusion.2 = bf16[512,1024]{1,0:T(8,128)(2,1)S(1)} fusion(bf16[512,2048]{1,0:T(8,128)(2,1)} %all-gather.4.cloned.1.call-done, bf16[2048,1024]{1,0:T(8,128)(2,1)} %bitcast.109), kind=kOutput, calls=%fused_computation.37 | convolution fusion | flops 2148007936 | bytes 7340032 | tf_op jit(solution)/shard_map/dot_general | solution.py:146
  435.8 10.0 %psum.7 = f32[1,21]{1,0:T(1,128)} all-reduce(f32[1,21]{1,0:T(1,128)S(1)} %bitcast.122), channel_id=1, replica_groups=mesh['dp'=4,'expert'=2,'tensor'=4] {'tensor'}, use_global_device_ids=true, to_apply=%region_8.9 | all-reduce | flops 21 | bytes 168 | tf_op jit(solution)/shard_map/psum | solution.py:187
  (83 shorter events, 51.1 us)
Async XLA Ops:
  7.2 58.4 %all-gather.6.cloned.1.call-start = ((), (), s32[]{:S(2)}) async-start(), calls=%async_computation.9 | async-start | bytes 1474560 | tf_op jit(solution)/shard_map/all_gather | solution.py:71
  15.0 60.8 %all-to-all-start.1 = ((bf16[4,128,1024]{2,1,0:T(8,128)(2,1)}), bf16[4,128,1024]{2,1,0:T(8,128)(2,1)S(1)}, u32[]{:S(2)}, u32[]{:S(2)}) async-start(bf16[4,128,1024]{2,1,0:T(8,128)(2,1)} %broadcast_in_dim.66), calls=%async_computation.1 | async-start | bytes 2097152 | tf_op jit(solution)/shard_map/all_to_all | solution.py:72
  75.8 53.7 %all-to-all-start = ((bf16[8,256,1024]{2,1,0:T(8,128)(2,1)}), bf16[8,256,1024]{2,1,0:T(8,128)(2,1)}, u32[]{:S(2)}, u32[]{:S(2)}) async-start(bf16[8,256,1024]{2,1,0:T(8,128)(2,1)} %bitcast.101), calls=%async_computation | async-start | bytes 8388608 | tf_op jit(solution)/shard_map/all_to_all | solution.py:103
  129.5 54.0 %all-to-all-start.2 = ((bf16[8,256,1024]{2,1,0:T(8,128)(2,1)}), bf16[8,256,1024]{2,1,0:T(8,128)(2,1)}, u32[]{:S(2)}, u32[]{:S(2)}) async-start(bf16[8,256,1024]{2,1,0:T(8,128)(2,1)} %bitcast.100), calls=%async_computation.2 | async-start | bytes 8388608 | tf_op jit(solution)/shard_map/all_to_all | solution.py:103
  134.3 8.8 %copy-start.5 = (f32[1,16,12]{1,0,2:T(1,128)S(1)}, f32[1,16,12]{1,0,2:T(1,128)}, u32[]{:S(2)}) copy-start(f32[1,16,12]{1,0,2:T(1,128)} %param.17) | copy-start | bytes 2308
  134.4 8.9 %copy-start.6 = (f32[1,6,16]{2,0,1:T(1,128)S(1)}, f32[1,6,16]{2,0,1:T(1,128)}, u32[]{:S(2)}) copy-start(f32[1,6,16]{2,0,1:T(1,128)} %param.19) | copy-start | bytes 1156
  147.9 8.4 %copy-start = (bf16[2048,1536]{0,1:T(8,128)(2,1)}, bf16[2048,1536]{0,1:T(8,128)(2,1)S(1)}, u32[]{:S(2)}) copy-start(bf16[2048,1536]{0,1:T(8,128)(2,1)S(1)} %fusion) | copy-start | bytes 18874372
  147.9 4.2 copy-start.2
  195.2 2.1 copy-start.3
  197.3 15.4 %copy-start.4 = (bf16[2048,768]{1,0:T(8,128)(2,1)}, bf16[2048,768]{1,0:T(8,128)(2,1)S(1)}, u32[]{:S(2)}) copy-start(bf16[2048,768]{1,0:T(8,128)(2,1)S(1)} %fusion.3) | copy-start | bytes 9437188
  212.7 53.7 %all-to-all-start.3 = ((bf16[8,256,1024]{2,1,0:T(8,128)(2,1)}), bf16[8,256,1024]{2,1,0:T(8,128)(2,1)}, u32[]{:S(2)}, u32[]{:S(2)}) async-start(bf16[8,256,1024]{2,1,0:T(8,128)(2,1)} %bitcast.110), calls=%async_computation.3 | async-start | bytes 8388608 | tf_op jit(solution)/shard_map/all_to_all | solution.py:103
  266.4 53.7 %all-to-all-start.4 = ((bf16[8,256,1024]{2,1,0:T(8,128)(2,1)}), bf16[8,256,1024]{2,1,0:T(8,128)(2,1)}, u32[]{:S(2)}, u32[]{:S(2)}) async-start(bf16[8,256,1024]{2,1,0:T(8,128)(2,1)} %bitcast.108), calls=%async_computation.5 | async-start | bytes 8388608 | tf_op jit(solution)/shard_map/all_to_all | solution.py:103
  271.0 105.9 %reduce-scatter.2.cloned.1.call-start = ((), (), s32[]{:S(2)}) async-start(), calls=%async_computation.7 | async-start | bytes 2621440 | tf_op jit(solution)/shard_map/reduce_scatter | solution.py:135
  327.5 4.0 copy-start.1
  327.5 49.2 %all-to-all-start.5 = ((f32[4,128,1024]{2,1,0:T(8,128)}), f32[4,128,1024]{2,1,0:T(8,128)S(1)}, u32[]{:S(2)}, u32[]{:S(2)}) async-start(f32[4,128,1024]{2,1,0:T(8,128)} %bitcast_add_fusion), calls=%async_computation.6 | async-start | bytes 4194304 | tf_op jit(solution)/shard_map/all_to_all | solution.py:140
  331.3 94.6 %all-gather.4.cloned.1.call-start = ((), (), s32[]{:S(2)}) async-start(), calls=%async_computation.8 | async-start | bytes 2621440 | tf_op jit(solution)/shard_map/all_gather | solution.py:147
  379.3 5.4 %copy-start.8 = (s32[21]{0:T(128)S(1)}, s32[21]{0:T(128)}, u32[]{:S(2)}) copy-start(s32[21]{0:T(128)} %param.23) | copy-start | bytes 256
  379.3 5.4 %copy-start.7 = (s32[1,2,256]{2,1,0:T(2,128)S(1)}, s32[1,2,256]{2,1,0:T(2,128)}, u32[]{:S(2)}) copy-start(s32[1,2,256]{2,1,0:T(2,128)} %param.22) | copy-start | bytes 6148
  425.8 6.2 %copy-start.9 = (f32[4]{0:T(128)S(1)}, f32[4]{0:T(128)}, u32[]{:S(2)}) copy-start(f32[4]{0:T(128)} %param.21) | copy-start | bytes 52
Sparse Core Ops, SparseCore 0:
  14.1 51.4 all-gather.5
  284.9 44.1 reduce-scatter.1
  379.4 46.3 all-gather.3

commit v6 on v4

--- a/solution.py
+++ b/solution.py
@@ -173,7 +173,12 @@
     counts = (frames - jnp.abs(lag_offsets)).astype(jnp.float32)
     score = sums / jnp.sqrt(counts * head_size)[None, :]
     partial_logits = jnp.sum(head_weight[:, None] * score, axis=0)
-    sync_logits = lax.psum(partial_logits, "tensor")
+    sync_logits = partial_logits
+    step = 1
+    while step < lines:
+        pairs = [(i, i ^ step) for i in range(lines)]
+        sync_logits = sync_logits + lax.ppermute(sync_logits, "tensor", pairs)
+        step *= 2
     return (mixed, sync_logits[None, :])
 
 

time: 424 us -> 423 us (level)
  blocking collectives: 10 us -> 0 us
  waiting for transfers between devices: 250 us -> 257 us
    psum x1 -> x0, blocking collectives: 10 us -> none  [shards(): sync_logits = lax.psum(partial_logits, 'tensor')]
    ppermute x0 -> x2, waiting for transfers between devices: none -> 6.92 us  [shards(): sync_logits = sync_logits + lax.ppermute(sync_logits, 'tensor', pairs)]
  transfers between devices with their start and end apart: 9 -> 11, of which waited for: 8 -> 10; matrix products, arithmetic and copies ran while one was open for 17% -> 17% of each run, Pallas kernels for 0% -> 0%
where the time goes in v6:
time: 423 us; the launch traced here: 414 us
  waiting for transfers between devices  257 us (61%)
  matrix products  67.3 us (16%)
  other arithmetic  28.3 us (7%)
  local copies, waits for them, and re-layouts  26.8 us (6%)
  starting transfers between devices  20 us (5%)
  between operations  14.6 us (3%)
    all_to_all x4, waiting for transfers between devices, send(): lax.all_to_all(part.reshape(plane, cap, part.shape[1]), group, split_axis...  106 us
    reduce_scatter x2, waiting for transfers between devices, shards(): lax.psum_scatter(partial.reshape(lines * rows, half), 'tensor', scatter_d...  41.2 us
    all_gather x1, waiting for transfers between devices, shards(): lax.all_gather(mixed, 'tensor', axis=0, tiled=True)  40 us
    all_gather x1, waiting for transfers between devices, shards(): line_a = lax.all_gather(packed, 'tensor', axis=0, tiled=False)  33.3 us
    all_gather x1, waiting for transfers between devices, shards(): line_b = lax.all_gather(normed[:, half:], 'tensor', axis=0, tiled=False)  29.2 us
    all_to_all x4, starting transfers between devices, send(): lax.all_to_all(part.reshape(plane, cap, part.shape[1]), group, split_axis...  18.5 us
    unnamed x30, local copies, waits for them, and re-layouts  17.5 us
    dot_general x2, matrix products, shards(): jnp.dot(hidden, down_proj[:, h * half:(h + 1) * half], preferred_element_...  12.8 us
  transfers between devices with their start and end apart: 11, of which 10 were waited for; matrix products, arithmetic and copies ran while one was open for 17% of the time, Pallas kernels for 0%

profile of v6, /device:TPU:0, one launch (start us, length us, event | category | flops | bytes accessed | tf_op | source)
XLA Modules:
  0.0 414.3 jit_solution(18193351095152592969)
XLA Ops:
  14.6 33.3 %all-gather.8.cloned.1.call-done = bf16[576,1024]{1,0:T(8,128)(2,1)} async-done(((bf16[144,1024]{1,0:T(8,128)(2,1)}), bf16[576,1024]{1,0:T(8,128)(2,1)}) %all-gather.8.cloned.1.call-update) | async-done | bytes 1179664 | tf_op jit(solution)/shard_map/all_gather | solution.py:71
  49.4 4.0 fusion.1
  58.2 4.6 %all-to-all-start = ((bf16[8,256,1024]{2,1,0:T(8,128)(2,1)}), bf16[8,256,1024]{2,1,0:T(8,128)(2,1)}, u32[]{:S(2)}, u32[]{:S(2)}) async-start(bf16[8,256,1024]{2,1,0:T(8,128)(2,1)} %bitcast.104), calls=%async_computation | async-start | bytes 8388608 | tf_op jit(solution)/shard_map/all_to_all | solution.py:97
  63.6 29.2 %all-gather.10.cloned.1.call-done = bf16[512,1024]{1,0:T(8,128)(2,1)} async-done(((bf16[128,1024]{1,0:T(8,128)(2,1)}), bf16[512,1024]{1,0:T(8,128)(2,1)}) %all-gather.10.cloned.1.call-update) | async-done | bytes 1048592 | tf_op jit(solution)/shard_map/all_gather | solution.py:72
  97.7 14.3 %all-to-all-done = bf16[8,256,1024]{2,1,0:T(8,128)(2,1)} async-done(((bf16[8,256,1024]{2,1,0:T(8,128)(2,1)}), bf16[8,256,1024]{2,1,0:T(8,128)(2,1)}, u32[]{:S(2)}, u32[]{:S(2)}) %all-to-all-start) | async-done | bytes 4194336 | tf_op jit(solution)/shard_map/all_to_all | solution.py:97
  112.0 4.7 %all-to-all-start.1 = ((bf16[8,256,1024]{2,1,0:T(8,128)(2,1)}), bf16[8,256,1024]{2,1,0:T(8,128)(2,1)}, u32[]{:S(2)}, u32[]{:S(2)}) async-start(bf16[8,256,1024]{2,1,0:T(8,128)(2,1)} %bitcast.103), calls=%async_computation.1 | async-start | bytes 8388608 | tf_op jit(solution)/shard_map/all_to_all | solution.py:97
  116.7 8.7 %copy.63 = bf16[1,2048,1536]{1,2,0:T(8,128)(2,1)} copy(bf16[1,2048,1536]{2,1,0:T(8,128)(2,1)} %param.16) | data formatting | bytes 12582912 | tf_op args[4]
  125.6 4.6 %fusion = bf16[2048,1536]{0,1:T(8,128)(2,1)S(1)} fusion(bf16[1,2048,1536]{1,2,0:T(8,128)(2,1)} %copy.63, f32[2048,12]{0,1:T(8,128)S(1)} %bitcast.121), kind=kLoop, calls=%fused_computation.1 | loop fusion | flops 9437184 | bytes 12681216 | tf_op jit(solution)/shard_map/convert_element_type | solution.py:10
  138.0 12.6 %fusion.16 = f32[2048,1536]{1,0:T(8,128)} fusion(bf16[2048,1024]{1,0:T(8,128)(2,1)} %bitcast.7, bf16[2048,1536]{0,1:T(8,128)(2,1)S(1)} %fusion), kind=kOutput, calls=%fused_computation.28 | convolution fusion | flops 6442450944 | bytes 19922944 | tf_op jit(solution)/shard_map/dot_general | solution.py:112
  150.6 15.2 %all-to-all-done.1 = bf16[8,256,1024]{2,1,0:T(8,128)(2,1)} async-done(((bf16[8,256,1024]{2,1,0:T(8,128)(2,1)}), bf16[8,256,1024]{2,1,0:T(8,128)(2,1)}, u32[]{:S(2)}, u32[]{:S(2)}) %all-to-all-start.1) | async-done | bytes 4194336 | tf_op jit(solution)/shard_map/all_to_all | solution.py:97
  165.8 11.7 %convolution_add_fusion = f32[2048,1536]{1,0:T(8,128)S(1)} fusion(f32[2048,1536]{1,0:T(8,128)} %fusion.16, bf16[2048,1024]{1,0:T(8,128)(2,1)} %bitcast.15, bf16[2048,1536]{0,1:T(8,128)(2,1)} %copy-done), kind=kOutput, calls=%fused_computation.2 | convolution fusion | flops 6445596672 | bytes 32505856 | tf_op jit(solution)/shard_map/dot_general | solution.py:112
  179.9 5.1 %convolution_convert_fusion = bf16[2048,1024]{1,0:T(8,128)(2,1)} fusion(bf16[2048,768]{1,0:T(8,128)(2,1)S(1)} %fusion.3, bf16[768,2048]{1,0:T(8,128)(2,1)S(1)} %fusion.2), kind=kOutput, calls=%fused_computation.17 | convolution fusion | flops 3223322624 | bytes 8912896 | tf_op jit(solution)/shard_map/dot_general | solution.py:120
  185.0 4.6 %all-to-all-start.3 = ((bf16[8,256,1024]{2,1,0:T(8,128)(2,1)}), bf16[8,256,1024]{2,1,0:T(8,128)(2,1)}, u32[]{:S(2)}, u32[]{:S(2)}) async-start(bf16[8,256,1024]{2,1,0:T(8,128)(2,1)} %bitcast.113), calls=%async_computation.4 | async-start | bytes 8388608 | tf_op jit(solution)/shard_map/all_to_all | solution.py:97
  189.9 6.0 %select_reduce_fusion.1 = (bf16[4,512,128]{2,1,0:T(8,128)(2,1)S(1)}, bf16[4,512,128]{2,1,0:T(8,128)(2,1)S(1)}) fusion(f32[4,128,8]{1,2,0:T(8,128)S(1)} %convert_element_type.124, s32[4,128,8]{1,2,0:T(8,128)S(1)} %copy.60, f32[4,128,8]{1,2,0:T(8,128)S(1)} %convert_element_type.139), kind=kLoop, calls=%fused_computation.4 | loop fusion | flops 9961472 | bytes 1097728 | tf_op jit(solution)/shard_map/reduce_sum | solution.py:83
  195.9 7.7 %convolution_convert_fusion.1 = bf16[2048,1024]{1,0:T(8,128)(2,1)} fusion(bf16[2048,768]{1,0:T(8,128)(2,1)} %copy-done.4, bf16[768,2048]{1,0:T(8,128)(2,1)} %copy-done.3), kind=kOutput, calls=%fused_computation.18 | convolution fusion | flops 3223322624 | bytes 8912896 | tf_op jit(solution)/shard_map/dot_general | solution.py:120
  203.6 35.0 %all-to-all-done.3 = bf16[8,256,1024]{2,1,0:T(8,128)(2,1)} async-done(((bf16[8,256,1024]{2,1,0:T(8,128)(2,1)}), bf16[8,256,1024]{2,1,0:T(8,128)(2,1)}, u32[]{:S(2)}, u32[]{:S(2)}) %all-to-all-start.3) | async-done | bytes 4194336 | tf_op jit(solution)/shard_map/all_to_all | solution.py:97
  238.6 4.6 %all-to-all-start.2 = ((bf16[8,256,1024]{2,1,0:T(8,128)(2,1)}), bf16[8,256,1024]{2,1,0:T(8,128)(2,1)}, u32[]{:S(2)}, u32[]{:S(2)}) async-start(bf16[8,256,1024]{2,1,0:T(8,128)(2,1)} %bitcast.112), calls=%async_computation.2 | async-start | bytes 8388608 | tf_op jit(solution)/shard_map/all_to_all | solution.py:97
  246.3 4.4 %bitcast_add_fusion = f32[4,128,1024]{2,1,0:T(8,128)} fusion(f32[4,128,1024,1]{2,1,3,0:T(8,128)S(1)} %fusion.7, bf16[4,8,64,128]{3,2,1,0:T(8,128)(2,1)S(1)} %bitcast.107, bf16[8,4,64,1024]{3,2,1,0:T(8,128)(2,1)} %bitcast.27), kind=kOutput, calls=%fused_computation.32 | convolution fusion | flops 537395200 | bytes 8912896 | tf_op jit(solution)/shard_map/bpsr,pbsd->brd/dot_general | solution.py:125
  251.0 41.4 %all-to-all-done.2 = bf16[8,256,1024]{2,1,0:T(8,128)(2,1)} async-done(((bf16[8,256,1024]{2,1,0:T(8,128)(2,1)}), bf16[8,256,1024]{2,1,0:T(8,128)(2,1)}, u32[]{:S(2)}, u32[]{:S(2)}) %all-to-all-start.2) | async-done | bytes 4194336 | tf_op jit(solution)/shard_map/all_to_all | solution.py:97
  295.4 4.5 %bitcast_add_fusion.1 = f32[4,128,1024]{2,1,0:T(8,128)} fusion(f32[4,128,1024,1]{2,1,3,0:T(8,128)S(1)} %fusion.11, bf16[4,8,64,128]{3,2,1,0:T(8,128)(2,1)S(1)} %bitcast.108, bf16[8,4,64,1024]{3,2,1,0:T(8,128)(2,1)} %bitcast.19), kind=kOutput, calls=%fused_computation.33 | convolution fusion | flops 537395200 | bytes 8912896 | tf_op jit(solution)/shard_map/bpsr,pbsd->brd/dot_general | solution.py:125
  300.0 41.2 %reduce-scatter.3.cloned.1.call-done = f32[128,1024]{1,0:T(8,128)} async-done(((f32[512,1024]{1,0:T(8,128)}), f32[128,1024]{1,0:T(8,128)}) %reduce-scatter.3.cloned.1.call-update) | async-done | bytes 524304 | tf_op jit(solution)/shard_map/reduce_scatter | solution.py:128
  343.5 5.3 %copy.87 = bf16[256,8,2,512]{3,1,2,0:T(8,128)(2,1)} copy(bf16[256,8,2,512]{3,2,1,0:T(2,128)(2,1)} %bitcast.111) | data formatting | bytes 8388608
  348.9 40.0 %all-gather.6.cloned.1.call-done = bf16[512,2048]{1,0:T(8,128)(2,1)} async-done(((bf16[128,2048]{1,0:T(8,128)(2,1)}), bf16[512,2048]{1,0:T(8,128)(2,1)}) %all-gather.6.cloned.1.call-update) | async-done | bytes 2097168 | tf_op jit(solution)/shard_map/all_gather | solution.py:136
  388.9 5.2 %convolution_convert_fusion.2 = bf16[512,1024]{1,0:T(8,128)(2,1)S(1)} fusion(bf16[512,2048]{1,0:T(8,128)(2,1)} %all-gather.6.cloned.1.call-done, bf16[2048,1024]{1,0:T(8,128)(2,1)} %bitcast.114), kind=kOutput, calls=%fused_computation.37 | convolution fusion | flops 2148007936 | bytes 7340032 | tf_op jit(solution)/shard_map/dot_general | solution.py:135
  (88 shorter events, 52.0 us)
Async XLA Ops:
  7.2 40.8 %all-gather.8.cloned.1.call-start = ((), (), s32[]{:S(2)}) async-start(), calls=%async_computation.9 | async-start | bytes 1474560 | tf_op jit(solution)/shard_map/all_gather | solution.py:71
  58.2 53.7 %all-to-all-start = ((bf16[8,256,1024]{2,1,0:T(8,128)(2,1)}), bf16[8,256,1024]{2,1,0:T(8,128)(2,1)}, u32[]{:S(2)}, u32[]{:S(2)}) async-start(bf16[8,256,1024]{2,1,0:T(8,128)(2,1)} %bitcast.104), calls=%async_computation | async-start | bytes 8388608 | tf_op jit(solution)/shard_map/all_to_all | solution.py:97
  62.8 29.9 %all-gather.10.cloned.1.call-start = ((), (), s32[]{:S(2)}) async-start(), calls=%async_computation.10 | async-start | bytes 1310720 | tf_op jit(solution)/shard_map/all_gather | solution.py:72
  112.0 53.9 %all-to-all-start.1 = ((bf16[8,256,1024]{2,1,0:T(8,128)(2,1)}), bf16[8,256,1024]{2,1,0:T(8,128)(2,1)}, u32[]{:S(2)}, u32[]{:S(2)}) async-start(bf16[8,256,1024]{2,1,0:T(8,128)(2,1)} %bitcast.103), calls=%async_computation.1 | async-start | bytes 8388608 | tf_op jit(solution)/shard_map/all_to_all | solution.py:97
  116.7 8.7 %copy-start.5 = (f32[1,16,12]{1,0,2:T(1,128)S(1)}, f32[1,16,12]{1,0,2:T(1,128)}, u32[]{:S(2)}) copy-start(f32[1,16,12]{1,0,2:T(1,128)} %param.17) | copy-start | bytes 2308
  116.7 8.9 %copy-start.6 = (f32[1,6,16]{2,0,1:T(1,128)S(1)}, f32[1,6,16]{2,0,1:T(1,128)}, u32[]{:S(2)}) copy-start(f32[1,6,16]{2,0,1:T(1,128)} %param.19) | copy-start | bytes 1156
  130.2 7.9 %copy-start = (bf16[2048,1536]{0,1:T(8,128)(2,1)}, bf16[2048,1536]{0,1:T(8,128)(2,1)S(1)}, u32[]{:S(2)}) copy-start(bf16[2048,1536]{0,1:T(8,128)(2,1)S(1)} %fusion) | copy-start | bytes 18874372
  130.2 4.2 %copy-start.2 = (bf16[1,768,2048]{2,1,0:T(8,128)(2,1)S(1)}, bf16[1,768,2048]{2,1,0:T(8,128)(2,1)}, u32[]{:S(2)}) copy-start(bf16[1,768,2048]{2,1,0:T(8,128)(2,1)} %param.18) | copy-start | bytes 9437188
  138.0 41.9 %copy-start.3 = (bf16[768,2048]{1,0:T(8,128)(2,1)}, bf16[768,2048]{1,0:T(8,128)(2,1)S(1)}, u32[]{:S(2)}) copy-start(bf16[768,2048]{1,0:T(8,128)(2,1)S(1)} %fusion.2) | copy-start | bytes 9437188
  179.9 5.1 %copy-start.4 = (bf16[2048,768]{1,0:T(8,128)(2,1)}, bf16[2048,768]{1,0:T(8,128)(2,1)S(1)}, u32[]{:S(2)}) copy-start(bf16[2048,768]{1,0:T(8,128)(2,1)S(1)} %fusion.3) | copy-start | bytes 9437188
  185.0 53.7 %all-to-all-start.3 = ((bf16[8,256,1024]{2,1,0:T(8,128)(2,1)}), bf16[8,256,1024]{2,1,0:T(8,128)(2,1)}, u32[]{:S(2)}, u32[]{:S(2)}) async-start(bf16[8,256,1024]{2,1,0:T(8,128)(2,1)} %bitcast.113), calls=%async_computation.4 | async-start | bytes 8388608 | tf_op jit(solution)/shard_map/all_to_all | solution.py:97
  238.6 53.7 %all-to-all-start.2 = ((bf16[8,256,1024]{2,1,0:T(8,128)(2,1)}), bf16[8,256,1024]{2,1,0:T(8,128)(2,1)}, u32[]{:S(2)}, u32[]{:S(2)}) async-start(bf16[8,256,1024]{2,1,0:T(8,128)(2,1)} %bitcast.112), calls=%async_computation.2 | async-start | bytes 8388608 | tf_op jit(solution)/shard_map/all_to_all | solution.py:97
  243.3 56.8 %reduce-scatter.5.cloned.1.call-start = ((), (), s32[]{:S(2)}) async-start(), calls=%async_computation.7 | async-start | bytes 2621440 | tf_op jit(solution)/shard_map/reduce_scatter | solution.py:128
  250.7 90.6 %reduce-scatter.3.cloned.1.call-start = ((), (), s32[]{:S(2)}) async-start(), calls=%async_computation.6 | async-start | bytes 2621440 | tf_op jit(solution)/shard_map/reduce_scatter | solution.py:128
  295.4 4.5 %copy-start.1 = (bf16[128,2048]{1,0:T(8,128)(2,1)S(1)}, bf16[128,2048]{1,0:T(8,128)(2,1)}, u32[]{:S(2)}) copy-start(bf16[128,2048]{1,0:T(8,128)(2,1)} %param.12) | copy-start | bytes 1572868
  299.8 89.0 %all-gather.6.cloned.1.call-start = ((), (), s32[]{:S(2)}) async-start(), calls=%async_computation.8 | async-start | bytes 2621440 | tf_op jit(solution)/shard_map/all_gather | solution.py:136
  343.5 5.4 %copy-start.8 = (s32[21]{0:T(128)S(1)}, s32[21]{0:T(128)}, u32[]{:S(2)}) copy-start(s32[21]{0:T(128)} %param.23) | copy-start | bytes 256
  343.5 5.4 %copy-start.7 = (s32[1,2,256]{2,1,0:T(2,128)S(1)}, s32[1,2,256]{2,1,0:T(2,128)}, u32[]{:S(2)}) copy-start(s32[1,2,256]{2,1,0:T(2,128)} %param.22) | copy-start | bytes 6148
  388.9 6.2 %copy-start.9 = (f32[4]{0:T(128)S(1)}, f32[4]{0:T(128)}, u32[]{:S(2)}) copy-start(f32[4]{0:T(128)} %param.21) | copy-start | bytes 52
  398.8 3.6 collective-permute-start
  402.4 4.4 %collective-permute-start.1 = (f32[21]{0:T(128)S(1)}, f32[21]{0:T(128)S(1)}, u32[]{:S(2)}, u32[]{:S(2)}) collective-permute-start(f32[21]{0:T(128)S(1)} %add.60), channel_id=1, source_target_pairs={{0,2},{1,3},{2,0},{3,1},{4,6},{5,7},{6,4},{7,5},{8,10},{9,11},{10,... | collective-permute-start | bytes 260 | tf_op jit(solution)/shard_map/ppermute | solution.py:180
Sparse Core Ops, SparseCore 0:
  14.8 33.1 all-gather.7
  65.2 27.4 all-gather.9
  250.8 43.3 reduce-scatter.4
  300.0 41.2 reduce-scatter.2
  343.6 45.2 all-gather.5

commit v7 on v6

--- a/solution.py
+++ b/solution.py
@@ -128,14 +128,23 @@
         combined = lax.psum_scatter(
             partial.reshape(lines * rows, half), "tensor", scatter_dimension=0, tiled=True
         )
-        mixed_parts.append(x_float[:, h * half : (h + 1) * half] + combined)
-    mixed = jnp.concatenate(mixed_parts, axis=1).astype(jnp.bfloat16)
+        mixed_parts.append((x_float[:, h * half : (h + 1) * half] + combined).astype(jnp.bfloat16))
+    mixed = jnp.concatenate(mixed_parts, axis=1)
+    line_mixed = [
+        lax.all_to_all(
+            jnp.broadcast_to(mixed_parts[0][None], (lines, rows, half)),
+            "tensor",
+            split_axis=0,
+            concat_axis=0,
+            tiled=True,
+        ).reshape(lines * rows, half),
+        lax.all_gather(mixed_parts[1], "tensor", axis=0, tiled=True),
+    ]
 
     local_sync = w_sync.reshape(width, -1)
-    proj = jnp.dot(
-        lax.all_gather(mixed, "tensor", axis=0, tiled=True),
-        local_sync,
-        preferred_element_type=jnp.float32,
+    proj = (
+        jnp.dot(line_mixed[0], local_sync[:half], preferred_element_type=jnp.float32)
+        + jnp.dot(line_mixed[1], local_sync[half:], preferred_element_type=jnp.float32)
     ).astype(jnp.bfloat16)
     half = proj.shape[1] // 2
     heads_here = head_weight.shape[0]

time: 423 us -> 425 us (level)
  waiting for transfers between devices: 257 us -> 250 us
    all_gather x1, waiting for transfers between devices: 40 us -> 0.01 us  [shards(): lax.all_gather(mixed_parts[1], 'tensor', axis=0, tiled=True)]
    all_to_all x0 -> x1, waiting for transfers between devices: none -> 32 us  [shards(): lax.all_to_all(jnp.broadcast_to(mixed_parts[0][None], (lines, rows, half)...]
    slice x0 -> x1, local copies, waits for them, and re-layouts: none -> 4.68 us  [shards(): local_sync[half:]]
    unnamed x30 -> x35, local copies, waits for them, and re-layouts: 17.5 us -> 14.7 us
  transfers between devices with their start and end apart: 11 -> 12, of which waited for: 10 -> 10; matrix products, arithmetic and copies ran while one was open for 17% -> 19% of each run, Pallas kernels for 0% -> 0%
where the time goes in v7:
time: 425 us; the launch traced here: 416 us
  waiting for transfers between devices  250 us (59%)
  matrix products  69.6 us (16%)
  other arithmetic  29.8 us (7%)
  local copies, waits for them, and re-layouts  29.7 us (7%)
  starting transfers between devices  22.5 us (5%)
  between operations  14.7 us (3%)
    all_to_all x4, waiting for transfers between devices, send(): lax.all_to_all(part.reshape(plane, cap, part.shape[1]), group, split_axis...  106 us
    reduce_scatter x2, waiting for transfers between devices, shards(): lax.psum_scatter(partial.reshape(lines * rows, half), 'tensor', scatter_d...  41.3 us
    all_gather x1, waiting for transfers between devices, shards(): line_a = lax.all_gather(packed, 'tensor', axis=0, tiled=False)  33.3 us
    all_to_all x1, waiting for transfers between devices, shards(): lax.all_to_all(jnp.broadcast_to(mixed_parts[0][None], (lines, rows, half)...  32 us
    all_gather x1, waiting for transfers between devices, shards(): line_b = lax.all_gather(normed[:, half:], 'tensor', axis=0, tiled=False)  29.2 us
    all_to_all x4, starting transfers between devices, send(): lax.all_to_all(part.reshape(plane, cap, part.shape[1]), group, split_axis...  18.5 us
    unnamed x35, local copies, waits for them, and re-layouts  14.7 us
    dot_general x2, matrix products, shards(): jnp.dot(hidden, down_proj[:, h * half:(h + 1) * half], preferred_element_...  12.8 us
  transfers between devices with their start and end apart: 12, of which 10 were waited for; matrix products, arithmetic and copies ran while one was open for 19% of the time, Pallas kernels for 0%

profile of v7, /device:TPU:0, one launch (start us, length us, event | category | flops | bytes accessed | tf_op | source)
XLA Modules:
  0.0 416.1 jit_solution(14725292041479259336)
XLA Ops:
  14.6 33.3 %all-gather.8.cloned.1.call-done = bf16[576,1024]{1,0:T(8,128)(2,1)} async-done(((bf16[144,1024]{1,0:T(8,128)(2,1)}), bf16[576,1024]{1,0:T(8,128)(2,1)}) %all-gather.8.cloned.1.call-update) | async-done | bytes 1179664 | tf_op jit(solution)/shard_map/all_gather | solution.py:71
  49.4 4.0 fusion.1
  58.2 4.5 %all-to-all-start = ((bf16[8,256,1024]{2,1,0:T(8,128)(2,1)}), bf16[8,256,1024]{2,1,0:T(8,128)(2,1)}, u32[]{:S(2)}, u32[]{:S(2)}) async-start(bf16[8,256,1024]{2,1,0:T(8,128)(2,1)} %bitcast.109), calls=%async_computation | async-start | bytes 8388608 | tf_op jit(solution)/shard_map/all_to_all | solution.py:97
  63.5 29.2 %all-gather.10.cloned.1.call-done = bf16[512,1024]{1,0:T(8,128)(2,1)} async-done(((bf16[128,1024]{1,0:T(8,128)(2,1)}), bf16[512,1024]{1,0:T(8,128)(2,1)}) %all-gather.10.cloned.1.call-update) | async-done | bytes 1048592 | tf_op jit(solution)/shard_map/all_gather | solution.py:72
  97.7 14.2 %all-to-all-done = bf16[8,256,1024]{2,1,0:T(8,128)(2,1)} async-done(((bf16[8,256,1024]{2,1,0:T(8,128)(2,1)}), bf16[8,256,1024]{2,1,0:T(8,128)(2,1)}, u32[]{:S(2)}, u32[]{:S(2)}) %all-to-all-start) | async-done | bytes 4194336 | tf_op jit(solution)/shard_map/all_to_all | solution.py:97
  111.9 4.7 %all-to-all-start.1 = ((bf16[8,256,1024]{2,1,0:T(8,128)(2,1)}), bf16[8,256,1024]{2,1,0:T(8,128)(2,1)}, u32[]{:S(2)}, u32[]{:S(2)}) async-start(bf16[8,256,1024]{2,1,0:T(8,128)(2,1)} %bitcast.108), calls=%async_computation.1 | async-start | bytes 8388608 | tf_op jit(solution)/shard_map/all_to_all | solution.py:97
  116.7 8.8 %copy.63 = bf16[1,2048,1536]{1,2,0:T(8,128)(2,1)} copy(bf16[1,2048,1536]{2,1,0:T(8,128)(2,1)} %param.16) | data formatting | bytes 12582912 | tf_op args[4]
  125.6 4.6 %fusion = bf16[2048,1536]{0,1:T(8,128)(2,1)S(1)} fusion(bf16[1,2048,1536]{1,2,0:T(8,128)(2,1)} %copy.63, f32[2048,12]{0,1:T(8,128)S(1)} %bitcast.129), kind=kLoop, calls=%fused_computation.1 | loop fusion | flops 9437184 | bytes 12681216 | tf_op jit(solution)/shard_map/convert_element_type | solution.py:10
  138.0 12.7 %fusion.16 = f32[2048,1536]{1,0:T(8,128)} fusion(bf16[2048,1024]{1,0:T(8,128)(2,1)} %bitcast.7, bf16[2048,1536]{0,1:T(8,128)(2,1)S(1)} %fusion), kind=kOutput, calls=%fused_computation.28 | convolution fusion | flops 6442450944 | bytes 19922944 | tf_op jit(solution)/shard_map/dot_general | solution.py:112
  150.7 15.0 %all-to-all-done.1 = bf16[8,256,1024]{2,1,0:T(8,128)(2,1)} async-done(((bf16[8,256,1024]{2,1,0:T(8,128)(2,1)}), bf16[8,256,1024]{2,1,0:T(8,128)(2,1)}, u32[]{:S(2)}, u32[]{:S(2)}) %all-to-all-start.1) | async-done | bytes 4194336 | tf_op jit(solution)/shard_map/all_to_all | solution.py:97
  165.8 11.7 %convolution_add_fusion = f32[2048,1536]{1,0:T(8,128)S(1)} fusion(f32[2048,1536]{1,0:T(8,128)} %fusion.16, bf16[2048,1024]{1,0:T(8,128)(2,1)} %bitcast.15, bf16[2048,1536]{0,1:T(8,128)(2,1)} %copy-done), kind=kOutput, calls=%fused_computation.2 | convolution fusion | flops 6445596672 | bytes 32505856 | tf_op jit(solution)/shard_map/dot_general | solution.py:112
  179.8 5.1 %convolution_convert_fusion = bf16[2048,1024]{1,0:T(8,128)(2,1)} fusion(bf16[2048,768]{1,0:T(8,128)(2,1)S(1)} %fusion.3, bf16[768,2048]{1,0:T(8,128)(2,1)S(1)} %fusion.2), kind=kOutput, calls=%fused_computation.17 | convolution fusion | flops 3223322624 | bytes 8912896 | tf_op jit(solution)/shard_map/dot_general | solution.py:120
  184.9 4.6 %all-to-all-start.3 = ((bf16[8,256,1024]{2,1,0:T(8,128)(2,1)}), bf16[8,256,1024]{2,1,0:T(8,128)(2,1)}, u32[]{:S(2)}, u32[]{:S(2)}) async-start(bf16[8,256,1024]{2,1,0:T(8,128)(2,1)} %bitcast.119), calls=%async_computation.4 | async-start | bytes 8388608 | tf_op jit(solution)/shard_map/all_to_all | solution.py:97
  189.8 6.0 %select_reduce_fusion.1 = (bf16[4,512,128]{2,1,0:T(8,128)(2,1)S(1)}, bf16[4,512,128]{2,1,0:T(8,128)(2,1)S(1)}) fusion(f32[4,128,8]{1,2,0:T(8,128)S(1)} %convert_element_type.129, s32[4,128,8]{1,2,0:T(8,128)S(1)} %copy.60, f32[4,128,8]{1,2,0:T(8,128)S(1)} %convert_element_type.144), kind=kLoop, calls=%fused_computation.4 | loop fusion | flops 9961472 | bytes 1097728 | tf_op jit(solution)/shard_map/reduce_sum | solution.py:83
  195.9 7.7 %convolution_convert_fusion.1 = bf16[2048,1024]{1,0:T(8,128)(2,1)} fusion(bf16[2048,768]{1,0:T(8,128)(2,1)} %copy-done.4, bf16[768,2048]{1,0:T(8,128)(2,1)} %copy-done.3), kind=kOutput, calls=%fused_computation.18 | convolution fusion | flops 3223322624 | bytes 8912896 | tf_op jit(solution)/shard_map/dot_general | solution.py:120
  203.6 35.0 %all-to-all-done.3 = bf16[8,256,1024]{2,1,0:T(8,128)(2,1)} async-done(((bf16[8,256,1024]{2,1,0:T(8,128)(2,1)}), bf16[8,256,1024]{2,1,0:T(8,128)(2,1)}, u32[]{:S(2)}, u32[]{:S(2)}) %all-to-all-start.3) | async-done | bytes 4194336 | tf_op jit(solution)/shard_map/all_to_all | solution.py:97
  238.6 4.6 %all-to-all-start.2 = ((bf16[8,256,1024]{2,1,0:T(8,128)(2,1)}), bf16[8,256,1024]{2,1,0:T(8,128)(2,1)}, u32[]{:S(2)}, u32[]{:S(2)}) async-start(bf16[8,256,1024]{2,1,0:T(8,128)(2,1)} %bitcast.118), calls=%async_computation.2 | async-start | bytes 8388608 | tf_op jit(solution)/shard_map/all_to_all | solution.py:97
  246.3 4.4 %bitcast_add_fusion = f32[4,128,1024]{2,1,0:T(8,128)} fusion(f32[4,128,1024,1]{2,1,3,0:T(8,128)S(1)} %fusion.7, bf16[4,8,64,128]{3,2,1,0:T(8,128)(2,1)S(1)} %bitcast.114, bf16[8,4,64,1024]{3,2,1,0:T(8,128)(2,1)} %bitcast.27), kind=kOutput, calls=%fused_computation.32 | convolution fusion | flops 537395200 | bytes 8912896 | tf_op jit(solution)/shard_map/bpsr,pbsd->brd/dot_general | solution.py:125
  251.0 41.4 %all-to-all-done.2 = bf16[8,256,1024]{2,1,0:T(8,128)(2,1)} async-done(((bf16[8,256,1024]{2,1,0:T(8,128)(2,1)}), bf16[8,256,1024]{2,1,0:T(8,128)(2,1)}, u32[]{:S(2)}, u32[]{:S(2)}) %all-to-all-start.2) | async-done | bytes 4194336 | tf_op jit(solution)/shard_map/all_to_all | solution.py:97
  295.4 4.4 %bitcast_add_fusion.1 = f32[4,128,1024]{2,1,0:T(8,128)} fusion(f32[4,128,1024,1]{2,1,3,0:T(8,128)S(1)} %fusion.11, bf16[4,8,64,128]{3,2,1,0:T(8,128)(2,1)S(1)} %bitcast.115, bf16[8,4,64,1024]{3,2,1,0:T(8,128)(2,1)} %bitcast.19), kind=kOutput, calls=%fused_computation.33 | convolution fusion | flops 537395200 | bytes 8912896 | tf_op jit(solution)/shard_map/bpsr,pbsd->brd/dot_general | solution.py:125
  300.0 41.3 %reduce-scatter.3.cloned.1.call-done = f32[128,1024]{1,0:T(8,128)} async-done(((f32[512,1024]{1,0:T(8,128)}), f32[128,1024]{1,0:T(8,128)}) %reduce-scatter.3.cloned.1.call-update) | async-done | bytes 524304 | tf_op jit(solution)/shard_map/reduce_scatter | solution.py:128
  348.5 4.7 %fusion.68 = (bf16[1024,2,512]{2,1,0:T(2,128)(2,1)S(1)}, bf16[1024,2,512]{2,1,0:T(2,128)(2,1)S(1)}) fusion(bf16[2048,2,512]{2,1,0:T(2,128)(2,1)} %param.20), kind=kLoop, calls=%fused_computation.100 | loop fusion | bytes 8388608 | tf_op jit(solution)/shard_map/slice | solution.py:147
  356.4 32.0 %all-to-all-done.4 = bf16[4,128,1024]{2,1,0:T(8,128)(2,1)S(1)} async-done(((bf16[4,128,1024]{2,1,0:T(8,128)(2,1)}), bf16[4,128,1024]{2,1,0:T(8,128)(2,1)S(1)}, u32[]{:S(2)}, u32[]{:S(2)}) %all-to-all-start.4) | async-done | bytes 1048608 | tf_op jit(solution)/shard_map/all_to_all | solution.py:134
  388.5 4.1 fusion.72
  (98 shorter events, 63.4 us)
Async XLA Ops:
  7.2 40.8 %all-gather.8.cloned.1.call-start = ((), (), s32[]{:S(2)}) async-start(), calls=%async_computation.10 | async-start | bytes 1474560 | tf_op jit(solution)/shard_map/all_gather | solution.py:71
  58.2 53.7 %all-to-all-start = ((bf16[8,256,1024]{2,1,0:T(8,128)(2,1)}), bf16[8,256,1024]{2,1,0:T(8,128)(2,1)}, u32[]{:S(2)}, u32[]{:S(2)}) async-start(bf16[8,256,1024]{2,1,0:T(8,128)(2,1)} %bitcast.109), calls=%async_computation | async-start | bytes 8388608 | tf_op jit(solution)/shard_map/all_to_all | solution.py:97
  62.8 29.9 %all-gather.10.cloned.1.call-start = ((), (), s32[]{:S(2)}) async-start(), calls=%async_computation.11 | async-start | bytes 1310720 | tf_op jit(solution)/shard_map/all_gather | solution.py:72
  111.9 53.9 %all-to-all-start.1 = ((bf16[8,256,1024]{2,1,0:T(8,128)(2,1)}), bf16[8,256,1024]{2,1,0:T(8,128)(2,1)}, u32[]{:S(2)}, u32[]{:S(2)}) async-start(bf16[8,256,1024]{2,1,0:T(8,128)(2,1)} %bitcast.108), calls=%async_computation.1 | async-start | bytes 8388608 | tf_op jit(solution)/shard_map/all_to_all | solution.py:97
  116.6 8.8 %copy-start.7 = (f32[1,16,12]{1,0,2:T(1,128)S(1)}, f32[1,16,12]{1,0,2:T(1,128)}, u32[]{:S(2)}) copy-start(f32[1,16,12]{1,0,2:T(1,128)} %param.17) | copy-start | bytes 2308
  116.6 8.9 %copy-start.8 = (f32[1,6,16]{2,0,1:T(1,128)S(1)}, f32[1,6,16]{2,0,1:T(1,128)}, u32[]{:S(2)}) copy-start(f32[1,6,16]{2,0,1:T(1,128)} %param.19) | copy-start | bytes 1156
  130.2 7.9 %copy-start = (bf16[2048,1536]{0,1:T(8,128)(2,1)}, bf16[2048,1536]{0,1:T(8,128)(2,1)S(1)}, u32[]{:S(2)}) copy-start(bf16[2048,1536]{0,1:T(8,128)(2,1)S(1)} %fusion) | copy-start | bytes 18874372
  130.2 4.2 %copy-start.2 = (bf16[1,768,2048]{2,1,0:T(8,128)(2,1)S(1)}, bf16[1,768,2048]{2,1,0:T(8,128)(2,1)}, u32[]{:S(2)}) copy-start(bf16[1,768,2048]{2,1,0:T(8,128)(2,1)} %param.18) | copy-start | bytes 9437188
  138.0 41.8 %copy-start.3 = (bf16[768,2048]{1,0:T(8,128)(2,1)}, bf16[768,2048]{1,0:T(8,128)(2,1)S(1)}, u32[]{:S(2)}) copy-start(bf16[768,2048]{1,0:T(8,128)(2,1)S(1)} %fusion.2) | copy-start | bytes 9437188
  179.8 5.1 %copy-start.4 = (bf16[2048,768]{1,0:T(8,128)(2,1)}, bf16[2048,768]{1,0:T(8,128)(2,1)S(1)}, u32[]{:S(2)}) copy-start(bf16[2048,768]{1,0:T(8,128)(2,1)S(1)} %fusion.3) | copy-start | bytes 9437188
  184.9 53.7 %all-to-all-start.3 = ((bf16[8,256,1024]{2,1,0:T(8,128)(2,1)}), bf16[8,256,1024]{2,1,0:T(8,128)(2,1)}, u32[]{:S(2)}, u32[]{:S(2)}) async-start(bf16[8,256,1024]{2,1,0:T(8,128)(2,1)} %bitcast.119), calls=%async_computation.4 | async-start | bytes 8388608 | tf_op jit(solution)/shard_map/all_to_all | solution.py:97
  238.6 53.7 %all-to-all-start.2 = ((bf16[8,256,1024]{2,1,0:T(8,128)(2,1)}), bf16[8,256,1024]{2,1,0:T(8,128)(2,1)}, u32[]{:S(2)}, u32[]{:S(2)}) async-start(bf16[8,256,1024]{2,1,0:T(8,128)(2,1)} %bitcast.118), calls=%async_computation.2 | async-start | bytes 8388608 | tf_op jit(solution)/shard_map/all_to_all | solution.py:97
  243.3 56.7 %reduce-scatter.5.cloned.1.call-start = ((), (), s32[]{:S(2)}) async-start(), calls=%async_computation.8 | async-start | bytes 2621440 | tf_op jit(solution)/shard_map/reduce_scatter | solution.py:128
  250.7 90.6 %reduce-scatter.3.cloned.1.call-start = ((), (), s32[]{:S(2)}) async-start(), calls=%async_computation.7 | async-start | bytes 2621440 | tf_op jit(solution)/shard_map/reduce_scatter | solution.py:128
  295.4 4.5 %copy-start.1 = (bf16[128,2048]{1,0:T(8,128)(2,1)S(1)}, bf16[128,2048]{1,0:T(8,128)(2,1)}, u32[]{:S(2)}) copy-start(bf16[128,2048]{1,0:T(8,128)(2,1)} %param.12) | copy-start | bytes 1572868
  344.4 44.1 %all-to-all-start.4 = ((bf16[4,128,1024]{2,1,0:T(8,128)(2,1)}), bf16[4,128,1024]{2,1,0:T(8,128)(2,1)S(1)}, u32[]{:S(2)}, u32[]{:S(2)}) async-start(bf16[4,128,1024]{2,1,0:T(8,128)(2,1)} %broadcast_in_dim.69), calls=%async_computation.6 | async-start | bytes 2097152 | tf_op jit(solution)/shard_map/all_to_all | solution.py:134
  347.9 44.7 %all-gather.6.cloned.1.call-start = ((), (), s32[]{:S(2)}) async-start(), calls=%async_computation.9 | async-start | bytes 1310720 | tf_op jit(solution)/shard_map/all_gather | solution.py:141
  353.2 3.2 copy-start.10
  353.2 3.2 copy-start.9
  392.6 4.2 %copy-start.6 = (s32[256,256]{1,0:T(8,128)S(1)}, s32[256,256]{1,0:T(8,128)}, u32[]{:S(2)}) copy-start(s32[256,256]{1,0:T(8,128)} %iota_subtract_fusion) | copy-start | bytes 786436
  392.6 4.3 %copy-start.11 = (f32[4]{0:T(128)S(1)}, f32[4]{0:T(128)}, u32[]{:S(2)}) copy-start(f32[4]{0:T(128)} %param.21) | copy-start | bytes 52
  395.8 8.4 %copy-start.5 = (bf16[128,1024]{1,0:T(8,128)(2,1)S(1)}, bf16[128,1024]{1,0:T(8,128)(2,1)}, u32[]{:S(2)}) copy-start(bf16[128,1024]{1,0:T(8,128)(2,1)} %get-tuple-element.7) | copy-start | bytes 786436
  400.6 3.6 collective-permute-start
  404.2 4.4 %collective-permute-start.1 = (f32[21]{0:T(128)S(1)}, f32[21]{0:T(128)S(1)}, u32[]{:S(2)}, u32[]{:S(2)}) collective-permute-start(f32[21]{0:T(128)S(1)} %add.64), channel_id=1, source_target_pairs={{0,2},{1,3},{2,0},{3,1},{4,6},{5,7},{6,4},{7,5},{8,10},{9,11},{10,... | collective-permute-start | bytes 260 | tf_op jit(solution)/shard_map/ppermute | solution.py:189
Sparse Core Ops, SparseCore 0:
  14.7 33.1 all-gather.7
  65.2 27.4 all-gather.9
  250.8 43.3 reduce-scatter.4
  300.0 41.2 reduce-scatter.2
  350.6 40.3 all-gather.5

commit v8 on v6

--- a/solution.py
+++ b/solution.py
@@ -79,39 +79,63 @@
     target = jnp.where(mine, (ids_l // lines) * most + slot_l, -1)
     slot_ids = jnp.arange(plane * most, dtype=jnp.int32)
     match = target[:, None, :, :] == slot_ids[None, :, None, None]
-    select = jnp.any(match, axis=3)
+    order = (here + jnp.arange(lines, dtype=jnp.int32)) % lines
+    select = jnp.any(match, axis=3).astype(jnp.bfloat16).reshape(lines, plane, most, rows)
+    select_rel = jnp.take(select, order[1:], axis=0)
     weight_hi = jnp.sum(jnp.where(match, gate_hi[:, None, :, :], 0.0), axis=3)
     weight_lo = jnp.sum(jnp.where(match, gate_lo[:, None, :, :], 0.0), axis=3)
-    select = select.astype(jnp.bfloat16).reshape(lines, plane, most, rows)
-    select_pad = jnp.pad(select, ((0, 0), (0, 0), (0, 0), (0, padded - rows)))
-    weight_hi = weight_hi.astype(jnp.bfloat16).reshape(lines, plane, most, rows)
-    weight_lo = weight_lo.astype(jnp.bfloat16).reshape(lines, plane, most, rows)
-    line_parts = [line_a, line_b]
-    select_parts = [select_pad, select]
+    weight_hi = jnp.take(
+        weight_hi.astype(jnp.bfloat16).reshape(lines, plane, most, rows), order, axis=0
+    )
+    weight_lo = jnp.take(
+        weight_lo.astype(jnp.bfloat16).reshape(lines, plane, most, rows), order, axis=0
+    )
+    line_parts = [
+        jnp.take(line_a[:, :rows], order[1:], axis=0),
+        jnp.take(line_b, order[1:], axis=0),
+    ]
+    own_target = jnp.where(
+        (expert_ids % lines) == here,
+        (expert_ids // lines) * most + slots.astype(jnp.int32),
+        -1,
+    )
+    own_select = jnp.any(
+        own_target[None, :, :] == slot_ids[:, None, None], axis=2
+    ).astype(jnp.bfloat16)
     gate_up = dequant(w_in[0], scale_in[0])
     down_proj = dequant(w_out[0], scale_out[0])
     hidden_width = down_proj.shape[0]
     group = ("dp", "expert")
 
-    def send(part):
+    def send(part, depth):
         moved = lax.all_to_all(
-            part.reshape(plane, cap, part.shape[1]), group, split_axis=0, concat_axis=0, tiled=True
+            part.reshape(plane, depth, part.shape[-1]), group, split_axis=0, concat_axis=0, tiled=True
         )
-        return moved.reshape(plane * cap, part.shape[1])
-
+        return moved.reshape(plane * depth, part.shape[-1])
+
+    own_block = send(
+        jnp.dot(own_select, normed, preferred_element_type=jnp.float32).astype(jnp.bfloat16), most
+    )
     blocks = [
         send(
             jnp.einsum(
-                "bpsr,brd->pbsd", select_parts[h], line_parts[h], preferred_element_type=jnp.float32
-            )
-            .astype(jnp.bfloat16)
-            .reshape(plane * cap, half)
+                "dpsr,drD->pdsD", select_rel, line_parts[h], preferred_element_type=jnp.float32
+            ).astype(jnp.bfloat16),
+            cap - most,
         )
         for h in range(2)
     ]
+    own_in = jnp.dot(own_block, gate_up, preferred_element_type=jnp.float32)
     mixed_in = jnp.dot(blocks[0], gate_up[:half], preferred_element_type=jnp.float32) + jnp.dot(
         blocks[1], gate_up[half:], preferred_element_type=jnp.float32
     )
+    mixed_in = jnp.concatenate(
+        [
+            own_in.reshape(plane, most, -1),
+            mixed_in.reshape(plane, cap - most, -1),
+        ],
+        axis=1,
+    ).reshape(plane * cap, -1)
     hidden = (jax.nn.silu(mixed_in[:, :hidden_width]) * mixed_in[:, hidden_width:]).astype(
         jnp.bfloat16
     )
@@ -120,11 +144,12 @@
         output = jnp.dot(
             hidden, down_proj[:, h * half : (h + 1) * half], preferred_element_type=jnp.float32
         ).astype(jnp.bfloat16)
-        back = send(output)
+        back = send(output, cap)
         back = back.reshape(plane, lines, most, half)
         partial = jnp.einsum(
             "bpsr,pbsd->brd", weight_hi, back, preferred_element_type=jnp.float32
         ) + jnp.einsum("bpsr,pbsd->brd", weight_lo, back, preferred_element_type=jnp.float32)
+        partial = jnp.take(partial, (jnp.arange(lines, dtype=jnp.int32) - here) % lines, axis=0)
         combined = lax.psum_scatter(
             partial.reshape(lines * rows, half), "tensor", scatter_dimension=0, tiled=True
         )

time: 423 us -> 476 us (1.13)
  other arithmetic: 28.3 us -> 48.2 us
  waiting for transfers between devices: 257 us -> 270 us
  local copies, waits for them, and re-layouts: 26.8 us -> 37.8 us
  starting transfers between devices: 20 us -> 25.6 us
    reduce_scatter x2, waiting for transfers between devices: 41.2 us -> 85.7 us  [shards(): lax.psum_scatter(partial.reshape(lines * rows, half), 'tensor', scatter_d...]
    all_to_all x4 -> x5, waiting for transfers between devices: 106 us -> 82.4 us  [send(): lax.all_to_all(part.reshape(plane, depth, part.shape[-1]), group, split_a...]
    concatenate x0 -> x1, other arithmetic: none -> 10.4 us  [shards(): jnp.concatenate([own_in.reshape(plane, most, -1), mixed_in.reshape(plane,...]
    gather x0 -> x7, local copies, waits for them, and re-layouts: none -> 10.1 us  [the longest x2 5.74 us: shards(): jnp.take(partial, (jnp.arange(lines, dtype=jnp.int32) - here) % lines, ax...]
    all_gather x1, waiting for transfers between devices: 33.3 us -> 24.9 us  [shards(): line_a = lax.all_gather(packed, 'tensor', axis=0, tiled=False)]
    dot_general x2 -> x4, matrix products: 4.97 us -> 10.9 us  [the longest x1 6.79 us: shards(): own_in = jnp.dot(own_block, gate_up, preferred_element_type=jnp.float32)]
    all_to_all x4 -> x5, starting transfers between devices: 18.5 us -> 23.8 us  [send(): lax.all_to_all(part.reshape(plane, depth, part.shape[-1]), group, split_a...]
    unnamed x30 -> x34, local copies, waits for them, and re-layouts: 17.5 us -> 17.7 us
  transfers between devices with their start and end apart: 11 -> 12, of which waited for: 10 -> 10; matrix products, arithmetic and copies ran while one was open for 17% -> 17% of each run, Pallas kernels for 0% -> 0%
where the time goes in v8:
time: 476 us; the launch traced here: 467 us
  waiting for transfers between devices  270 us (57%)
  matrix products  70.3 us (15%)
  other arithmetic  48.2 us (10%)
  local copies, waits for them, and re-layouts  37.8 us (8%)
  starting transfers between devices  25.6 us (5%)
  between operations  14.7 us (3%)
    reduce_scatter x2, waiting for transfers between devices, shards(): lax.psum_scatter(partial.reshape(lines * rows, half), 'tensor', scatter_d...  85.7 us
    all_to_all x5, waiting for transfers between devices, send(): lax.all_to_all(part.reshape(plane, depth, part.shape[-1]), group, split_a...  82.4 us
    all_gather x1, waiting for transfers between devices, shards(): lax.all_gather(mixed, 'tensor', axis=0, tiled=True)  40 us
    all_gather x1, waiting for transfers between devices, shards(): line_b = lax.all_gather(normed[:, half:], 'tensor', axis=0, tiled=False)  29.2 us
    all_gather x1, waiting for transfers between devices, shards(): line_a = lax.all_gather(packed, 'tensor', axis=0, tiled=False)  24.9 us
    all_to_all x5, starting transfers between devices, send(): lax.all_to_all(part.reshape(plane, depth, part.shape[-1]), group, split_a...  23.8 us
    unnamed x34, local copies, waits for them, and re-layouts  17.7 us
    dot_general x2, matrix products, shards(): jnp.dot(hidden, down_proj[:, h * half:(h + 1) * half], preferred_element_...  12.9 us
  transfers between devices with their start and end apart: 12, of which 10 were waited for; matrix products, arithmetic and copies ran while one was open for 17% of the time, Pallas kernels for 0%

profile of v8, /device:TPU:0, one launch (start us, length us, event | category | flops | bytes accessed | tf_op | source)
XLA Modules:
  0.0 466.9 jit_solution(13818687059788800563)
XLA Ops:
  17.8 5.2 %all-to-all-start = ((bf16[8,64,2048]{2,1,0:T(8,128)(2,1)}), bf16[8,64,2048]{2,1,0:T(8,128)(2,1)}, u32[]{:S(2)}, u32[]{:S(2)}) async-start(bf16[8,64,2048]{2,1,0:T(8,128)(2,1)} %bitcast.2), calls=%async_computation | async-start | bytes 4194304 | tf_op jit(solution)/shard_map/all_to_all | solution.py:111
  23.1 24.9 %all-gather.8.cloned.1.call-done = bf16[576,1024]{1,0:T(8,128)(2,1)} async-done(((bf16[144,1024]{1,0:T(8,128)(2,1)}), bf16[576,1024]{1,0:T(8,128)(2,1)}) %all-gather.8.cloned.1.call-update) | async-done | bytes 1179664 | tf_op jit(solution)/shard_map/all_gather | solution.py:71
  59.1 4.6 all-to-all-start.1
  64.5 29.2 %all-gather.10.cloned.1.call-done = bf16[512,1024]{1,0:T(8,128)(2,1)} async-done(((bf16[128,1024]{1,0:T(8,128)(2,1)}), bf16[512,1024]{1,0:T(8,128)(2,1)}) %all-gather.10.cloned.1.call-update) | async-done | bytes 1048592 | tf_op jit(solution)/shard_map/all_gather | solution.py:72
  101.6 4.9 %all-to-all-start.2 = ((bf16[8,192,1024]{2,1,0:T(8,128)(2,1)}), bf16[8,192,1024]{2,1,0:T(8,128)(2,1)}, u32[]{:S(2)}, u32[]{:S(2)}) async-start(bf16[8,192,1024]{2,1,0:T(8,128)(2,1)} %bitcast.16), calls=%async_computation.2 | async-start | bytes 6291456 | tf_op jit(solution)/shard_map/all_to_all | solution.py:111
  106.6 8.8 %copy.84 = bf16[1,2048,1536]{1,2,0:T(8,128)(2,1)} copy(bf16[1,2048,1536]{2,1,0:T(8,128)(2,1)} %param.22) | data formatting | bytes 12582912 | tf_op args[4]
  128.5 6.8 %fusion.4 = f32[8,64,1536]{2,1,0:T(8,128)} fusion(bf16[8,64,2048]{2,1,0:T(8,128)(2,1)} %all-to-all-done, bf16[2048,1536]{0,1:T(8,128)(2,1)S(1)} %fusion), kind=kOutput, calls=%fused_computation.19 | convolution fusion | flops 3221225472 | bytes 11534336 | tf_op jit(solution)/shard_map/dot_general | solution.py:128
  135.3 9.5 %fusion.18 = f32[1536,1536]{1,0:T(8,128)} fusion(bf16[1536,1024]{1,0:T(8,128)(2,1)} %bitcast.11, bf16[2048,1536]{0,1:T(8,128)(2,1)S(1)} %fusion), kind=kOutput, calls=%fused_computation.36 | convolution fusion | flops 4831838208 | bytes 15728640 | tf_op jit(solution)/shard_map/dot_general | solution.py:129
  144.8 11.5 %convolution_add_fusion = f32[1536,1536]{1,0:T(8,128)} fusion(f32[1536,1536]{1,0:T(8,128)} %fusion.18, bf16[1536,1024]{1,0:T(8,128)(2,1)} %bitcast.17, bf16[2048,1536]{0,1:T(8,128)(2,1)} %copy-done.2), kind=kOutput, calls=%fused_computation.10 | convolution fusion | flops 4834197504 | bytes 25165824 | tf_op jit(solution)/shard_map/dot_general | solution.py:129
  156.2 10.4 %pad_maximum_fusion = f32[8,256,1536]{2,1,0:T(8,128)} fusion(f32[8,192,1536]{2,1,0:T(8,128)} %bitcast.108, f32[8,64,1536]{2,1,0:T(8,128)} %fusion.4), kind=kLoop, calls=%fused_computation.7 | loop fusion | flops 3145728 | bytes 25165824 | tf_op jit(solution)/shard_map/concatenate | solution.py:132
  166.6 5.7 %fusion.3 = bf16[2048,768]{1,0:T(8,128)(2,1)S(1)} fusion(f32[2048,1536]{1,0:T(8,128)} %bitcast.106), kind=kLoop, calls=%fused_computation.18 | loop fusion | flops 9437184 | bytes 15728640 | tf_op jit(solution)/shard_map/convert_element_type | solution.py:139
  172.3 5.1 %convolution_convert_fusion = bf16[2048,1024]{1,0:T(8,128)(2,1)} fusion(bf16[2048,768]{1,0:T(8,128)(2,1)S(1)} %fusion.3, bf16[768,2048]{1,0:T(8,128)(2,1)S(1)} %copy-done.5), kind=kOutput, calls=%fused_computation.25 | convolution fusion | flops 3223322624 | bytes 8912896 | tf_op jit(solution)/shard_map/dot_general | solution.py:144
  177.5 4.6 all-to-all-start.4
  182.0 7.8 %convolution_convert_fusion.1 = bf16[2048,1024]{1,0:T(8,128)(2,1)} fusion(bf16[2048,768]{1,0:T(8,128)(2,1)} %copy-done.6, bf16[768,2048]{1,0:T(8,128)(2,1)} %fusion.2), kind=kOutput, calls=%fused_computation.26 | convolution fusion | flops 3223322624 | bytes 8912896 | tf_op jit(solution)/shard_map/dot_general | solution.py:144
  189.8 41.4 %all-to-all-done.4 = bf16[8,256,1024]{2,1,0:T(8,128)(2,1)} async-done(((bf16[8,256,1024]{2,1,0:T(8,128)(2,1)}), bf16[8,256,1024]{2,1,0:T(8,128)(2,1)}, u32[]{:S(2)}, u32[]{:S(2)}) %all-to-all-start.4) | async-done | bytes 4194336 | tf_op jit(solution)/shard_map/all_to_all | solution.py:111
  231.1 4.6 all-to-all-start.3
  236.4 6.0 %select_reduce_fusion.1 = (bf16[4,512,128]{2,1,0:T(8,128)(2,1)S(1)}, bf16[4,512,128]{2,1,0:T(8,128)(2,1)S(1)}) fusion(f32[4,128,8]{1,2,0:T(8,128)S(1)} %convert_element_type.141, s32[4,128,8]{1,2,0:T(8,128)S(1)} %copy.77, f32[4,128,8]{1,2,0:T(8,128)S(1)} %convert_element_type.161), kind=kLoop, calls=%fused_computation.12 | loop fusion | flops 9961472 | bytes 1097728 | tf_op jit(solution)/shard_map/reduce_sum | solution.py:85
  246.7 38.1 %all-to-all-done.3 = bf16[8,256,1024]{2,1,0:T(8,128)(2,1)} async-done(((bf16[8,256,1024]{2,1,0:T(8,128)(2,1)}), bf16[8,256,1024]{2,1,0:T(8,128)(2,1)}, u32[]{:S(2)}, u32[]{:S(2)}) %all-to-all-start.3) | async-done | bytes 4194336 | tf_op jit(solution)/shard_map/all_to_all | solution.py:111
  292.3 4.6 bitcast_add_fusion.1
  308.1 40.2 %reduce-scatter.3.cloned.1.call-done = f32[128,1024]{1,0:T(8,128)} async-done(((f32[512,1024]{1,0:T(8,128)}), f32[128,1024]{1,0:T(8,128)}) %reduce-scatter.3.cloned.1.call-update) | async-done | bytes 524304 | tf_op jit(solution)/shard_map/reduce_scatter | solution.py:153
  348.3 45.5 %reduce-scatter.5.cloned.1.call-done = f32[128,1024]{1,0:T(8,128)} async-done(((f32[512,1024]{1,0:T(8,128)}), f32[128,1024]{1,0:T(8,128)}) %reduce-scatter.5.cloned.1.call-update) | async-done | bytes 524304 | tf_op jit(solution)/shard_map/reduce_scatter | solution.py:153
  396.0 5.3 %copy.112 = bf16[256,8,2,512]{3,1,2,0:T(8,128)(2,1)} copy(bf16[256,8,2,512]{3,2,1,0:T(2,128)(2,1)} %bitcast.111) | data formatting | bytes 8388608
  401.4 40.0 %all-gather.6.cloned.1.call-done = bf16[512,2048]{1,0:T(8,128)(2,1)} async-done(((bf16[128,2048]{1,0:T(8,128)(2,1)}), bf16[512,2048]{1,0:T(8,128)(2,1)}) %all-gather.6.cloned.1.call-update) | async-done | bytes 2097168 | tf_op jit(solution)/shard_map/all_gather | solution.py:161
  441.4 5.2 %convolution_convert_fusion.3 = bf16[512,1024]{1,0:T(8,128)(2,1)S(1)} fusion(bf16[512,2048]{1,0:T(8,128)(2,1)} %all-gather.6.cloned.1.call-done, bf16[2048,1024]{1,0:T(8,128)(2,1)} %bitcast.113), kind=kOutput, calls=%fused_computation.49 | convolution fusion | flops 2148007936 | bytes 7340032 | tf_op jit(solution)/shard_map/dot_general | solution.py:160
  (120 shorter events, 82.7 us)
Async XLA Ops:
  7.2 40.8 %all-gather.8.cloned.1.call-start = ((), (), s32[]{:S(2)}) async-start(), calls=%async_computation.10 | async-start | bytes 1474560 | tf_op jit(solution)/shard_map/all_gather | solution.py:71
  17.8 41.3 %all-to-all-start = ((bf16[8,64,2048]{2,1,0:T(8,128)(2,1)}), bf16[8,64,2048]{2,1,0:T(8,128)(2,1)}, u32[]{:S(2)}, u32[]{:S(2)}) async-start(bf16[8,64,2048]{2,1,0:T(8,128)(2,1)} %bitcast.2), calls=%async_computation | async-start | bytes 4194304 | tf_op jit(solution)/shard_map/all_to_all | solution.py:111
  59.1 5.3 %copy-start.7 = (f32[1,16,12]{1,0,2:T(1,128)S(1)}, f32[1,16,12]{1,0,2:T(1,128)}, u32[]{:S(2)}) copy-start(f32[1,16,12]{1,0,2:T(1,128)} %param.23) | copy-start | bytes 2308
  59.1 42.5 %all-to-all-start.1 = ((bf16[8,192,1024]{2,1,0:T(8,128)(2,1)}), bf16[8,192,1024]{2,1,0:T(8,128)(2,1)}, u32[]{:S(2)}, u32[]{:S(2)}) async-start(bf16[8,192,1024]{2,1,0:T(8,128)(2,1)} %bitcast.10), calls=%async_computation.1 | async-start | bytes 6291456 | tf_op jit(solution)/shard_map/all_to_all | solution.py:111
  63.7 29.9 %all-gather.10.cloned.1.call-start = ((), (), s32[]{:S(2)}) async-start(), calls=%async_computation.11 | async-start | bytes 1310720 | tf_op jit(solution)/shard_map/all_gather | solution.py:72
  101.6 43.1 %all-to-all-start.2 = ((bf16[8,192,1024]{2,1,0:T(8,128)(2,1)}), bf16[8,192,1024]{2,1,0:T(8,128)(2,1)}, u32[]{:S(2)}, u32[]{:S(2)}) async-start(bf16[8,192,1024]{2,1,0:T(8,128)(2,1)} %bitcast.16), calls=%async_computation.2 | async-start | bytes 6291456 | tf_op jit(solution)/shard_map/all_to_all | solution.py:111
  106.6 8.8 %copy-start.8 = (f32[1,6,16]{2,0,1:T(1,128)S(1)}, f32[1,6,16]{2,0,1:T(1,128)}, u32[]{:S(2)}) copy-start(f32[1,6,16]{2,0,1:T(1,128)} %param.25) | copy-start | bytes 1156
  120.1 15.2 %copy-start.2 = (bf16[2048,1536]{0,1:T(8,128)(2,1)}, bf16[2048,1536]{0,1:T(8,128)(2,1)S(1)}, u32[]{:S(2)}) copy-start(bf16[2048,1536]{0,1:T(8,128)(2,1)S(1)} %fusion) | copy-start | bytes 18874372
  120.1 4.1 copy-start.4
  166.6 5.7 %copy-start.5 = (bf16[768,2048]{1,0:T(8,128)(2,1)S(1)}, bf16[768,2048]{1,0:T(8,128)(2,1)}, u32[]{:S(2)}) copy-start(bf16[768,2048]{1,0:T(8,128)(2,1)} %fusion.2) | copy-start | bytes 9437188
  172.3 5.2 %copy-start.6 = (bf16[2048,768]{1,0:T(8,128)(2,1)}, bf16[2048,768]{1,0:T(8,128)(2,1)S(1)}, u32[]{:S(2)}) copy-start(bf16[2048,768]{1,0:T(8,128)(2,1)S(1)} %fusion.3) | copy-start | bytes 9437188
  177.5 53.7 %all-to-all-start.4 = ((bf16[8,256,1024]{2,1,0:T(8,128)(2,1)}), bf16[8,256,1024]{2,1,0:T(8,128)(2,1)}, u32[]{:S(2)}, u32[]{:S(2)}) async-start(bf16[8,256,1024]{2,1,0:T(8,128)(2,1)} %bitcast.114), calls=%async_computation.5 | async-start | bytes 8388608 | tf_op jit(solution)/shard_map/all_to_all | solution.py:111
  231.1 53.7 %all-to-all-start.3 = ((bf16[8,256,1024]{2,1,0:T(8,128)(2,1)}), bf16[8,256,1024]{2,1,0:T(8,128)(2,1)}, u32[]{:S(2)}, u32[]{:S(2)}) async-start(bf16[8,256,1024]{2,1,0:T(8,128)(2,1)} %bitcast.112), calls=%async_computation.3 | async-start | bytes 8388608 | tf_op jit(solution)/shard_map/all_to_all | solution.py:111
  235.7 112.6 %reduce-scatter.3.cloned.1.call-start = ((), (), s32[]{:S(2)}) async-start(), calls=%async_computation.7 | async-start | bytes 2621440 | tf_op jit(solution)/shard_map/reduce_scatter | solution.py:153
  292.3 4.6 copy-start
  299.0 3.7 copy-start.1
  307.0 1.0 copy-start.3
  307.0 86.8 %reduce-scatter.5.cloned.1.call-start = ((), (), s32[]{:S(2)}) async-start(), calls=%async_computation.8 | async-start | bytes 2621440 | tf_op jit(solution)/shard_map/reduce_scatter | solution.py:153
  307.6 133.9 %all-gather.6.cloned.1.call-start = ((), (), s32[]{:S(2)}) async-start(), calls=%async_computation.9 | async-start | bytes 2621440 | tf_op jit(solution)/shard_map/all_gather | solution.py:161
  396.0 5.4 %copy-start.10 = (s32[21]{0:T(128)S(1)}, s32[21]{0:T(128)}, u32[]{:S(2)}) copy-start(s32[21]{0:T(128)} %param.29) | copy-start | bytes 256
  396.0 5.4 %copy-start.9 = (s32[1,2,256]{2,1,0:T(2,128)S(1)}, s32[1,2,256]{2,1,0:T(2,128)}, u32[]{:S(2)}) copy-start(s32[1,2,256]{2,1,0:T(2,128)} %param.28) | copy-start | bytes 6148
  446.6 1.0 copy-start.11
  451.3 3.6 collective-permute-start
  455.0 4.4 collective-permute-start.1
Sparse Core Ops, SparseCore 0:
  14.8 33.1 all-gather.7
  66.1 27.4 all-gather.9
  307.1 41.1 reduce-scatter.2
  350.6 43.1 reduce-scatter.4
  396.1 45.2 all-gather.5

commit v9 on v8

--- a/solution.py
+++ b/solution.py
@@ -140,20 +140,24 @@
         jnp.bfloat16
     )
     mixed_parts = []
+    scattered = None
     for h in range(2):
         output = jnp.dot(
             hidden, down_proj[:, h * half : (h + 1) * half], preferred_element_type=jnp.float32
         ).astype(jnp.bfloat16)
+        if scattered is not None:
+            scattered, output = lax.optimization_barrier((scattered, output))
         back = send(output, cap)
         back = back.reshape(plane, lines, most, half)
         partial = jnp.einsum(
             "bpsr,pbsd->brd", weight_hi, back, preferred_element_type=jnp.float32
         ) + jnp.einsum("bpsr,pbsd->brd", weight_lo, back, preferred_element_type=jnp.float32)
         partial = jnp.take(partial, (jnp.arange(lines, dtype=jnp.int32) - here) % lines, axis=0)
-        combined = lax.psum_scatter(
-            partial.reshape(lines * rows, half), "tensor", scatter_dimension=0, tiled=True
-        )
-        mixed_parts.append(x_float[:, h * half : (h + 1) * half] + combined)
+        scattered = partial.reshape(lines * rows, half)
+        mixed_parts.append(scattered)
+    for h in range(2):
+        combined = lax.psum_scatter(mixed_parts[h], "tensor", scatter_dimension=0, tiled=True)
+        mixed_parts[h] = x_float[:, h * half : (h + 1) * half] + combined
     mixed = jnp.concatenate(mixed_parts, axis=1).astype(jnp.bfloat16)
 
     local_sync = w_sync.reshape(width, -1)

time: 476 us -> 437 us (0.918); the launches traced: 467 us -> 434 us
  waiting for transfers between devices: 270 us -> 228 us
  starting transfers between devices: 25.6 us -> 37 us
    reduce_scatter x2, waiting for transfers between devices: 85.7 us -> 41.2 us  [shards(): lax.psum_scatter(mixed_parts[h], 'tensor', scatter_dimension=0, tiled=True)]
    all_to_all x5, starting transfers between devices: 23.8 us -> 35.5 us  [send(): lax.all_to_all(part.reshape(plane, depth, part.shape[-1]), group, split_a...]
    unnamed x34 -> x30, local copies, waits for them, and re-layouts: 17.7 us -> 17.6 us
  transfers between devices with their start and end apart: 12 -> 12, of which waited for: 10 -> 9; matrix products, arithmetic and copies ran while one was open for 17% -> 20% of each run, Pallas kernels for 0% -> 0%
where the time goes in v9:
time: 437 us; the launch traced here: 434 us
  waiting for transfers between devices  228 us (52%)
  matrix products  67.3 us (15%)
  other arithmetic  50.7 us (12%)
  starting transfers between devices  37 us (8%)
  local copies, waits for them, and re-layouts  36.1 us (8%)
  between operations  14.5 us (3%)
    all_to_all x5, waiting for transfers between devices, send(): lax.all_to_all(part.reshape(plane, depth, part.shape[-1]), group, split_a...  84.7 us
    reduce_scatter x2, waiting for transfers between devices, shards(): lax.psum_scatter(mixed_parts[h], 'tensor', scatter_dimension=0, tiled=True)  41.2 us
    all_gather x1, waiting for transfers between devices, shards(): lax.all_gather(mixed, 'tensor', axis=0, tiled=True)  40 us
    all_to_all x5, starting transfers between devices, send(): lax.all_to_all(part.reshape(plane, depth, part.shape[-1]), group, split_a...  35.5 us
    all_gather x1, waiting for transfers between devices, shards(): line_b = lax.all_gather(normed[:, half:], 'tensor', axis=0, tiled=False)  29.2 us
    all_gather x1, waiting for transfers between devices, shards(): line_a = lax.all_gather(packed, 'tensor', axis=0, tiled=False)  24.9 us
    unnamed x30, local copies, waits for them, and re-layouts  17.6 us
    dot_general x2, matrix products, shards(): jnp.dot(hidden, down_proj[:, h * half:(h + 1) * half], preferred_element_...  12.8 us
  transfers between devices with their start and end apart: 12, of which 9 were waited for; matrix products, arithmetic and copies ran while one was open for 20% of the time, Pallas kernels for 0%

profile of v9, /device:TPU:0, one launch (start us, length us, event | category | flops | bytes accessed | tf_op | source)
XLA Modules:
  0.0 433.7 jit_solution(14115672975125255759)
XLA Ops:
  17.8 5.2 %all-to-all-start = ((bf16[8,64,2048]{2,1,0:T(8,128)(2,1)}), bf16[8,64,2048]{2,1,0:T(8,128)(2,1)}, u32[]{:S(2)}, u32[]{:S(2)}) async-start(bf16[8,64,2048]{2,1,0:T(8,128)(2,1)} %bitcast.2), calls=%async_computation | async-start | bytes 4194304 | tf_op jit(solution)/shard_map/all_to_all | solution.py:111
  23.1 24.9 %all-gather.8.cloned.1.call-done = bf16[576,1024]{1,0:T(8,128)(2,1)} async-done(((bf16[144,1024]{1,0:T(8,128)(2,1)}), bf16[576,1024]{1,0:T(8,128)(2,1)}) %all-gather.8.cloned.1.call-update) | async-done | bytes 1179664 | tf_op jit(solution)/shard_map/all_gather | solution.py:71
  59.2 4.6 %all-to-all-start.1 = ((bf16[8,192,1024]{2,1,0:T(8,128)(2,1)}), bf16[8,192,1024]{2,1,0:T(8,128)(2,1)}, u32[]{:S(2)}, u32[]{:S(2)}) async-start(bf16[8,192,1024]{2,1,0:T(8,128)(2,1)} %bitcast.10), calls=%async_computation.1 | async-start | bytes 6291456 | tf_op jit(solution)/shard_map/all_to_all | solution.py:111
  64.5 29.2 %all-gather.10.cloned.1.call-done = bf16[512,1024]{1,0:T(8,128)(2,1)} async-done(((bf16[128,1024]{1,0:T(8,128)(2,1)}), bf16[512,1024]{1,0:T(8,128)(2,1)}) %all-gather.10.cloned.1.call-update) | async-done | bytes 1048592 | tf_op jit(solution)/shard_map/all_gather | solution.py:72
  101.7 16.2 %all-to-all-start.2 = ((bf16[8,192,1024]{2,1,0:T(8,128)(2,1)}), bf16[8,192,1024]{2,1,0:T(8,128)(2,1)}, u32[]{:S(2)}, u32[]{:S(2)}) async-start(bf16[8,192,1024]{2,1,0:T(8,128)(2,1)} %bitcast.16), calls=%async_computation.2 | async-start | bytes 6291456 | tf_op jit(solution)/shard_map/all_to_all | solution.py:111
  118.0 8.7 %copy.84 = bf16[1,2048,1536]{1,2,0:T(8,128)(2,1)} copy(bf16[1,2048,1536]{2,1,0:T(8,128)(2,1)} %param.22) | data formatting | bytes 12582912 | tf_op args[4]
  126.8 4.6 %fusion = bf16[2048,1536]{0,1:T(8,128)(2,1)S(1)} fusion(bf16[1,2048,1536]{1,2,0:T(8,128)(2,1)} %copy.84, f32[2048,12]{0,1:T(8,128)S(1)} %bitcast.122), kind=kLoop, calls=%fused_computation.9 | loop fusion | flops 9437184 | bytes 12681216 | tf_op jit(solution)/shard_map/convert_element_type | solution.py:10
  135.5 4.3 fusion.2
  139.8 6.8 %fusion.4 = f32[8,64,1536]{2,1,0:T(8,128)} fusion(bf16[8,64,2048]{2,1,0:T(8,128)(2,1)} %all-to-all-done, bf16[2048,1536]{0,1:T(8,128)(2,1)S(1)} %fusion), kind=kOutput, calls=%fused_computation.19 | convolution fusion | flops 3221225472 | bytes 11534336 | tf_op jit(solution)/shard_map/dot_general | solution.py:128
  146.6 9.5 %fusion.18 = f32[1536,1536]{1,0:T(8,128)} fusion(bf16[1536,1024]{1,0:T(8,128)(2,1)} %bitcast.11, bf16[2048,1536]{0,1:T(8,128)(2,1)S(1)} %fusion), kind=kOutput, calls=%fused_computation.36 | convolution fusion | flops 4831838208 | bytes 15728640 | tf_op jit(solution)/shard_map/dot_general | solution.py:129
  156.1 11.3 %convolution_add_fusion = f32[1536,1536]{1,0:T(8,128)} fusion(f32[1536,1536]{1,0:T(8,128)} %fusion.18, bf16[1536,1024]{1,0:T(8,128)(2,1)} %bitcast.17, bf16[2048,1536]{0,1:T(8,128)(2,1)} %copy-done), kind=kOutput, calls=%fused_computation.10 | convolution fusion | flops 4834197504 | bytes 25165824 | tf_op jit(solution)/shard_map/dot_general | solution.py:129
  167.4 10.4 %pad_maximum_fusion = f32[8,256,1536]{2,1,0:T(8,128)} fusion(f32[8,192,1536]{2,1,0:T(8,128)} %bitcast.108, f32[8,64,1536]{2,1,0:T(8,128)} %fusion.4), kind=kLoop, calls=%fused_computation.7 | loop fusion | flops 3145728 | bytes 25165824 | tf_op jit(solution)/shard_map/concatenate | solution.py:132
  177.7 5.7 %fusion.3 = bf16[2048,768]{1,0:T(8,128)(2,1)S(1)} fusion(f32[2048,1536]{1,0:T(8,128)} %bitcast.106), kind=kLoop, calls=%fused_computation.18 | loop fusion | flops 9437184 | bytes 15728640 | tf_op jit(solution)/shard_map/convert_element_type | solution.py:139
  183.4 5.1 %convolution_convert_fusion.1 = bf16[2048,1024]{1,0:T(8,128)(2,1)} fusion(bf16[2048,768]{1,0:T(8,128)(2,1)S(1)} %fusion.3, bf16[768,2048]{1,0:T(8,128)(2,1)S(1)} %copy-done.3), kind=kOutput, calls=%fused_computation.26 | convolution fusion | flops 3223322624 | bytes 8912896 | tf_op jit(solution)/shard_map/dot_general | solution.py:145
  188.5 5.0 %all-to-all-start.3 = ((bf16[8,256,1024]{2,1,0:T(8,128)(2,1)}), bf16[8,256,1024]{2,1,0:T(8,128)(2,1)}, u32[]{:S(2)}, u32[]{:S(2)}) async-start(bf16[8,256,1024]{2,1,0:T(8,128)(2,1)} %bitcast.112), calls=%async_computation.3 | async-start | bytes 8388608 | tf_op jit(solution)/shard_map/all_to_all | solution.py:111
  193.9 6.0 %select_reduce_fusion.1 = (bf16[4,512,128]{2,1,0:T(8,128)(2,1)S(1)}, bf16[4,512,128]{2,1,0:T(8,128)(2,1)S(1)}) fusion(f32[4,128,8]{1,2,0:T(8,128)S(1)} %convert_element_type.141, s32[4,128,8]{1,2,0:T(8,128)S(1)} %copy.77, f32[4,128,8]{1,2,0:T(8,128)S(1)} %convert_element_type.161), kind=kLoop, calls=%fused_computation.12 | loop fusion | flops 9961472 | bytes 1097728 | tf_op jit(solution)/shard_map/reduce_sum | solution.py:85
  201.2 7.7 %convolution_convert_fusion = bf16[2048,1024]{1,0:T(8,128)(2,1)} fusion(bf16[2048,768]{1,0:T(8,128)(2,1)} %copy-done.4, bf16[768,2048]{1,0:T(8,128)(2,1)} %fusion.2), kind=kOutput, calls=%fused_computation.25 | convolution fusion | flops 3223322624 | bytes 8912896 | tf_op jit(solution)/shard_map/dot_general | solution.py:145
  209.0 33.6 %all-to-all-done.3 = bf16[8,256,1024]{2,1,0:T(8,128)(2,1)} async-done(((bf16[8,256,1024]{2,1,0:T(8,128)(2,1)}), bf16[8,256,1024]{2,1,0:T(8,128)(2,1)}, u32[]{:S(2)}, u32[]{:S(2)}) %all-to-all-start.3) | async-done | bytes 4194336 | tf_op jit(solution)/shard_map/all_to_all | solution.py:111
  254.3 4.5 %all-to-all-start.4 = ((bf16[8,256,1024]{2,1,0:T(8,128)(2,1)}), bf16[8,256,1024]{2,1,0:T(8,128)(2,1)}, u32[]{:S(2)}, u32[]{:S(2)}) async-start(bf16[8,256,1024]{2,1,0:T(8,128)(2,1)} %bitcast.113), calls=%async_computation.5 | async-start | bytes 8388608 | tf_op jit(solution)/shard_map/all_to_all | solution.py:111
  259.8 48.2 %all-to-all-done.4 = bf16[8,256,1024]{2,1,0:T(8,128)(2,1)} async-done(((bf16[8,256,1024]{2,1,0:T(8,128)(2,1)}), bf16[8,256,1024]{2,1,0:T(8,128)(2,1)}, u32[]{:S(2)}, u32[]{:S(2)}) %all-to-all-start.4) | async-done | bytes 4194336 | tf_op jit(solution)/shard_map/all_to_all | solution.py:111
  319.8 41.1 %reduce-scatter.5.cloned.1.call-done = f32[128,1024]{1,0:T(8,128)} async-done(((f32[512,1024]{1,0:T(8,128)}), f32[128,1024]{1,0:T(8,128)}) %reduce-scatter.5.cloned.1.call-update) | async-done | bytes 524304 | tf_op jit(solution)/shard_map/reduce_scatter | solution.py:159
  363.1 5.3 %copy.112 = bf16[256,8,2,512]{3,1,2,0:T(8,128)(2,1)} copy(bf16[256,8,2,512]{3,2,1,0:T(2,128)(2,1)} %bitcast.111) | data formatting | bytes 8388608
  368.5 40.0 %all-gather.6.cloned.1.call-done = bf16[512,2048]{1,0:T(8,128)(2,1)} async-done(((bf16[128,2048]{1,0:T(8,128)(2,1)}), bf16[512,2048]{1,0:T(8,128)(2,1)}) %all-gather.6.cloned.1.call-update) | async-done | bytes 2097168 | tf_op jit(solution)/shard_map/all_gather | solution.py:165
  408.5 5.1 %convolution_convert_fusion.3 = bf16[512,1024]{1,0:T(8,128)(2,1)S(1)} fusion(bf16[512,2048]{1,0:T(8,128)(2,1)} %all-gather.6.cloned.1.call-done, bf16[2048,1024]{1,0:T(8,128)(2,1)} %bitcast.114), kind=kOutput, calls=%fused_computation.49 | convolution fusion | flops 2148007936 | bytes 7340032 | tf_op jit(solution)/shard_map/dot_general | solution.py:164
  (117 shorter events, 76.4 us)
Async XLA Ops:
  7.2 40.8 %all-gather.8.cloned.1.call-start = ((), (), s32[]{:S(2)}) async-start(), calls=%async_computation.10 | async-start | bytes 1474560 | tf_op jit(solution)/shard_map/all_gather | solution.py:71
  17.8 41.3 %all-to-all-start = ((bf16[8,64,2048]{2,1,0:T(8,128)(2,1)}), bf16[8,64,2048]{2,1,0:T(8,128)(2,1)}, u32[]{:S(2)}, u32[]{:S(2)}) async-start(bf16[8,64,2048]{2,1,0:T(8,128)(2,1)} %bitcast.2), calls=%async_computation | async-start | bytes 4194304 | tf_op jit(solution)/shard_map/all_to_all | solution.py:111
  59.2 5.4 %copy-start.5 = (f32[1,16,12]{1,0,2:T(1,128)S(1)}, f32[1,16,12]{1,0,2:T(1,128)}, u32[]{:S(2)}) copy-start(f32[1,16,12]{1,0,2:T(1,128)} %param.23) | copy-start | bytes 2308
  59.2 42.5 %all-to-all-start.1 = ((bf16[8,192,1024]{2,1,0:T(8,128)(2,1)}), bf16[8,192,1024]{2,1,0:T(8,128)(2,1)}, u32[]{:S(2)}, u32[]{:S(2)}) async-start(bf16[8,192,1024]{2,1,0:T(8,128)(2,1)} %bitcast.10), calls=%async_computation.1 | async-start | bytes 6291456 | tf_op jit(solution)/shard_map/all_to_all | solution.py:111
  63.8 29.9 %all-gather.10.cloned.1.call-start = ((), (), s32[]{:S(2)}) async-start(), calls=%async_computation.11 | async-start | bytes 1310720 | tf_op jit(solution)/shard_map/all_gather | solution.py:72
  101.7 54.4 %all-to-all-start.2 = ((bf16[8,192,1024]{2,1,0:T(8,128)(2,1)}), bf16[8,192,1024]{2,1,0:T(8,128)(2,1)}, u32[]{:S(2)}, u32[]{:S(2)}) async-start(bf16[8,192,1024]{2,1,0:T(8,128)(2,1)} %bitcast.16), calls=%async_computation.2 | async-start | bytes 6291456 | tf_op jit(solution)/shard_map/all_to_all | solution.py:111
  117.9 8.8 %copy-start.6 = (f32[1,6,16]{2,0,1:T(1,128)S(1)}, f32[1,6,16]{2,0,1:T(1,128)}, u32[]{:S(2)}) copy-start(f32[1,6,16]{2,0,1:T(1,128)} %param.25) | copy-start | bytes 1156
  131.3 15.2 %copy-start = (bf16[2048,1536]{0,1:T(8,128)(2,1)}, bf16[2048,1536]{0,1:T(8,128)(2,1)S(1)}, u32[]{:S(2)}) copy-start(bf16[2048,1536]{0,1:T(8,128)(2,1)S(1)} %fusion) | copy-start | bytes 18874372
  131.4 4.1 copy-start.2
  177.7 5.7 %copy-start.3 = (bf16[768,2048]{1,0:T(8,128)(2,1)S(1)}, bf16[768,2048]{1,0:T(8,128)(2,1)}, u32[]{:S(2)}) copy-start(bf16[768,2048]{1,0:T(8,128)(2,1)} %fusion.2) | copy-start | bytes 9437188
  183.4 5.1 %copy-start.4 = (bf16[2048,768]{1,0:T(8,128)(2,1)}, bf16[2048,768]{1,0:T(8,128)(2,1)S(1)}, u32[]{:S(2)}) copy-start(bf16[2048,768]{1,0:T(8,128)(2,1)S(1)} %fusion.3) | copy-start | bytes 9437188
  188.5 54.1 %all-to-all-start.3 = ((bf16[8,256,1024]{2,1,0:T(8,128)(2,1)}), bf16[8,256,1024]{2,1,0:T(8,128)(2,1)}, u32[]{:S(2)}, u32[]{:S(2)}) async-start(bf16[8,256,1024]{2,1,0:T(8,128)(2,1)} %bitcast.112), calls=%async_computation.3 | async-start | bytes 8388608 | tf_op jit(solution)/shard_map/all_to_all | solution.py:111
  254.3 53.7 %all-to-all-start.4 = ((bf16[8,256,1024]{2,1,0:T(8,128)(2,1)}), bf16[8,256,1024]{2,1,0:T(8,128)(2,1)}, u32[]{:S(2)}, u32[]{:S(2)}) async-start(bf16[8,256,1024]{2,1,0:T(8,128)(2,1)} %bitcast.113), calls=%async_computation.5 | async-start | bytes 8388608 | tf_op jit(solution)/shard_map/all_to_all | solution.py:111
  258.8 61.0 %reduce-scatter.3.cloned.1.call-start = ((), (), s32[]{:S(2)}) async-start(), calls=%async_computation.7 | async-start | bytes 2621440 | tf_op jit(solution)/shard_map/reduce_scatter | solution.py:159
  259.5 101.4 %reduce-scatter.5.cloned.1.call-start = ((), (), s32[]{:S(2)}) async-start(), calls=%async_computation.8 | async-start | bytes 2621440 | tf_op jit(solution)/shard_map/reduce_scatter | solution.py:159
  316.1 3.5 copy-start.1
  319.6 89.0 %all-gather.6.cloned.1.call-start = ((), (), s32[]{:S(2)}) async-start(), calls=%async_computation.9 | async-start | bytes 2621440 | tf_op jit(solution)/shard_map/all_gather | solution.py:165
  363.1 5.4 %copy-start.8 = (s32[21]{0:T(128)S(1)}, s32[21]{0:T(128)}, u32[]{:S(2)}) copy-start(s32[21]{0:T(128)} %param.29) | copy-start | bytes 256
  363.1 5.4 %copy-start.7 = (s32[1,2,256]{2,1,0:T(2,128)S(1)}, s32[1,2,256]{2,1,0:T(2,128)}, u32[]{:S(2)}) copy-start(s32[1,2,256]{2,1,0:T(2,128)} %param.28) | copy-start | bytes 6148
  413.7 1.0 copy-start.9
  418.5 3.6 collective-permute-start
  422.1 4.4 %collective-permute-start.1 = (f32[21]{0:T(128)S(1)}, f32[21]{0:T(128)S(1)}, u32[]{:S(2)}, u32[]{:S(2)}) collective-permute-start(f32[21]{0:T(128)S(1)} %add.108), channel_id=1, source_target_pairs={{0,2},{1,3},{2,0},{3,1},{4,6},{5,7},{6,4},{7,5},{8,10},{9,11},{10,... | collective-permute-start | bytes 260 | tf_op jit(solution)/shard_map/ppermute | solution.py:209
Sparse Core Ops, SparseCore 0:
  14.8 33.1 all-gather.7
  66.2 27.4 all-gather.9
  261.9 43.3 reduce-scatter.2
  319.7 41.1 reduce-scatter.4
  363.2 45.2 all-gather.5

commit v10 on v9

--- a/solution.py
+++ b/solution.py
@@ -125,20 +125,23 @@
         )
         for h in range(2)
     ]
-    own_in = jnp.dot(own_block, gate_up, preferred_element_type=jnp.float32)
-    mixed_in = jnp.dot(blocks[0], gate_up[:half], preferred_element_type=jnp.float32) + jnp.dot(
-        blocks[1], gate_up[half:], preferred_element_type=jnp.float32
-    )
-    mixed_in = jnp.concatenate(
+    def activate(mixed_in):
+        return (jax.nn.silu(mixed_in[:, :hidden_width]) * mixed_in[:, hidden_width:]).astype(
+            jnp.bfloat16
+        )
+
+    own_hidden = activate(jnp.dot(own_block, gate_up, preferred_element_type=jnp.float32))
+    rest_hidden = activate(
+        jnp.dot(blocks[0], gate_up[:half], preferred_element_type=jnp.float32)
+        + jnp.dot(blocks[1], gate_up[half:], preferred_element_type=jnp.float32)
+    )
+    hidden = jnp.concatenate(
         [
-            own_in.reshape(plane, most, -1),
-            mixed_in.reshape(plane, cap - most, -1),
+            own_hidden.reshape(plane, most, hidden_width),
+            rest_hidden.reshape(plane, cap - most, hidden_width),
         ],
         axis=1,
-    ).reshape(plane * cap, -1)
-    hidden = (jax.nn.silu(mixed_in[:, :hidden_width]) * mixed_in[:, hidden_width:]).astype(
-        jnp.bfloat16
-    )
+    ).reshape(plane * cap, hidden_width)
     mixed_parts = []
     scattered = None
     for h in range(2):

time: 437 us -> 420 us (0.961)
  waiting for transfers between devices: 228 us -> 218 us
  other arithmetic: 50.7 us -> 45 us
    all_gather x1, waiting for transfers between devices: 29.2 us -> 6.01 us  [shards(): line_b = lax.all_gather(normed[:, half:], 'tensor', axis=0, tiled=False)]
    all_to_all x5, waiting for transfers between devices: 84.7 us -> 98.4 us  [send(): lax.all_to_all(part.reshape(plane, depth, part.shape[-1]), group, split_a...]
    all_to_all x5, starting transfers between devices: 35.5 us -> 23.2 us  [send(): lax.all_to_all(part.reshape(plane, depth, part.shape[-1]), group, split_a...]
    all_gather x1, starting transfers between devices: 0.04 us -> 12.1 us  [shards(): line_b = lax.all_gather(normed[:, half:], 'tensor', axis=0, tiled=False)]
    concatenate x1, other arithmetic: 10.4 us -> 0.21 us  [shards(): jnp.concatenate([own_hidden.reshape(plane, most, hidden_width), rest_hidd...]
    convert_element_type x2 -> x3, other arithmetic: 8.82 us -> 16.5 us  [dequant(): return (weights.astype(jnp.float32) * full).astype(jnp.bfloat16)]
    unnamed x30 -> x40, local copies, waits for them, and re-layouts: 17.6 us -> 18.1 us
  transfers between devices with their start and end apart: 12 -> 12, of which waited for: 9 -> 9; matrix products, arithmetic and copies ran while one was open for 20% -> 23% of each run, Pallas kernels for 0% -> 0%
where the time goes in v10:
time: 420 us; the launch traced here: 415 us
  waiting for transfers between devices  218 us (52%)
  matrix products  63.7 us (15%)
  other arithmetic  45 us (11%)
  starting transfers between devices  36.8 us (9%)
  local copies, waits for them, and re-layouts  36.6 us (9%)
  between operations  14.6 us (3%)
    all_to_all x5, waiting for transfers between devices, send(): lax.all_to_all(part.reshape(plane, depth, part.shape[-1]), group, split_a...  98.4 us
    reduce_scatter x2, waiting for transfers between devices, shards(): lax.psum_scatter(mixed_parts[h], 'tensor', scatter_dimension=0, tiled=True)  41.6 us
    all_gather x1, waiting for transfers between devices, shards(): lax.all_gather(mixed, 'tensor', axis=0, tiled=True)  40 us
    all_gather x1, waiting for transfers between devices, shards(): line_a = lax.all_gather(packed, 'tensor', axis=0, tiled=False)  24.9 us
    all_to_all x5, starting transfers between devices, send(): lax.all_to_all(part.reshape(plane, depth, part.shape[-1]), group, split_a...  23.2 us
    unnamed x40, local copies, waits for them, and re-layouts  18.1 us
    convert_element_type x3, other arithmetic, dequant(): return (weights.astype(jnp.float32) * full).astype(jnp.bfloat16)  16.5 us
    dot_general x2, matrix products, shards(): jnp.dot(hidden, down_proj[:, h * half:(h + 1) * half], preferred_element_...  12.8 us
  transfers between devices with their start and end apart: 12, of which 9 were waited for; matrix products, arithmetic and copies ran while one was open for 23% of the time, Pallas kernels for 0%

profile of v10, /device:TPU:0, one launch (start us, length us, event | category | flops | bytes accessed | tf_op | source)
XLA Modules:
  0.0 415.1 jit_solution(12202414387706838252)
XLA Ops:
  17.8 5.2 %all-to-all-start = ((bf16[8,64,2048]{2,1,0:T(8,128)(2,1)}), bf16[8,64,2048]{2,1,0:T(8,128)(2,1)}, u32[]{:S(2)}, u32[]{:S(2)}) async-start(bf16[8,64,2048]{2,1,0:T(8,128)(2,1)} %bitcast.2), calls=%async_computation | async-start | bytes 4194304 | tf_op jit(solution)/shard_map/all_to_all | solution.py:111
  23.1 24.9 %all-gather.8.cloned.1.call-done = bf16[576,1024]{1,0:T(8,128)(2,1)} async-done(((bf16[144,1024]{1,0:T(8,128)(2,1)}), bf16[576,1024]{1,0:T(8,128)(2,1)}) %all-gather.8.cloned.1.call-update) | async-done | bytes 1179664 | tf_op jit(solution)/shard_map/all_gather | solution.py:71
  59.2 4.4 %all-to-all-start.1 = ((bf16[8,192,1024]{2,1,0:T(8,128)(2,1)}), bf16[8,192,1024]{2,1,0:T(8,128)(2,1)}, u32[]{:S(2)}, u32[]{:S(2)}) async-start(bf16[8,192,1024]{2,1,0:T(8,128)(2,1)} %bitcast.11), calls=%async_computation.1 | async-start | bytes 6291456 | tf_op jit(solution)/shard_map/all_to_all | solution.py:111
  63.6 12.1 %all-gather.10.cloned.1.call-start = ((), (), s32[]{:S(2)}) async-start(), calls=%async_computation.11 | async-start | bytes 1310720 | tf_op jit(solution)/shard_map/all_gather | solution.py:72
  75.8 8.7 %copy.81 = bf16[1,2048,1536]{1,2,0:T(8,128)(2,1)} copy(bf16[1,2048,1536]{2,1,0:T(8,128)(2,1)} %param.22) | data formatting | bytes 12582912 | tf_op args[4]
  84.8 7.8 %fusion = bf16[2048,1536]{0,1:T(8,128)(2,1)} fusion(f32[2048,12]{0,1:T(8,128)S(1)} %bitcast.133, bf16[1,2048,1536]{1,2,0:T(8,128)(2,1)} %copy.81), kind=kLoop, calls=%fused_computation.8 | loop fusion | flops 9437184 | bytes 12681216 | tf_op jit(solution)/shard_map/convert_element_type | solution.py:10
  92.6 4.5 %multiply_convert_fusion = bf16[2048,12,128]{0,2,1:T(8,128)(2,1)} fusion(f32[2048,12]{0,1:T(8,128)S(1)} %bitcast.134, bf16[2048,12,128]{0,2,1:T(8,128)(2,1)S(1)} %bitcast.112), kind=kLoop, calls=%fused_computation.9 | loop fusion | flops 9437184 | bytes 12681216 | tf_op jit(solution)/shard_map/convert_element_type | solution.py:10
  97.1 6.0 %all-gather.10.cloned.1.call-done = bf16[512,1024]{1,0:T(8,128)(2,1)} async-done(((bf16[128,1024]{1,0:T(8,128)(2,1)}), bf16[512,1024]{1,0:T(8,128)(2,1)}) %all-gather.10.cloned.1.call-update) | async-done | bytes 1048592 | tf_op jit(solution)/shard_map/all_gather | solution.py:72
  108.2 4.4 %all-to-all-start.2 = ((bf16[8,192,1024]{2,1,0:T(8,128)(2,1)}), bf16[8,192,1024]{2,1,0:T(8,128)(2,1)}, u32[]{:S(2)}, u32[]{:S(2)}) async-start(bf16[8,192,1024]{2,1,0:T(8,128)(2,1)} %bitcast.19), calls=%async_computation.2 | async-start | bytes 6291456 | tf_op jit(solution)/shard_map/all_to_all | solution.py:111
  118.7 5.2 %fusion.94 = f32[512,1536]{1,0:T(8,128)S(1)} fusion(bf16[512,2048]{1,0:T(8,128)(2,1)} %bitcast.3, bf16[2048,1536]{0,1:T(8,128)(2,1)S(1)} %bitcast.121), kind=kOutput, calls=%fused_computation.164 | convolution fusion | flops 3221225472 | bytes 11534336 | tf_op jit(solution)/shard_map/dot_general | solution.py:133
  124.3 9.6 %fusion.16 = f32[1536,1536]{1,0:T(8,128)} fusion(bf16[1536,1024]{1,0:T(8,128)(2,1)} %bitcast.12, bf16[2048,1536]{0,1:T(8,128)(2,1)S(1)} %bitcast.118), kind=kOutput, calls=%fused_computation.34 | convolution fusion | flops 4831838208 | bytes 15728640 | tf_op jit(solution)/shard_map/dot_general | solution.py:135
  133.9 16.6 %all-to-all-done.2 = bf16[8,192,1024]{2,1,0:T(8,128)(2,1)} async-done(((bf16[8,192,1024]{2,1,0:T(8,128)(2,1)}), bf16[8,192,1024]{2,1,0:T(8,128)(2,1)}, u32[]{:S(2)}, u32[]{:S(2)}) %all-to-all-start.2) | async-done | bytes 3145760 | tf_op jit(solution)/shard_map/all_to_all | solution.py:111
  150.5 9.3 %convolution_add_fusion = f32[1536,1536]{1,0:T(8,128)S(1)} fusion(f32[1536,1536]{1,0:T(8,128)} %fusion.16, bf16[1536,1024]{1,0:T(8,128)(2,1)} %bitcast.20, bf16[2048,1536]{0,1:T(8,128)(2,1)} %fusion), kind=kOutput, calls=%fused_computation.10 | convolution fusion | flops 4834197504 | bytes 25165824 | tf_op jit(solution)/shard_map/dot_general | solution.py:136
  164.8 5.1 %convolution_convert_fusion.1 = bf16[2048,1024]{1,0:T(8,128)(2,1)} fusion(bf16[2048,768]{1,0:T(8,128)(2,1)S(1)} %bitcast.126, bf16[768,2048]{1,0:T(8,128)(2,1)S(1)} %copy-done.3), kind=kOutput, calls=%fused_computation.24 | convolution fusion | flops 3223322624 | bytes 8912896 | tf_op jit(solution)/shard_map/dot_general | solution.py:148
  169.8 4.6 %all-to-all-start.3 = ((bf16[8,256,1024]{2,1,0:T(8,128)(2,1)}), bf16[8,256,1024]{2,1,0:T(8,128)(2,1)}, u32[]{:S(2)}, u32[]{:S(2)}) async-start(bf16[8,256,1024]{2,1,0:T(8,128)(2,1)} %bitcast.123), calls=%async_computation.3 | async-start | bytes 8388608 | tf_op jit(solution)/shard_map/all_to_all | solution.py:111
  174.8 6.0 %select_reduce_fusion.1 = (bf16[4,512,128]{2,1,0:T(8,128)(2,1)S(1)}, bf16[4,512,128]{2,1,0:T(8,128)(2,1)S(1)}) fusion(f32[4,128,8]{1,2,0:T(8,128)S(1)} %convert_element_type.163, s32[4,128,8]{1,2,0:T(8,128)S(1)} %copy.74, f32[4,128,8]{1,2,0:T(8,128)S(1)} %convert_element_type.188), kind=kLoop, calls=%fused_computation.12 | loop fusion | flops 9961472 | bytes 1097728 | tf_op jit(solution)/shard_map/reduce_sum | solution.py:85
  182.1 7.7 %convolution_convert_fusion = bf16[2048,1024]{1,0:T(8,128)(2,1)} fusion(bf16[2048,768]{1,0:T(8,128)(2,1)} %bitcast.127, bf16[768,2048]{1,0:T(8,128)(2,1)} %fusion.2), kind=kOutput, calls=%fused_computation.23 | convolution fusion | flops 3223322624 | bytes 8912896 | tf_op jit(solution)/shard_map/dot_general | solution.py:148
  189.9 33.6 %all-to-all-done.3 = bf16[8,256,1024]{2,1,0:T(8,128)(2,1)} async-done(((bf16[8,256,1024]{2,1,0:T(8,128)(2,1)}), bf16[8,256,1024]{2,1,0:T(8,128)(2,1)}, u32[]{:S(2)}, u32[]{:S(2)}) %all-to-all-start.3) | async-done | bytes 4194336 | tf_op jit(solution)/shard_map/all_to_all | solution.py:111
  235.1 4.6 %all-to-all-start.4 = ((bf16[8,256,1024]{2,1,0:T(8,128)(2,1)}), bf16[8,256,1024]{2,1,0:T(8,128)(2,1)}, u32[]{:S(2)}, u32[]{:S(2)}) async-start(bf16[8,256,1024]{2,1,0:T(8,128)(2,1)} %bitcast.124), calls=%async_computation.5 | async-start | bytes 8388608 | tf_op jit(solution)/shard_map/all_to_all | solution.py:111
  240.7 48.2 %all-to-all-done.4 = bf16[8,256,1024]{2,1,0:T(8,128)(2,1)} async-done(((bf16[8,256,1024]{2,1,0:T(8,128)(2,1)}), bf16[8,256,1024]{2,1,0:T(8,128)(2,1)}, u32[]{:S(2)}, u32[]{:S(2)}) %all-to-all-start.4) | async-done | bytes 4194336 | tf_op jit(solution)/shard_map/all_to_all | solution.py:111
  300.7 41.5 %reduce-scatter.5.cloned.1.call-done = f32[128,1024]{1,0:T(8,128)} async-done(((f32[512,1024]{1,0:T(8,128)}), f32[128,1024]{1,0:T(8,128)}) %reduce-scatter.5.cloned.1.call-update) | async-done | bytes 524304 | tf_op jit(solution)/shard_map/reduce_scatter | solution.py:162
  344.4 5.3 %copy.106 = bf16[256,8,2,512]{3,1,2,0:T(8,128)(2,1)} copy(bf16[256,8,2,512]{3,2,1,0:T(2,128)(2,1)} %bitcast.122) | data formatting | bytes 8388608
  349.9 40.0 %all-gather.6.cloned.1.call-done = bf16[512,2048]{1,0:T(8,128)(2,1)} async-done(((bf16[128,2048]{1,0:T(8,128)(2,1)}), bf16[512,2048]{1,0:T(8,128)(2,1)}) %all-gather.6.cloned.1.call-update) | async-done | bytes 2097168 | tf_op jit(solution)/shard_map/all_gather | solution.py:168
  389.9 5.2 %convolution_convert_fusion.3 = bf16[512,1024]{1,0:T(8,128)(2,1)S(1)} fusion(bf16[512,2048]{1,0:T(8,128)(2,1)} %all-gather.6.cloned.1.call-done, bf16[2048,1024]{1,0:T(8,128)(2,1)} %bitcast.125), kind=kOutput, calls=%fused_computation.50 | convolution fusion | flops 2148007936 | bytes 7340032 | tf_op jit(solution)/shard_map/dot_general | solution.py:167
  (132 shorter events, 80.0 us)
Async XLA Ops:
  7.2 40.8 %all-gather.8.cloned.1.call-start = ((), (), s32[]{:S(2)}) async-start(), calls=%async_computation.10 | async-start | bytes 1474560 | tf_op jit(solution)/shard_map/all_gather | solution.py:71
  17.8 41.4 %all-to-all-start = ((bf16[8,64,2048]{2,1,0:T(8,128)(2,1)}), bf16[8,64,2048]{2,1,0:T(8,128)(2,1)}, u32[]{:S(2)}, u32[]{:S(2)}) async-start(bf16[8,64,2048]{2,1,0:T(8,128)(2,1)} %bitcast.2), calls=%async_computation | async-start | bytes 4194304 | tf_op jit(solution)/shard_map/all_to_all | solution.py:111
  59.2 49.0 %all-to-all-start.1 = ((bf16[8,192,1024]{2,1,0:T(8,128)(2,1)}), bf16[8,192,1024]{2,1,0:T(8,128)(2,1)}, u32[]{:S(2)}, u32[]{:S(2)}) async-start(bf16[8,192,1024]{2,1,0:T(8,128)(2,1)} %bitcast.11), calls=%async_computation.1 | async-start | bytes 6291456 | tf_op jit(solution)/shard_map/all_to_all | solution.py:111
  63.6 39.5 %all-gather.10.cloned.1.call-start = ((), (), s32[]{:S(2)}) async-start(), calls=%async_computation.11 | async-start | bytes 1310720 | tf_op jit(solution)/shard_map/all_gather | solution.py:72
  75.8 8.8 %copy-start.4 = (f32[1,16,12]{1,0,2:T(1,128)S(1)}, f32[1,16,12]{1,0,2:T(1,128)}, u32[]{:S(2)}) copy-start(f32[1,16,12]{1,0,2:T(1,128)} %param.23) | copy-start | bytes 2308
  75.8 8.9 %copy-start.5 = (f32[1,6,16]{2,0,1:T(1,128)S(1)}, f32[1,6,16]{2,0,1:T(1,128)}, u32[]{:S(2)}) copy-start(f32[1,6,16]{2,0,1:T(1,128)} %param.25) | copy-start | bytes 1156
  84.7 7.9 %slice-start = ((s8[6291456]{0:T(1024)(128)(4,1)}), s8[4194304]{0:T(1024)(128)(4,1)S(1)}, s32[]{:S(2)}) async-start(s8[6291456]{0:T(1024)(128)(4,1)} %bitcast.110), calls=%async_computation.12 | async-start | bytes 8388608
  84.8 7.8 %slice-start.1 = ((s8[6291456]{0:T(1024)(128)(4,1)}), s8[2097152]{0:T(1024)(128)(4,1)S(1)}, s32[]{:S(2)}) async-start(s8[6291456]{0:T(1024)(128)(4,1)} %bitcast.110), calls=%async_computation.13 | async-start | bytes 4194304
  108.2 42.3 %all-to-all-start.2 = ((bf16[8,192,1024]{2,1,0:T(8,128)(2,1)}), bf16[8,192,1024]{2,1,0:T(8,128)(2,1)}, u32[]{:S(2)}, u32[]{:S(2)}) async-start(bf16[8,192,1024]{2,1,0:T(8,128)(2,1)} %bitcast.19), calls=%async_computation.2 | async-start | bytes 6291456 | tf_op jit(solution)/shard_map/all_to_all | solution.py:111
  112.7 6.0 %slice-start.4 = ((s8[6291456]{0:T(1024)(128)(4,1)}), s8[4194304]{0:T(1024)(128)(4,1)S(1)}, s32[]{:S(2)}) async-start(s8[6291456]{0:T(1024)(128)(4,1)} %bitcast.119), calls=%async_computation.16 | async-start | bytes 8388608
  114.5 4.1 slice-start.5
  114.5 9.8 %slice-start.2 = ((s8[6291456]{0:T(1024)(128)(4,1)}), s8[2097152]{0:T(1024)(128)(4,1)S(1)}, s32[]{:S(2)}) async-start(s8[6291456]{0:T(1024)(128)(4,1)} %bitcast.117), calls=%async_computation.14 | async-start | bytes 4194304
  118.6 5.7 %slice-start.3 = ((s8[6291456]{0:T(1024)(128)(4,1)}), s8[4194304]{0:T(1024)(128)(4,1)S(1)}, s32[]{:S(2)}) async-start(s8[6291456]{0:T(1024)(128)(4,1)} %bitcast.117), calls=%async_computation.15 | async-start | bytes 8388608
  162.0 7.9 %copy-start.1 = (bf16[8,256,768]{2,1,0:T(8,128)(2,1)}, bf16[8,256,768]{2,1,0:T(8,128)(2,1)S(1)}, u32[]{:S(2)}) copy-start(bf16[8,256,768]{2,1,0:T(8,128)(2,1)S(1)} %pad_maximum_fusion) | copy-start | bytes 9437188
  169.8 53.7 %all-to-all-start.3 = ((bf16[8,256,1024]{2,1,0:T(8,128)(2,1)}), bf16[8,256,1024]{2,1,0:T(8,128)(2,1)}, u32[]{:S(2)}, u32[]{:S(2)}) async-start(bf16[8,256,1024]{2,1,0:T(8,128)(2,1)} %bitcast.123), calls=%async_computation.3 | async-start | bytes 8388608 | tf_op jit(solution)/shard_map/all_to_all | solution.py:111
  235.1 53.7 %all-to-all-start.4 = ((bf16[8,256,1024]{2,1,0:T(8,128)(2,1)}), bf16[8,256,1024]{2,1,0:T(8,128)(2,1)}, u32[]{:S(2)}, u32[]{:S(2)}) async-start(bf16[8,256,1024]{2,1,0:T(8,128)(2,1)} %bitcast.124), calls=%async_computation.5 | async-start | bytes 8388608 | tf_op jit(solution)/shard_map/all_to_all | solution.py:111
  239.7 61.0 %reduce-scatter.3.cloned.1.call-start = ((), (), s32[]{:S(2)}) async-start(), calls=%async_computation.7 | async-start | bytes 2621440 | tf_op jit(solution)/shard_map/reduce_scatter | solution.py:162
  240.5 101.8 %reduce-scatter.5.cloned.1.call-start = ((), (), s32[]{:S(2)}) async-start(), calls=%async_computation.8 | async-start | bytes 2621440 | tf_op jit(solution)/shard_map/reduce_scatter | solution.py:162
  297.1 3.5 copy-start
  300.5 89.3 %all-gather.6.cloned.1.call-start = ((), (), s32[]{:S(2)}) async-start(), calls=%async_computation.9 | async-start | bytes 2621440 | tf_op jit(solution)/shard_map/all_gather | solution.py:168
  344.4 5.4 %copy-start.7 = (s32[21]{0:T(128)S(1)}, s32[21]{0:T(128)}, u32[]{:S(2)}) copy-start(s32[21]{0:T(128)} %param.29) | copy-start | bytes 256
  344.4 5.4 %copy-start.6 = (s32[1,2,256]{2,1,0:T(2,128)S(1)}, s32[1,2,256]{2,1,0:T(2,128)}, u32[]{:S(2)}) copy-start(s32[1,2,256]{2,1,0:T(2,128)} %param.28) | copy-start | bytes 6148
  399.8 3.6 collective-permute-start
  403.4 4.4 %collective-permute-start.1 = (f32[21]{0:T(128)S(1)}, f32[21]{0:T(128)S(1)}, u32[]{:S(2)}, u32[]{:S(2)}) collective-permute-start(f32[21]{0:T(128)S(1)} %add.113), channel_id=1, source_target_pairs={{0,2},{1,3},{2,0},{3,1},{4,6},{5,7},{6,4},{7,5},{8,10},{9,11},{10,... | collective-permute-start | bytes 260 | tf_op jit(solution)/shard_map/ppermute | solution.py:212
  (3 other events, 6.0 us)
Sparse Core Ops, SparseCore 0:
  14.7 33.1 all-gather.7
  75.9 27.1 all-gather.9
  242.9 43.7 reduce-scatter.2
  300.6 41.5 reduce-scatter.4
  344.5 45.2 all-gather.5
